TPU v7x, 512 devices: a whole 4x4x16 slice. The times are simulated.
512 devices in a mesh: gx: 32 (over z, core), gy: 16 (over x, y).
Axes of the slice: x: 4, y: 4, z: 16, core: 2. Of those that a mesh axis runs over, the one named last changes fastest.
Arguments:
- field: bfloat16 [1024, 65536], P('gx', 'gy'), may hold values from -6 to 6
- dw0: float32 [9, 32], replicated, may hold values from -2 to 2
- pw0: bfloat16 [32, 32], replicated, may hold values from -1.5 to 1.5
- dw1: float32 [9, 32], replicated, may hold values from -2 to 2
- pw1: bfloat16 [32, 64], replicated, may hold values from -1.5 to 1.5
- dw2: float32 [9, 64], replicated, may hold values from -2 to 2
- pw2: bfloat16 [64, 128], replicated, may hold values from -1 to 1
- dw3: float32 [9, 128], replicated, may hold values from -2 to 2
- pw3: bfloat16 [128, 256], replicated, may hold values from -0.75 to 0.75
- dw4: float32 [9, 256], replicated, may hold values from -2 to 2
- pw4: bfloat16 [256, 512], replicated, may hold values from -0.5 to 0.5
- dwc: float32 [4, 9, 512], replicated, may hold values from -2 to 2
- pwc: bfloat16 [4, 512, 512], replicated, may hold values from -0.375 to 0.375
Outputs:
- fine: bfloat16 [1024, 65536], P('gx', 'gy')
- coarse: bfloat16 [4, 4096], replicated
All inputs are finite; a program needn't handle non-finite values.
Results may differ from a plain program's by a relative error of at most 0.024.
Values may be sent and summed in bfloat16 or wider, within the bound.
No kernel may reach another device: no remote copies, remote signals or barrier semaphores. Data moves between devices by JAX's collectives and lax.ppermute only.
A program may use at most 64 MiB of HBM per device.

v0:
```python
import jax
import jax.numpy as jnp
from jax import lax
from jax.sharding import PartitionSpec as P

LC = 4


def shifted(value, axis, steps):
    count = lax.axis_size(axis)
    leading, last = (max(0, -steps), min(count, count - steps))
    return lax.ppermute(value, axis, [(source, source + steps) for source in range(leading, last)])


def padded_2(block, sides, width):
    for axis, dim in sides:
        count = lax.axis_size(axis)
        forward = [(i, i + 1) for i in range(count - 1)]
        backward = [(target, source) for source, target in forward]
        low = lax.ppermute(
            lax.slice_in_dim(block, block.shape[dim] - width, None, axis=dim), axis, forward
        )
        high = lax.ppermute(lax.slice_in_dim(block, 0, width, axis=dim), axis, backward)
        block = jnp.concatenate([low, block, high], axis=dim)
    return block


def gelu_tanh(value):
    return jax.nn.gelu(value, approximate=True)


def point_flat(spread, weight, rows, cols):
    chans = weight.shape[0]
    flat = spread.astype(jnp.bfloat16).reshape(rows * cols, chans)
    mixed = jnp.dot(flat, weight, preferred_element_type=jnp.float32)
    return gelu_tanh(mixed).reshape(rows, cols * weight.shape[1])


def down_level(field, taps, weight, split_rows, split_cols):
    chans = taps.shape[1]
    rows = field.shape[0]
    cols = field.shape[1] // chans
    half_rows = rows // 2
    half_cols = cols // 2
    if split_rows:
        upper = shifted(field[-1:], "gx", 1)
    else:
        upper = jnp.zeros((1, cols * chans), jnp.bfloat16)
    extended = jnp.concatenate([upper, field], axis=0)
    if split_cols:
        leftside = shifted(extended[:, -chans:], "gy", 1)
    else:
        leftside = jnp.zeros((rows + 1, chans), jnp.bfloat16)
    tiled = jnp.tile(taps, (1, half_cols))
    total = jnp.zeros((half_rows, half_cols * chans), jnp.float32)
    for first in range(3):
        slab = extended[first : first + rows : 2]
        left_slab = leftside[first : first + rows : 2]
        pairs = slab.reshape(half_rows, half_cols, 2 * chans)
        even_cells = pairs[:, :, :chans].reshape(half_rows, half_cols * chans)
        odd_cells = pairs[:, :, chans:].reshape(half_rows, half_cols * chans)
        before = jnp.concatenate([left_slab, odd_cells[:, :-chans]], axis=1)
        for second, piece in enumerate((before, even_cells, odd_cells)):
            total = total + piece.astype(jnp.float32) * tiled[3 * first + second]
    return point_flat(total, weight, half_rows, half_cols).astype(jnp.bfloat16)


def local(field, dw0, pw0, dw1, pw1, dw2, pw2, dw3, pw3, dw4, pw4, dwc, pwc):
    chans = dw0.shape[1]
    rows = field.shape[0]
    cols = field.shape[1] // chans
    grid = field.reshape(rows, cols, chans)
    padded = padded_2(grid, (("gx", 0), ("gy", 1)), 2)
    flat_pad = padded.reshape(rows + 4, (cols + 4) * chans)
    tiled = jnp.tile(dw0, (1, cols))
    total = jnp.zeros((rows, cols * chans), jnp.float32)
    for first in range(3):
        for second in range(3):
            piece = flat_pad[
                2 * first : 2 * first + rows, 2 * second * chans : 2 * second * chans + cols * chans
            ]
            total = total + piece.astype(jnp.float32) * tiled[3 * first + second]
    hidden = (field.astype(jnp.float32) + point_flat(total, pw0, rows, cols)).astype(jnp.bfloat16)
    fine = hidden
    for taps, weight in ((dw1, pw1), (dw2, pw2), (dw3, pw3), (dw4, pw4)):
        hidden = down_level(hidden, taps, weight, True, True)
    coarse_chans = dwc.shape[2]
    finished = 0
    for level in range(LC):
        if (
            finished == level
            and hidden.shape[0] % 2 == 0
            and (hidden.shape[1] // coarse_chans % 2 == 0)
        ):
            hidden = down_level(hidden, dwc[level], pwc[level], True, True)
            finished = level + 1
    hidden = lax.all_gather(hidden, "gx", axis=0, tiled=True)
    hidden = lax.all_gather(hidden, "gy", axis=1, tiled=True)
    for level in range(finished, LC):
        hidden = down_level(hidden, dwc[level], pwc[level], False, False)
    return (fine, hidden)


def solution(mesh):
    placed = (P("gx", "gy"), P(), P(), P(), P(), P(), P(), P(), P(), P(), P(), P(), P())
    return jax.shard_map(
        local, mesh=mesh, in_specs=placed, out_specs=(P("gx", "gy"), P()), check_vma=False
    )
```

profile of v0, /device:TPU:6, one launch (start us, length us, event | category | flops | bytes accessed | tf_op | source)
XLA Modules:
  0.0 278.5 jit_solution(14854291314269597330)
XLA Ops:
  8.3 1.7 collective-permute-start
  10.1 1.3 collective-permute-start.1
  11.4 1.5 fusion.196
  12.9 1.5 fusion.195
  14.5 1.0 slice_bitcast_fusion.52
  15.5 1.6 slice_bitcast_fusion.43
  17.1 1.6 fusion.201
  24.4 1.6 slice_bitcast_fusion.34
  26.0 1.7 reshape.1235
  28.4 3.5 %collective-permute-start.2 = (bf16[36,2,32]{1,2,0:T(8,128)(2,1)S(1)}, bf16[36,2,32]{1,2,0:T(8,128)(2,1)S(1)}, u32[]{:S(2)}, u32[]{:S(2)}) collective-permute-start(bf16[36,2,32]{1,2,0:T(8,128)(2,1)S(1)} %get-tuple-element.8), channel_id=1, source_target_pairs={{0,1},{1,2},{2,3},{3,4},{4,5},{5,6},{6,7},{7,8},{8,9},{9,10},{10,1... | collective-permute-start | bytes 13832 | tf_op jit(solution)/shard_map/ppermute | solution.py:20
  31.9 4.5 %collective-permute-start.3 = (bf16[36,2,32]{1,2,0:T(8,128)(2,1)S(1)}, bf16[36,2,32]{1,2,0:T(8,128)(2,1)S(1)}, u32[]{:S(2)}, u32[]{:S(2)}) collective-permute-start(bf16[36,2,32]{1,2,0:T(8,128)(2,1)S(1)} %get-tuple-element.9), channel_id=1, source_target_pairs={{1,0},{2,1},{3,2},{4,3},{5,4},{6,5},{7,6},{8,7},{9,8},{10,9},{11,1... | collective-permute-start | bytes 13832 | tf_op jit(solution)/shard_map/ppermute | solution.py:23
  46.8 1.0 reshape.1238
  48.0 4.1 %collective-permute-start.4 = (bf16[1,4096]{1,0:T(2,128)(2,1)S(1)}, bf16[1,4096]{1,0:T(2,128)(2,1)S(1)}, u32[]{:S(2)}, u32[]{:S(2)}) collective-permute-start(bf16[1,4096]{1,0:T(2,128)(2,1)S(1)} %slice.1366), channel_id=1, source_target_pairs={{0,16},{16,32},{32,48},{48,64},{64,80},{80,96},{96,112},{112,128},... | collective-permute-start | bytes 24584 | tf_op jit(solution)/shard_map/ppermute | solution.py:12
  53.8 2.6 collective-permute-start.5
  57.3 4.2 %collective-permute-done.5 = bf16[33,32]{1,0:T(8,128)(2,1)S(1)} collective-permute-done((bf16[33,32]{1,0:T(8,128)(2,1)S(1)}, bf16[33,32]{1,0:T(8,128)(2,1)S(1)}, u32[]{:S(2)}, u32[]{:S(2)}) %collective-permute-start.5) | collective-permute-done | bytes 2144 | tf_op jit(solution)/shard_map/ppermute | solution.py:12
  62.4 1.1 fusion.16
  64.8 4.7 %collective-permute-start.6 = (bf16[1,4096]{1,0:T(2,128)(2,1)S(1)}, bf16[1,4096]{1,0:T(2,128)(2,1)S(1)}, u32[]{:S(2)}, u32[]{:S(2)}) collective-permute-start(bf16[1,4096]{1,0:T(2,128)(2,1)S(1)} %slice.1129), channel_id=1, source_target_pairs={{0,16},{16,32},{32,48},{48,64},{64,80},{80,96},{96,112},{112,128},... | collective-permute-start | bytes 24584 | tf_op jit(solution)/shard_map/ppermute | solution.py:12
  70.5 1.9 collective-permute-start.7
  72.7 5.4 %collective-permute-done.7 = bf16[17,64]{1,0:T(8,128)(2,1)S(1)} collective-permute-done((bf16[17,64]{1,0:T(8,128)(2,1)S(1)}, bf16[17,64]{1,0:T(8,128)(2,1)S(1)}, u32[]{:S(2)}, u32[]{:S(2)}) %collective-permute-start.7) | collective-permute-done | bytes 2208 | tf_op jit(solution)/shard_map/ppermute | solution.py:12
  79.6 3.7 %collective-permute-start.8 = (bf16[1,4096]{1,0:T(2,128)(2,1)S(1)}, bf16[1,4096]{1,0:T(2,128)(2,1)S(1)}, u32[]{:S(2)}, u32[]{:S(2)}) collective-permute-start(bf16[1,4096]{1,0:T(2,128)(2,1)S(1)} %bitcast.639), channel_id=1, source_target_pairs={{0,16},{16,32},{32,48},{48,64},{64,80},{80,96},{96,112},{112,128},... | collective-permute-start | bytes 24584 | tf_op jit(solution)/shard_map/ppermute | solution.py:12
  84.1 1.9 collective-permute-start.9
  86.3 5.4 %collective-permute-done.9 = bf16[9,128]{1,0:T(8,128)(2,1)S(1)} collective-permute-done((bf16[9,128]{1,0:T(8,128)(2,1)S(1)}, bf16[9,128]{1,0:T(8,128)(2,1)S(1)}, u32[]{:S(2)}, u32[]{:S(2)}) %collective-permute-start.9) | collective-permute-done | bytes 2336 | tf_op jit(solution)/shard_map/ppermute | solution.py:12
  92.0 1.1 fusion.91
  93.4 4.2 %collective-permute-start.10 = (bf16[1,4096]{1,0:T(2,128)(2,1)S(1)}, bf16[1,4096]{1,0:T(2,128)(2,1)S(1)}, u32[]{:S(2)}, u32[]{:S(2)}) collective-permute-start(bf16[1,4096]{1,0:T(2,128)(2,1)S(1)} %bitcast.640), channel_id=1, source_target_pairs={{0,16},{16,32},{32,48},{48,64},{64,80},{80,96},{96,112},{112,128},... | collective-permute-start | bytes 24584 | tf_op jit(solution)/shard_map/ppermute | solution.py:12
  98.6 1.9 collective-permute-start.11
  100.6 5.6 %collective-permute-done.11 = bf16[5,256]{1,0:T(8,128)(2,1)S(1)} collective-permute-done((bf16[5,256]{1,0:T(8,128)(2,1)S(1)}, bf16[5,256]{1,0:T(8,128)(2,1)S(1)}, u32[]{:S(2)}, u32[]{:S(2)}) %collective-permute-start.11) | collective-permute-done | bytes 2592 | tf_op jit(solution)/shard_map/ppermute | solution.py:12
  106.8 4.2 %collective-permute-start.12 = (bf16[1,4096]{1,0:T(2,128)(2,1)S(1)}, bf16[1,4096]{1,0:T(2,128)(2,1)S(1)}, u32[]{:S(2)}, u32[]{:S(2)}) collective-permute-start(bf16[1,4096]{1,0:T(2,128)(2,1)S(1)} %bitcast.638), channel_id=1, source_target_pairs={{0,16},{16,32},{32,48},{48,64},{64,80},{80,96},{96,112},{112,128},... | collective-permute-start | bytes 24584 | tf_op jit(solution)/shard_map/ppermute | solution.py:12
  111.9 1.9 collective-permute-start.13
  113.9 5.5 %collective-permute-done.13 = bf16[3,512]{1,0:T(4,128)(2,1)S(1)} collective-permute-done((bf16[3,512]{1,0:T(4,128)(2,1)S(1)}, bf16[3,512]{1,0:T(4,128)(2,1)S(1)}, u32[]{:S(2)}, u32[]{:S(2)}) %collective-permute-start.13) | collective-permute-done | bytes 3104 | tf_op jit(solution)/shard_map/ppermute | solution.py:12
  119.7 1.2 fusion.153
  120.9 43.4 %all-gather = bf16[32,1,2048]{2,1,0:T(2,128)(2,1)S(1)} all-gather(bf16[1,1,2048]{2,1,0:T(2,128)(2,1)S(1)} %reshape.1338), channel_id=1, replica_groups=mesh['gx'=32,'gy'=16] {'gx'}, dimensions={0}, use_global_device_ids=true | all-gather | bytes 135168 | tf_op jit(solution)/shard_map/all_gather | solution.py:97
  180.3 41.0 %all-gather.3.cloned.1.call-done = bf16[32,32768]{1,0:T(8,128)(2,1)} async-done(((bf16[32,2048]{1,0:T(8,128)(2,1)}), bf16[32,32768]{1,0:T(8,128)(2,1)}) %all-gather.3.cloned.1.call-update) | async-done | bytes 2097168 | tf_op jit(solution)/shard_map/all_gather | solution.py:98
  221.3 1.8 concatenate.136
  223.2 7.5 %slice.1262 = bf16[16,32768]{1,0:T(8,128)(2,1)} slice(bf16[33,32768]{1,0:T(8,128)(2,1)S(1)} %concatenate.136), slice={[0:32:2], [0:32768:1]} | slice | bytes 2097152 | tf_op jit(solution)/shard_map/slice | solution.py:57
  230.7 1.8 copy.75
  232.6 1.6 copy.78
  235.4 7.5 %slice.1272 = bf16[16,32768]{1,0:T(8,128)(2,1)} slice(bf16[32,32768]{1,0:T(8,128)(2,1)S(1)} %copy-done.1), slice={[0:32:2], [0:32768:1]} | slice | bytes 2097152 | tf_op jit(solution)/shard_map/slice | solution.py:57
  242.8 1.8 copy.81
  244.8 1.6 copy.84
  246.4 7.5 %slice.1282 = bf16[16,32768]{1,0:T(8,128)(2,1)} slice(bf16[32,32768]{1,0:T(8,128)(2,1)S(1)} %copy-done.1), slice={[1:32:2], [0:32768:1]} | slice | bytes 2097152 | tf_op jit(solution)/shard_map/slice | solution.py:57
  253.9 1.8 copy.87
  258.2 0.9 add_convert_fusion
  259.4 1.7 fusion.7
  261.6 1.2 slice.1303
  262.8 1.2 slice.1313
  264.0 1.2 slice.1293
  265.8 1.4 fusion.55
  269.8 1.3 fusion.101
  (489 shorter events, 52.4 us)
Async XLA Ops:
  7.2 99.3 %copy-start = (bf16[256,512]{1,0:T(8,128)(2,1)S(1)}, bf16[256,512]{1,0:T(8,128)(2,1)}, u32[]{:S(2)}) copy-start(bf16[256,512]{1,0:T(8,128)(2,1)} %param.23) | copy-start | bytes 786436
  7.2 214.2 %all-gather.3.cloned.1.call-start = ((), (), s32[]{:S(2)}) async-start(), calls=%async_computation | async-start | bytes 2228224 | tf_op jit(solution)/shard_map/all_gather | solution.py:98
  8.3 19.8 %collective-permute-start = (bf16[2,128,32]{2,1,0:T(8,128)(2,1)S(1)}, bf16[2,128,32]{2,1,0:T(8,128)(2,1)S(1)}, u32[]{:S(2)}, u32[]{:S(2)}) collective-permute-start(bf16[2,128,32]{2,1,0:T(8,128)(2,1)S(1)} %slice.1061), channel_id=1, source_target_pairs={{0,16},{16,32},{32,48},{48,64},{64,80},{80,96},{96,112},{112,128},... | collective-permute-start | bytes 49160 | tf_op jit(solution)/shard_map/ppermute | solution.py:20
  10.1 18.0 %collective-permute-start.1 = (bf16[2,128,32]{2,1,0:T(8,128)(2,1)S(1)}, bf16[2,128,32]{2,1,0:T(8,128)(2,1)S(1)}, u32[]{:S(2)}, u32[]{:S(2)}) collective-permute-start(bf16[2,128,32]{2,1,0:T(8,128)(2,1)S(1)} %slice.1063), channel_id=1, source_target_pairs={{16,0},{32,16},{48,32},{64,48},{80,64},{96,80},{112,96},{128,112},... | collective-permute-start | bytes 49160 | tf_op jit(solution)/shard_map/ppermute | solution.py:23
  28.4 13.6 %collective-permute-start.2 = (bf16[36,2,32]{1,2,0:T(8,128)(2,1)S(1)}, bf16[36,2,32]{1,2,0:T(8,128)(2,1)S(1)}, u32[]{:S(2)}, u32[]{:S(2)}) collective-permute-start(bf16[36,2,32]{1,2,0:T(8,128)(2,1)S(1)} %get-tuple-element.8), channel_id=1, source_target_pairs={{0,1},{1,2},{2,3},{3,4},{4,5},{5,6},{6,7},{7,8},{8,9},{9,10},{10,1... | collective-permute-start | bytes 13832 | tf_op jit(solution)/shard_map/ppermute | solution.py:20
  31.9 10.3 %collective-permute-start.3 = (bf16[36,2,32]{1,2,0:T(8,128)(2,1)S(1)}, bf16[36,2,32]{1,2,0:T(8,128)(2,1)S(1)}, u32[]{:S(2)}, u32[]{:S(2)}) collective-permute-start(bf16[36,2,32]{1,2,0:T(8,128)(2,1)S(1)} %get-tuple-element.9), channel_id=1, source_target_pairs={{1,0},{2,1},{3,2},{4,3},{5,4},{6,5},{7,6},{8,7},{9,8},{10,9},{11,1... | collective-permute-start | bytes 13832 | tf_op jit(solution)/shard_map/ppermute | solution.py:23
  48.0 5.2 %collective-permute-start.4 = (bf16[1,4096]{1,0:T(2,128)(2,1)S(1)}, bf16[1,4096]{1,0:T(2,128)(2,1)S(1)}, u32[]{:S(2)}, u32[]{:S(2)}) collective-permute-start(bf16[1,4096]{1,0:T(2,128)(2,1)S(1)} %slice.1366), channel_id=1, source_target_pairs={{0,16},{16,32},{32,48},{48,64},{64,80},{80,96},{96,112},{112,128},... | collective-permute-start | bytes 24584 | tf_op jit(solution)/shard_map/ppermute | solution.py:12
  53.8 7.7 %collective-permute-start.5 = (bf16[33,32]{1,0:T(8,128)(2,1)S(1)}, bf16[33,32]{1,0:T(8,128)(2,1)S(1)}, u32[]{:S(2)}, u32[]{:S(2)}) collective-permute-start(bf16[33,32]{1,0:T(8,128)(2,1)S(1)} %fusion.143), channel_id=1, source_target_pairs={{0,1},{1,2},{2,3},{3,4},{4,5},{5,6},{6,7},{7,8},{8,9},{9,10},{10,1... | collective-permute-start | bytes 6344 | tf_op jit(solution)/shard_map/ppermute | solution.py:12
  64.8 5.4 %collective-permute-start.6 = (bf16[1,4096]{1,0:T(2,128)(2,1)S(1)}, bf16[1,4096]{1,0:T(2,128)(2,1)S(1)}, u32[]{:S(2)}, u32[]{:S(2)}) collective-permute-start(bf16[1,4096]{1,0:T(2,128)(2,1)S(1)} %slice.1129), channel_id=1, source_target_pairs={{0,16},{16,32},{32,48},{48,64},{64,80},{80,96},{96,112},{112,128},... | collective-permute-start | bytes 24584 | tf_op jit(solution)/shard_map/ppermute | solution.py:12
  70.5 7.6 %collective-permute-start.7 = (bf16[17,64]{1,0:T(8,128)(2,1)S(1)}, bf16[17,64]{1,0:T(8,128)(2,1)S(1)}, u32[]{:S(2)}, u32[]{:S(2)}) collective-permute-start(bf16[17,64]{1,0:T(8,128)(2,1)S(1)} %fusion.184), channel_id=1, source_target_pairs={{0,1},{1,2},{2,3},{3,4},{4,5},{5,6},{6,7},{7,8},{8,9},{9,10},{10,1... | collective-permute-start | bytes 6536 | tf_op jit(solution)/shard_map/ppermute | solution.py:12
  79.0 40.5 %copy-start.40 = (f32[1,1,4,512]{3,1,2,0:T(1,128)S(1)}, f32[1,1,4,512]{3,1,2,0:T(1,128)}, u32[]{:S(2)}) copy-start(f32[1,1,4,512]{3,1,2,0:T(1,128)} %copy.64) | copy-start | bytes 24580
  79.0 40.5 %copy-start.41 = (f32[1,1,4,512]{3,1,2,0:T(1,128)S(1)}, f32[1,1,4,512]{3,1,2,0:T(1,128)}, u32[]{:S(2)}) copy-start(f32[1,1,4,512]{3,1,2,0:T(1,128)} %copy.66) | copy-start | bytes 24580
  79.0 40.5 %copy-start.42 = (f32[1,1,4,512]{3,1,2,0:T(1,128)S(1)}, f32[1,1,4,512]{3,1,2,0:T(1,128)}, u32[]{:S(2)}) copy-start(f32[1,1,4,512]{3,1,2,0:T(1,128)} %copy.68) | copy-start | bytes 24580
  79.1 40.5 %copy-start.43 = (f32[1,1,4,512]{3,1,2,0:T(1,128)S(1)}, f32[1,1,4,512]{3,1,2,0:T(1,128)}, u32[]{:S(2)}) copy-start(f32[1,1,4,512]{3,1,2,0:T(1,128)} %copy.69) | copy-start | bytes 24580
  79.1 40.5 %copy-start.44 = (f32[1,1,4,512]{3,1,2,0:T(1,128)S(1)}, f32[1,1,4,512]{3,1,2,0:T(1,128)}, u32[]{:S(2)}) copy-start(f32[1,1,4,512]{3,1,2,0:T(1,128)} %copy.71) | copy-start | bytes 24580
  79.6 4.5 %collective-permute-start.8 = (bf16[1,4096]{1,0:T(2,128)(2,1)S(1)}, bf16[1,4096]{1,0:T(2,128)(2,1)S(1)}, u32[]{:S(2)}, u32[]{:S(2)}) collective-permute-start(bf16[1,4096]{1,0:T(2,128)(2,1)S(1)} %bitcast.639), channel_id=1, source_target_pairs={{0,16},{16,32},{32,48},{48,64},{64,80},{80,96},{96,112},{112,128},... | collective-permute-start | bytes 24584 | tf_op jit(solution)/shard_map/ppermute | solution.py:12
  84.1 7.6 %collective-permute-start.9 = (bf16[9,128]{1,0:T(8,128)(2,1)S(1)}, bf16[9,128]{1,0:T(8,128)(2,1)S(1)}, u32[]{:S(2)}, u32[]{:S(2)}) collective-permute-start(bf16[9,128]{1,0:T(8,128)(2,1)S(1)} %fusion.186), channel_id=1, source_target_pairs={{0,1},{1,2},{2,3},{3,4},{4,5},{5,6},{6,7},{7,8},{8,9},{9,10},{10,1... | collective-permute-start | bytes 6920 | tf_op jit(solution)/shard_map/ppermute | solution.py:12
  86.2 78.9 %copy-start.64 = (f32[1,1,512]{2,0,1:T(1,128)S(1)}, f32[1,1,512]{2,0,1:T(1,128)}, u32[]{:S(2)}) copy-start(f32[1,1,512]{2,0,1:T(1,128)} %get-tuple-element.39) | copy-start | bytes 6148
  86.2 78.9 %copy-start.14 = (f32[4,4,8,128]{3,2,1,0:T(8,128)S(1)}, f32[4,4,8,128]{3,2,1,0:T(8,128)}, u32[]{:S(2)}) copy-start(f32[4,4,8,128]{3,2,1,0:T(8,128)} %broadcast_bitcast_fusion.2) | copy-start | bytes 196612
  86.2 78.9 %copy-start.15 = (f32[4,4,8,128]{3,2,1,0:T(8,128)S(1)}, f32[4,4,8,128]{3,2,1,0:T(8,128)}, u32[]{:S(2)}) copy-start(f32[4,4,8,128]{3,2,1,0:T(8,128)} %broadcast_bitcast_fusion.1) | copy-start | bytes 196612
  91.7 73.4 %copy-start.16 = (f32[4,4,8,128]{3,2,1,0:T(8,128)S(1)}, f32[4,4,8,128]{3,2,1,0:T(8,128)}, u32[]{:S(2)}) copy-start(f32[4,4,8,128]{3,2,1,0:T(8,128)} %broadcast_bitcast_fusion) | copy-start | bytes 196612
  91.8 74.0 %copy-start.17 = (f32[4,4,8,128]{3,2,1,0:T(8,128)S(1)}, f32[4,4,8,128]{3,2,1,0:T(8,128)}, u32[]{:S(2)}) copy-start(f32[4,4,8,128]{3,2,1,0:T(8,128)} %broadcast_bitcast_fusion.8) | copy-start | bytes 196612
  91.9 74.5 %copy-start.18 = (f32[4,4,8,128]{3,2,1,0:T(8,128)S(1)}, f32[4,4,8,128]{3,2,1,0:T(8,128)}, u32[]{:S(2)}) copy-start(f32[4,4,8,128]{3,2,1,0:T(8,128)} %broadcast_bitcast_fusion.7) | copy-start | bytes 196612
  92.0 75.1 %copy-start.19 = (f32[4,4,8,128]{3,2,1,0:T(8,128)S(1)}, f32[4,4,8,128]{3,2,1,0:T(8,128)}, u32[]{:S(2)}) copy-start(f32[4,4,8,128]{3,2,1,0:T(8,128)} %broadcast_bitcast_fusion.6) | copy-start | bytes 196612
  92.0 75.8 %copy-start.20 = (f32[4,4,8,128]{3,2,1,0:T(8,128)S(1)}, f32[4,4,8,128]{3,2,1,0:T(8,128)}, u32[]{:S(2)}) copy-start(f32[4,4,8,128]{3,2,1,0:T(8,128)} %broadcast_bitcast_fusion.5) | copy-start | bytes 196612
  93.1 75.3 %copy-start.21 = (f32[4,4,8,128]{3,2,1,0:T(8,128)S(1)}, f32[4,4,8,128]{3,2,1,0:T(8,128)}, u32[]{:S(2)}) copy-start(f32[4,4,8,128]{3,2,1,0:T(8,128)} %broadcast_bitcast_fusion.4) | copy-start | bytes 196612
  93.1 75.9 %copy-start.22 = (f32[4,4,8,128]{3,2,1,0:T(8,128)S(1)}, f32[4,4,8,128]{3,2,1,0:T(8,128)}, u32[]{:S(2)}) copy-start(f32[4,4,8,128]{3,2,1,0:T(8,128)} %broadcast_bitcast_fusion.3) | copy-start | bytes 196612
  93.4 5.1 %collective-permute-start.10 = (bf16[1,4096]{1,0:T(2,128)(2,1)S(1)}, bf16[1,4096]{1,0:T(2,128)(2,1)S(1)}, u32[]{:S(2)}, u32[]{:S(2)}) collective-permute-start(bf16[1,4096]{1,0:T(2,128)(2,1)S(1)} %bitcast.640), channel_id=1, source_target_pairs={{0,16},{16,32},{32,48},{48,64},{64,80},{80,96},{96,112},{112,128},... | collective-permute-start | bytes 24584 | tf_op jit(solution)/shard_map/ppermute | solution.py:12
  97.7 72.6 %copy-start.63 = (f32[1,1,512]{2,0,1:T(1,128)S(1)}, f32[1,1,512]{2,0,1:T(1,128)}, u32[]{:S(2)}) copy-start(f32[1,1,512]{2,0,1:T(1,128)} %get-tuple-element.38) | copy-start | bytes 6148
  97.7 73.2 %copy-start.62 = (f32[1,1,512]{2,0,1:T(1,128)S(1)}, f32[1,1,512]{2,0,1:T(1,128)}, u32[]{:S(2)}) copy-start(f32[1,1,512]{2,0,1:T(1,128)} %get-tuple-element.37) | copy-start | bytes 6148
  98.6 73.0 %copy-start.61 = (f32[1,1,512]{2,0,1:T(1,128)S(1)}, f32[1,1,512]{2,0,1:T(1,128)}, u32[]{:S(2)}) copy-start(f32[1,1,512]{2,0,1:T(1,128)} %get-tuple-element.36) | copy-start | bytes 6148
  98.6 7.6 %collective-permute-start.11 = (bf16[5,256]{1,0:T(8,128)(2,1)S(1)}, bf16[5,256]{1,0:T(8,128)(2,1)S(1)}, u32[]{:S(2)}, u32[]{:S(2)}) collective-permute-start(bf16[5,256]{1,0:T(8,128)(2,1)S(1)} %fusion.185), channel_id=1, source_target_pairs={{0,1},{1,2},{2,3},{3,4},{4,5},{5,6},{6,7},{7,8},{8,9},{9,10},{10,1... | collective-permute-start | bytes 7688 | tf_op jit(solution)/shard_map/ppermute | solution.py:12
  100.6 71.7 %copy-start.60 = (f32[1,1,512]{2,0,1:T(1,128)S(1)}, f32[1,1,512]{2,0,1:T(1,128)}, u32[]{:S(2)}) copy-start(f32[1,1,512]{2,0,1:T(1,128)} %get-tuple-element.35) | copy-start | bytes 6148
  106.3 66.5 %copy-start.59 = (f32[1,1,512]{2,0,1:T(1,128)S(1)}, f32[1,1,512]{2,0,1:T(1,128)}, u32[]{:S(2)}) copy-start(f32[1,1,512]{2,0,1:T(1,128)} %get-tuple-element.34) | copy-start | bytes 6148
  106.4 67.1 %copy-start.58 = (f32[1,1,512]{2,0,1:T(1,128)S(1)}, f32[1,1,512]{2,0,1:T(1,128)}, u32[]{:S(2)}) copy-start(f32[1,1,512]{2,0,1:T(1,128)} %get-tuple-element.33) | copy-start | bytes 6148
  106.5 67.6 %copy-start.57 = (f32[1,1,512]{2,0,1:T(1,128)S(1)}, f32[1,1,512]{2,0,1:T(1,128)}, u32[]{:S(2)}) copy-start(f32[1,1,512]{2,0,1:T(1,128)} %get-tuple-element.32) | copy-start | bytes 6148
  106.5 68.2 %copy-start.56 = (f32[1,1,512]{2,0,1:T(1,128)S(1)}, f32[1,1,512]{2,0,1:T(1,128)}, u32[]{:S(2)}) copy-start(f32[1,1,512]{2,0,1:T(1,128)} %get-tuple-element.31) | copy-start | bytes 6148
  106.7 68.6 %copy-start.55 = (f32[1,1,512]{2,0,1:T(1,128)S(1)}, f32[1,1,512]{2,0,1:T(1,128)}, u32[]{:S(2)}) copy-start(f32[1,1,512]{2,0,1:T(1,128)} %get-tuple-element.24) | copy-start | bytes 6148
  106.7 68.6 %copy-start.54 = (f32[1,1,512]{2,0,1:T(1,128)S(1)}, f32[1,1,512]{2,0,1:T(1,128)}, u32[]{:S(2)}) copy-start(f32[1,1,512]{2,0,1:T(1,128)} %get-tuple-element.30) | copy-start | bytes 6148
  106.8 69.2 %copy-start.53 = (f32[1,1,512]{2,0,1:T(1,128)S(1)}, f32[1,1,512]{2,0,1:T(1,128)}, u32[]{:S(2)}) copy-start(f32[1,1,512]{2,0,1:T(1,128)} %get-tuple-element.29) | copy-start | bytes 6148
  106.8 5.1 %collective-permute-start.12 = (bf16[1,4096]{1,0:T(2,128)(2,1)S(1)}, bf16[1,4096]{1,0:T(2,128)(2,1)S(1)}, u32[]{:S(2)}, u32[]{:S(2)}) collective-permute-start(bf16[1,4096]{1,0:T(2,128)(2,1)S(1)} %bitcast.638), channel_id=1, source_target_pairs={{0,16},{16,32},{32,48},{48,64},{64,80},{80,96},{96,112},{112,128},... | collective-permute-start | bytes 24584 | tf_op jit(solution)/shard_map/ppermute | solution.py:12
  111.0 65.6 %copy-start.52 = (f32[1,1,512]{2,0,1:T(1,128)S(1)}, f32[1,1,512]{2,0,1:T(1,128)}, u32[]{:S(2)}) copy-start(f32[1,1,512]{2,0,1:T(1,128)} %get-tuple-element.28) | copy-start | bytes 6148
  111.1 66.1 %copy-start.51 = (f32[1,1,512]{2,0,1:T(1,128)S(1)}, f32[1,1,512]{2,0,1:T(1,128)}, u32[]{:S(2)}) copy-start(f32[1,1,512]{2,0,1:T(1,128)} %get-tuple-element.27) | copy-start | bytes 6148
  111.1 66.7 %copy-start.50 = (f32[1,1,512]{2,0,1:T(1,128)S(1)}, f32[1,1,512]{2,0,1:T(1,128)}, u32[]{:S(2)}) copy-start(f32[1,1,512]{2,0,1:T(1,128)} %get-tuple-element.26) | copy-start | bytes 6148
  111.2 67.2 %copy-start.49 = (f32[1,1,512]{2,0,1:T(1,128)S(1)}, f32[1,1,512]{2,0,1:T(1,128)}, u32[]{:S(2)}) copy-start(f32[1,1,512]{2,0,1:T(1,128)} %get-tuple-element.25) | copy-start | bytes 6148
  111.9 67.2 %copy-start.48 = (f32[1,1,512]{2,0,1:T(1,128)S(1)}, f32[1,1,512]{2,0,1:T(1,128)}, u32[]{:S(2)}) copy-start(f32[1,1,512]{2,0,1:T(1,128)} %get-tuple-element.43) | copy-start | bytes 6148
  111.9 7.6 %collective-permute-start.13 = (bf16[3,512]{1,0:T(4,128)(2,1)S(1)}, bf16[3,512]{1,0:T(4,128)(2,1)S(1)}, u32[]{:S(2)}, u32[]{:S(2)}) collective-permute-start(bf16[3,512]{1,0:T(4,128)(2,1)S(1)} %pad_maximum_fusion.6), channel_id=1, source_target_pairs={{0,1},{1,2},{2,3},{3,4},{4,5},{5,6},{6,7},{7,8},{8,9},{9,10},{10,1... | collective-permute-start | bytes 9224 | tf_op jit(solution)/shard_map/ppermute | solution.py:12
  113.9 65.8 %copy-start.47 = (f32[1,1,512]{2,0,1:T(1,128)S(1)}, f32[1,1,512]{2,0,1:T(1,128)}, u32[]{:S(2)}) copy-start(f32[1,1,512]{2,0,1:T(1,128)} %get-tuple-element.59) | copy-start | bytes 6148
  (60 other events, 693.9 us)
Sparse Core Ops, SparseCore 0:
  165.1 56.1 all-gather.2
where the time goes:
time: 280 us; the launch traced here: 279 us
  local copies, waits for them, and re-layouts  93.6 us (33%)
  waiting for transfers between devices  69.4 us (25%)
  blocking collectives  43.4 us (16%)
  starting transfers between devices  42.2 us (15%)
  between operations  16.7 us (6%)
  matrix products  7.75 us (3%)
  other arithmetic  5.42 us (2%)
    all_gather x1, blocking collectives, local(): hidden = lax.all_gather(hidden, 'gx', axis=0, tiled=True)  43.4 us
    all_gather x1, waiting for transfers between devices, local(): hidden = lax.all_gather(hidden, 'gy', axis=1, tiled=True)  41 us
    unnamed x313, local copies, waits for them, and re-layouts  37.7 us
    ppermute x10, starting transfers between devices, shifted(): lax.ppermute(value, axis, [(source, source + steps) for source in range(l...  31.2 us
    slice x22, local copies, waits for them, and re-layouts, down_level(): slab = extended[first:first + rows:2]  29.2 us
    ppermute x10, waiting for transfers between devices, shifted(): lax.ppermute(value, axis, [(source, source + steps) for source in range(l...  28.3 us
    slice x6, local copies, waits for them, and re-layouts, down_level(): total = total + piece.astype(jnp.float32) * tiled[3 * first + second]  8.45 us
    dot_general x9, matrix products, point_flat(): mixed = jnp.dot(flat, weight, preferred_element_type=jnp.float32)  7.75 us
  transfers between devices with their start and end apart: 15, of which 11 were waited for; matrix products, arithmetic and copies ran while one was open for 15% of the time, Pallas kernels for 0%

commit v1 on v0

--- a/solution.py
+++ b/solution.py
@@ -85,20 +85,40 @@
     for taps, weight in ((dw1, pw1), (dw2, pw2), (dw3, pw3), (dw4, pw4)):
         hidden = down_level(hidden, taps, weight, True, True)
     coarse_chans = dwc.shape[2]
-    finished = 0
-    for level in range(LC):
-        if (
-            finished == level
-            and hidden.shape[0] % 2 == 0
-            and (hidden.shape[1] // coarse_chans % 2 == 0)
-        ):
-            hidden = down_level(hidden, dwc[level], pwc[level], True, True)
-            finished = level + 1
+    halo = 2 ** (LC - 1) - 1
+    grid4 = hidden.reshape(hidden.shape[0], -1, coarse_chans)
+    upper = shifted(grid4[-1:], "gx", 1)
+    extended = jnp.concatenate([upper, grid4], axis=0)
+    leftside = shifted(extended[:, -halo:], "gy", 1)
+    extended = jnp.concatenate([leftside, extended], axis=1)
+    hidden = strided_cells(extended, dwc[0], pwc[0])
     hidden = lax.all_gather(hidden, "gx", axis=0, tiled=True)
+    for level in range(1, LC - 1):
+        hidden = strided_cells(pad_top(hidden), dwc[level], pwc[level])
     hidden = lax.all_gather(hidden, "gy", axis=1, tiled=True)
-    for level in range(finished, LC):
-        hidden = down_level(hidden, dwc[level], pwc[level], False, False)
-    return (fine, hidden)
+    hidden = strided_cells(pad_left(pad_top(hidden)), dwc[LC - 1], pwc[LC - 1])
+    return (fine, hidden.reshape(hidden.shape[0], -1))
+
+
+def pad_top(cells):
+    return jnp.concatenate([jnp.zeros_like(cells[:1]), cells], axis=0)
+
+
+def pad_left(cells):
+    return jnp.concatenate([jnp.zeros_like(cells[:, :1]), cells], axis=1)
+
+
+def strided_cells(padded, taps, weight):
+    rows = (padded.shape[0] - 1) // 2
+    cols = (padded.shape[1] - 1) // 2
+    total = jnp.zeros((rows, cols, padded.shape[2]), jnp.float32)
+    for first in range(3):
+        for second in range(3):
+            piece = padded[first : first + 2 * rows : 2, second : second + 2 * cols : 2]
+            total = total + piece.astype(jnp.float32) * taps[3 * first + second]
+    flat = total.astype(jnp.bfloat16).reshape(rows * cols, -1)
+    mixed = jnp.dot(flat, weight, preferred_element_type=jnp.float32)
+    return gelu_tanh(mixed).astype(jnp.bfloat16).reshape(rows, cols, weight.shape[1])
 
 
 def solution(mesh):

time: 280 us -> 176 us (0.63)
  local copies, waits for them, and re-layouts: 93.6 us -> 25.2 us
  waiting for transfers between devices: 69.4 us -> 32.9 us
  blocking collectives: 43.4 us -> 63.9 us
  between operations: 16.7 us -> 2.23 us
  matrix products: 7.75 us -> 2.91 us
    all_gather x1 -> x0, waiting for transfers between devices: 41 us -> none  [local(): hidden = lax.all_gather(hidden, 'gy', axis=1, tiled=True)]
    unnamed x313 -> x92, local copies, waits for them, and re-layouts: 37.7 us -> 0.38 us
    slice x22 -> x12, local copies, waits for them, and re-layouts: 29.2 us -> 1.5 us  [down_level(): slab = extended[first:first + rows:2]]
    all_gather x0 -> x1, blocking collectives: none -> 21.5 us  [local(): hidden = lax.all_gather(hidden, 'gy', axis=1, tiled=True)]
    dot_general x9 -> x5, matrix products: 7.75 us -> 2.02 us  [point_flat(): mixed = jnp.dot(flat, weight, preferred_element_type=jnp.float32)]
    slice x6 -> x4, local copies, waits for them, and re-layouts: 8.45 us -> 5.38 us  [down_level(): total = total + piece.astype(jnp.float32) * tiled[3 * first + second]]
    slice x3 -> x39, local copies, waits for them, and re-layouts: 0.06 us -> 3.1 us  [the longest x36 3.02 us: strided_cells(): piece = padded[first:first + 2 * rows:2, second:second + 2 * cols:2]]
  transfers between devices with their start and end apart: 15 -> 14, of which waited for: 11 -> 11; matrix products, arithmetic and copies ran while one was open for 15% -> 7% of each run, Pallas kernels for 0% -> 0%
where the time goes in v1:
time: 176 us; the launch traced here: 173 us
  blocking collectives  63.9 us (36%)
  starting transfers between devices  42.6 us (24%)
  waiting for transfers between devices  32.9 us (19%)
  local copies, waits for them, and re-layouts  25.2 us (14%)
  other arithmetic  3.56 us (2%)
  matrix products  2.91 us (2%)
  between operations  2.23 us (1%)
    all_gather x1, blocking collectives, local(): hidden = lax.all_gather(hidden, 'gx', axis=0, tiled=True)  42.4 us
    ppermute x10, starting transfers between devices, shifted(): lax.ppermute(value, axis, [(source, source + steps) for source in range(l...  31.6 us
    ppermute x10, waiting for transfers between devices, shifted(): lax.ppermute(value, axis, [(source, source + steps) for source in range(l...  28.5 us
    all_gather x1, blocking collectives, local(): hidden = lax.all_gather(hidden, 'gy', axis=1, tiled=True)  21.5 us
    ppermute x2, starting transfers between devices, padded_2(): lax.ppermute(lax.slice_in_dim(block, 0, width, axis=dim), axis, backward)  5.76 us
    slice x4, local copies, waits for them, and re-layouts, down_level(): total = total + piece.astype(jnp.float32) * tiled[3 * first + second]  5.38 us
    ppermute x2, starting transfers between devices, padded_2(): lax.ppermute(lax.slice_in_dim(block, block.shape[dim] - width, None, axis...  5.23 us
  transfers between devices with their start and end apart: 14, of which 11 were waited for; matrix products, arithmetic and copies ran while one was open for 7% of the time, Pallas kernels for 0%

profile of v1, /device:TPU:6, one launch (start us, length us, event | category | flops | bytes accessed | tf_op | source)
XLA Modules:
  0.0 173.2 jit_solution(16057777883930084446)
XLA Ops:
  0.6 0.9 fusion.205
  1.7 1.7 %collective-permute-start = (bf16[2,128,32]{2,1,0:T(8,128)(2,1)S(1)}, bf16[2,128,32]{2,1,0:T(8,128)(2,1)S(1)}, u32[]{:S(2)}, u32[]{:S(2)}) collective-permute-start(bf16[2,128,32]{2,1,0:T(8,128)(2,1)S(1)} %slice.906), channel_id=1, source_target_pairs={{0,16},{16,32},{32,48},{48,64},{64,80},{80,96},{96,112},{112,128},... | collective-permute-start | bytes 49160 | tf_op jit(solution)/shard_map/ppermute | solution.py:20
  3.6 1.3 collective-permute-start.1
  4.9 1.0 slice_bitcast_fusion.47
  5.8 1.6 slice_bitcast_fusion.38
  7.4 1.6 fusion.211
  9.0 1.6 slice_bitcast_fusion.29
  10.6 1.7 reshape.627
  12.3 0.3 copy.48
  13.1 3.5 %collective-permute-start.2 = (bf16[36,2,32]{1,2,0:T(8,128)(2,1)S(1)}, bf16[36,2,32]{1,2,0:T(8,128)(2,1)S(1)}, u32[]{:S(2)}, u32[]{:S(2)}) collective-permute-start(bf16[36,2,32]{1,2,0:T(8,128)(2,1)S(1)} %get-tuple-element.2), channel_id=1, source_target_pairs={{0,1},{1,2},{2,3},{3,4},{4,5},{5,6},{6,7},{7,8},{8,9},{9,10},{10,1... | collective-permute-start | bytes 13832 | tf_op jit(solution)/shard_map/ppermute | solution.py:20
  16.6 4.5 %collective-permute-start.3 = (bf16[36,2,32]{1,2,0:T(8,128)(2,1)S(1)}, bf16[36,2,32]{1,2,0:T(8,128)(2,1)S(1)}, u32[]{:S(2)}, u32[]{:S(2)}) collective-permute-start(bf16[36,2,32]{1,2,0:T(8,128)(2,1)S(1)} %get-tuple-element.3), channel_id=1, source_target_pairs={{1,0},{2,1},{3,2},{4,3},{5,4},{6,5},{7,6},{8,7},{9,8},{10,9},{11,1... | collective-permute-start | bytes 13832 | tf_op jit(solution)/shard_map/ppermute | solution.py:23
  21.1 0.6 slice_bitcast_fusion.20
  22.5 2.6 %collective-permute-done.2 = bf16[36,2,32]{1,2,0:T(8,128)(2,1)S(1)} collective-permute-done((bf16[36,2,32]{1,2,0:T(8,128)(2,1)S(1)}, bf16[36,2,32]{1,2,0:T(8,128)(2,1)S(1)}, u32[]{:S(2)}, u32[]{:S(2)}) %collective-permute-start.2) | collective-permute-done | bytes 4640 | tf_op jit(solution)/shard_map/ppermute | solution.py:20
  25.1 1.7 %collective-permute-done.3 = bf16[36,2,32]{1,2,0:T(8,128)(2,1)S(1)} collective-permute-done((bf16[36,2,32]{1,2,0:T(8,128)(2,1)S(1)}, bf16[36,2,32]{1,2,0:T(8,128)(2,1)S(1)}, u32[]{:S(2)}, u32[]{:S(2)}) %collective-permute-start.3) | collective-permute-done | bytes 4640 | tf_op jit(solution)/shard_map/ppermute | solution.py:23
  26.9 0.4 pad_maximum_fusion
  27.2 0.8 copy.50
  28.0 0.8 reshape.628
  28.8 0.7 add_convert_fusion.1
  29.5 0.8 reshape.629
  30.3 0.5 fusion.6
  30.9 0.6 copy.51
  31.5 1.0 reshape.630
  32.7 3.6 %collective-permute-start.4 = (bf16[1,4096]{1,0:T(2,128)(2,1)S(1)}, bf16[1,4096]{1,0:T(2,128)(2,1)S(1)}, u32[]{:S(2)}, u32[]{:S(2)}) collective-permute-start(bf16[1,4096]{1,0:T(2,128)(2,1)S(1)} %slice.1171), channel_id=1, source_target_pairs={{0,16},{16,32},{32,48},{48,64},{64,80},{80,96},{96,112},{112,128},... | collective-permute-start | bytes 24584 | tf_op jit(solution)/shard_map/ppermute | solution.py:12
  37.2 0.3 reshape.636
  38.1 3.1 %collective-permute-start.5 = (bf16[33,32]{1,0:T(8,128)(2,1)S(1)}, bf16[33,32]{1,0:T(8,128)(2,1)S(1)}, u32[]{:S(2)}, u32[]{:S(2)}) collective-permute-start(bf16[33,32]{1,0:T(8,128)(2,1)S(1)} %fusion.160), channel_id=1, source_target_pairs={{0,1},{1,2},{2,3},{3,4},{4,5},{5,6},{6,7},{7,8},{8,9},{9,10},{10,1... | collective-permute-start | bytes 6344 | tf_op jit(solution)/shard_map/ppermute | solution.py:12
  41.7 0.3 reshape.634
  42.0 3.9 %collective-permute-done.5 = bf16[33,32]{1,0:T(8,128)(2,1)S(1)} collective-permute-done((bf16[33,32]{1,0:T(8,128)(2,1)S(1)}, bf16[33,32]{1,0:T(8,128)(2,1)S(1)}, u32[]{:S(2)}, u32[]{:S(2)}) %collective-permute-start.5) | collective-permute-done | bytes 2144 | tf_op jit(solution)/shard_map/ppermute | solution.py:12
  46.8 1.1 fusion.8
  47.9 1.0 fusion.35
  49.9 4.8 %collective-permute-start.6 = (bf16[1,4096]{1,0:T(2,128)(2,1)S(1)}, bf16[1,4096]{1,0:T(2,128)(2,1)S(1)}, u32[]{:S(2)}, u32[]{:S(2)}) collective-permute-start(bf16[1,4096]{1,0:T(2,128)(2,1)S(1)} %slice.974), channel_id=1, source_target_pairs={{0,16},{16,32},{32,48},{48,64},{64,80},{80,96},{96,112},{112,128},... | collective-permute-start | bytes 24584 | tf_op jit(solution)/shard_map/ppermute | solution.py:12
  55.3 0.3 collective-permute-done.6
  55.8 2.1 %collective-permute-start.7 = (bf16[17,64]{1,0:T(8,128)(2,1)S(1)}, bf16[17,64]{1,0:T(8,128)(2,1)S(1)}, u32[]{:S(2)}, u32[]{:S(2)}) collective-permute-start(bf16[17,64]{1,0:T(8,128)(2,1)S(1)} %fusion.198), channel_id=1, source_target_pairs={{0,1},{1,2},{2,3},{3,4},{4,5},{5,6},{6,7},{7,8},{8,9},{9,10},{10,1... | collective-permute-start | bytes 6536 | tf_op jit(solution)/shard_map/ppermute | solution.py:12
  58.3 5.2 %collective-permute-done.7 = bf16[17,64]{1,0:T(8,128)(2,1)S(1)} collective-permute-done((bf16[17,64]{1,0:T(8,128)(2,1)S(1)}, bf16[17,64]{1,0:T(8,128)(2,1)S(1)}, u32[]{:S(2)}, u32[]{:S(2)}) %collective-permute-start.7) | collective-permute-done | bytes 2208 | tf_op jit(solution)/shard_map/ppermute | solution.py:12
  64.9 3.8 %collective-permute-start.8 = (bf16[1,4096]{1,0:T(2,128)(2,1)S(1)}, bf16[1,4096]{1,0:T(2,128)(2,1)S(1)}, u32[]{:S(2)}, u32[]{:S(2)}) collective-permute-start(bf16[1,4096]{1,0:T(2,128)(2,1)S(1)} %bitcast.361), channel_id=1, source_target_pairs={{0,16},{16,32},{32,48},{48,64},{64,80},{80,96},{96,112},{112,128},... | collective-permute-start | bytes 24584 | tf_op jit(solution)/shard_map/ppermute | solution.py:12
  68.8 0.7 collective-permute-done.8
  69.5 1.9 %collective-permute-start.9 = (bf16[9,128]{1,0:T(8,128)(2,1)S(1)}, bf16[9,128]{1,0:T(8,128)(2,1)S(1)}, u32[]{:S(2)}, u32[]{:S(2)}) collective-permute-start(bf16[9,128]{1,0:T(8,128)(2,1)S(1)} %fusion.200), channel_id=1, source_target_pairs={{0,1},{1,2},{2,3},{3,4},{4,5},{5,6},{6,7},{7,8},{8,9},{9,10},{10,1... | collective-permute-start | bytes 6920 | tf_op jit(solution)/shard_map/ppermute | solution.py:12
  71.6 5.5 %collective-permute-done.9 = bf16[9,128]{1,0:T(8,128)(2,1)S(1)} collective-permute-done((bf16[9,128]{1,0:T(8,128)(2,1)S(1)}, bf16[9,128]{1,0:T(8,128)(2,1)S(1)}, u32[]{:S(2)}, u32[]{:S(2)}) %collective-permute-start.9) | collective-permute-done | bytes 2336 | tf_op jit(solution)/shard_map/ppermute | solution.py:12
  77.9 4.2 %collective-permute-start.10 = (bf16[1,4096]{1,0:T(2,128)(2,1)S(1)}, bf16[1,4096]{1,0:T(2,128)(2,1)S(1)}, u32[]{:S(2)}, u32[]{:S(2)}) collective-permute-start(bf16[1,4096]{1,0:T(2,128)(2,1)S(1)} %bitcast.362), channel_id=1, source_target_pairs={{0,16},{16,32},{32,48},{48,64},{64,80},{80,96},{96,112},{112,128},... | collective-permute-start | bytes 24584 | tf_op jit(solution)/shard_map/ppermute | solution.py:12
  82.2 0.7 collective-permute-done.10
  83.1 1.9 %collective-permute-start.11 = (bf16[5,256]{1,0:T(8,128)(2,1)S(1)}, bf16[5,256]{1,0:T(8,128)(2,1)S(1)}, u32[]{:S(2)}, u32[]{:S(2)}) collective-permute-start(bf16[5,256]{1,0:T(8,128)(2,1)S(1)} %fusion.199), channel_id=1, source_target_pairs={{0,1},{1,2},{2,3},{3,4},{4,5},{5,6},{6,7},{7,8},{8,9},{9,10},{10,1... | collective-permute-start | bytes 7688 | tf_op jit(solution)/shard_map/ppermute | solution.py:12
  85.1 5.6 %collective-permute-done.11 = bf16[5,256]{1,0:T(8,128)(2,1)S(1)} collective-permute-done((bf16[5,256]{1,0:T(8,128)(2,1)S(1)}, bf16[5,256]{1,0:T(8,128)(2,1)S(1)}, u32[]{:S(2)}, u32[]{:S(2)}) %collective-permute-start.11) | collective-permute-done | bytes 2592 | tf_op jit(solution)/shard_map/ppermute | solution.py:12
  91.1 4.2 %collective-permute-start.12 = (bf16[1,8,512]{2,1,0:T(8,128)(2,1)S(1)}, bf16[1,8,512]{2,1,0:T(8,128)(2,1)S(1)}, u32[]{:S(2)}, u32[]{:S(2)}) collective-permute-start(bf16[1,8,512]{2,1,0:T(8,128)(2,1)S(1)} %slice_bitcast_fusion), channel_id=1, source_target_pairs={{0,16},{16,32},{32,48},{48,64},{64,80},{80,96},{96,112},{112,128},... | collective-permute-start | bytes 24584 | tf_op jit(solution)/shard_map/ppermute | solution.py:12
  95.4 0.8 collective-permute-done.12
  96.2 1.9 %collective-permute-start.13 = (bf16[3,7,512]{2,1,0:T(8,128)(2,1)S(1)}, bf16[3,7,512]{2,1,0:T(8,128)(2,1)S(1)}, u32[]{:S(2)}, u32[]{:S(2)}) collective-permute-start(bf16[3,7,512]{2,1,0:T(8,128)(2,1)S(1)} %pad_maximum_fusion.6), channel_id=1, source_target_pairs={{0,1},{1,2},{2,3},{3,4},{4,5},{5,6},{6,7},{7,8},{8,9},{9,10},{10,1... | collective-permute-start | bytes 64520 | tf_op jit(solution)/shard_map/ppermute | solution.py:12
  98.2 5.9 %collective-permute-done.13 = bf16[3,7,512]{2,1,0:T(8,128)(2,1)S(1)} collective-permute-done((bf16[3,7,512]{2,1,0:T(8,128)(2,1)S(1)}, bf16[3,7,512]{2,1,0:T(8,128)(2,1)S(1)}, u32[]{:S(2)}, u32[]{:S(2)}) %collective-permute-start.13) | collective-permute-done | bytes 21536 | tf_op jit(solution)/shard_map/ppermute | solution.py:12
  104.5 42.4 %all-gather.2 = bf16[32,7,512]{2,1,0:T(8,128)(2,1)S(1)} all-gather(bf16[1,7,512]{2,1,0:T(8,128)(2,1)S(1)} %fusion.123), channel_id=2, replica_groups=mesh['gx'=32,'gy'=16] {'gx'}, dimensions={0}, use_global_device_ids=true | all-gather | bytes 236544 | tf_op jit(solution)/shard_map/all_gather | solution.py:95
  149.3 21.5 %all-gather.1 = bf16[8,8192]{1,0:T(8,128)(2,1)S(1)} all-gather(bf16[8,512]{1,0:T(8,128)(2,1)S(1)} %fusion.135), channel_id=3, replica_groups=mesh['gx'=32,'gy'=16] {'gy'}, dimensions={1}, use_global_device_ids=true | all-gather | bytes 139264 | tf_op jit(solution)/shard_map/all_gather | solution.py:98
  172.6 0.6 reshape_reshape.3
  (262 shorter events, 13.5 us)
Async XLA Ops:
  0.6 90.3 %copy-start = (bf16[256,512]{1,0:T(8,128)(2,1)S(1)}, bf16[256,512]{1,0:T(8,128)(2,1)}, u32[]{:S(2)}) copy-start(bf16[256,512]{1,0:T(8,128)(2,1)} %param.23) | copy-start | bytes 786436
  1.7 11.0 %collective-permute-start = (bf16[2,128,32]{2,1,0:T(8,128)(2,1)S(1)}, bf16[2,128,32]{2,1,0:T(8,128)(2,1)S(1)}, u32[]{:S(2)}, u32[]{:S(2)}) collective-permute-start(bf16[2,128,32]{2,1,0:T(8,128)(2,1)S(1)} %slice.906), channel_id=1, source_target_pairs={{0,16},{16,32},{32,48},{48,64},{64,80},{80,96},{96,112},{112,128},... | collective-permute-start | bytes 49160 | tf_op jit(solution)/shard_map/ppermute | solution.py:20
  3.6 9.2 %collective-permute-start.1 = (bf16[2,128,32]{2,1,0:T(8,128)(2,1)S(1)}, bf16[2,128,32]{2,1,0:T(8,128)(2,1)S(1)}, u32[]{:S(2)}, u32[]{:S(2)}) collective-permute-start(bf16[2,128,32]{2,1,0:T(8,128)(2,1)S(1)} %slice.908), channel_id=1, source_target_pairs={{16,0},{32,16},{48,32},{64,48},{80,64},{96,80},{112,96},{128,112},... | collective-permute-start | bytes 49160 | tf_op jit(solution)/shard_map/ppermute | solution.py:23
  10.6 10.5 %copy-start.9 = (f32[9,128]{1,0:T(8,128)S(1)}, f32[9,128]{1,0:T(8,128)}, u32[]{:S(2)}) copy-start(f32[9,128]{1,0:T(8,128)} %param.20) | copy-start | bytes 13828
  13.1 12.0 %collective-permute-start.2 = (bf16[36,2,32]{1,2,0:T(8,128)(2,1)S(1)}, bf16[36,2,32]{1,2,0:T(8,128)(2,1)S(1)}, u32[]{:S(2)}, u32[]{:S(2)}) collective-permute-start(bf16[36,2,32]{1,2,0:T(8,128)(2,1)S(1)} %get-tuple-element.2), channel_id=1, source_target_pairs={{0,1},{1,2},{2,3},{3,4},{4,5},{5,6},{6,7},{7,8},{8,9},{9,10},{10,1... | collective-permute-start | bytes 13832 | tf_op jit(solution)/shard_map/ppermute | solution.py:20
  16.6 10.3 %collective-permute-start.3 = (bf16[36,2,32]{1,2,0:T(8,128)(2,1)S(1)}, bf16[36,2,32]{1,2,0:T(8,128)(2,1)S(1)}, u32[]{:S(2)}, u32[]{:S(2)}) collective-permute-start(bf16[36,2,32]{1,2,0:T(8,128)(2,1)S(1)} %get-tuple-element.3), channel_id=1, source_target_pairs={{1,0},{2,1},{3,2},{4,3},{5,4},{6,5},{7,6},{8,7},{9,8},{10,9},{11,1... | collective-permute-start | bytes 13832 | tf_op jit(solution)/shard_map/ppermute | solution.py:23
  28.8 1.5 copy-start.31
  30.9 1.6 copy-start.2
  32.5 5.6 %copy-start.1 = (bf16[32,4096]{1,0:T(8,128)(2,1)}, bf16[32,4096]{1,0:T(8,128)(2,1)S(1)}, u32[]{:S(2)}) copy-start(bf16[32,4096]{1,0:T(8,128)(2,1)S(1)} %add_convert_fusion) | copy-start | bytes 786436
  32.7 4.7 %collective-permute-start.4 = (bf16[1,4096]{1,0:T(2,128)(2,1)S(1)}, bf16[1,4096]{1,0:T(2,128)(2,1)S(1)}, u32[]{:S(2)}, u32[]{:S(2)}) collective-permute-start(bf16[1,4096]{1,0:T(2,128)(2,1)S(1)} %slice.1171), channel_id=1, source_target_pairs={{0,16},{16,32},{32,48},{48,64},{64,80},{80,96},{96,112},{112,128},... | collective-permute-start | bytes 24584 | tf_op jit(solution)/shard_map/ppermute | solution.py:12
  38.1 7.8 %collective-permute-start.5 = (bf16[33,32]{1,0:T(8,128)(2,1)S(1)}, bf16[33,32]{1,0:T(8,128)(2,1)S(1)}, u32[]{:S(2)}, u32[]{:S(2)}) collective-permute-start(bf16[33,32]{1,0:T(8,128)(2,1)S(1)} %fusion.160), channel_id=1, source_target_pairs={{0,1},{1,2},{2,3},{3,4},{4,5},{5,6},{6,7},{7,8},{8,9},{9,10},{10,1... | collective-permute-start | bytes 6344 | tf_op jit(solution)/shard_map/ppermute | solution.py:12
  49.1 15.0 %copy-start.10 = (f32[64]{0:T(128)S(1)}, f32[64]{0:T(128)}, u32[]{:S(2)}) copy-start(f32[64]{0:T(128)} %get-tuple-element.81) | copy-start | bytes 772
  49.1 15.0 %copy-start.11 = (f32[64]{0:T(128)S(1)}, f32[64]{0:T(128)}, u32[]{:S(2)}) copy-start(f32[64]{0:T(128)} %get-tuple-element.82) | copy-start | bytes 772
  49.1 15.0 %copy-start.12 = (f32[64]{0:T(128)S(1)}, f32[64]{0:T(128)}, u32[]{:S(2)}) copy-start(f32[64]{0:T(128)} %get-tuple-element.83) | copy-start | bytes 772
  49.1 15.0 %copy-start.13 = (f32[64]{0:T(128)S(1)}, f32[64]{0:T(128)}, u32[]{:S(2)}) copy-start(f32[64]{0:T(128)} %get-tuple-element.84) | copy-start | bytes 772
  49.1 15.0 %copy-start.14 = (f32[64]{0:T(128)S(1)}, f32[64]{0:T(128)}, u32[]{:S(2)}) copy-start(f32[64]{0:T(128)} %get-tuple-element.85) | copy-start | bytes 772
  49.1 15.0 %copy-start.15 = (f32[64]{0:T(128)S(1)}, f32[64]{0:T(128)}, u32[]{:S(2)}) copy-start(f32[64]{0:T(128)} %get-tuple-element.86) | copy-start | bytes 772
  49.1 15.0 %copy-start.16 = (f32[64]{0:T(128)S(1)}, f32[64]{0:T(128)}, u32[]{:S(2)}) copy-start(f32[64]{0:T(128)} %get-tuple-element.87) | copy-start | bytes 772
  49.1 15.0 %copy-start.17 = (f32[64]{0:T(128)S(1)}, f32[64]{0:T(128)}, u32[]{:S(2)}) copy-start(f32[64]{0:T(128)} %get-tuple-element.88) | copy-start | bytes 772
  49.1 15.0 %copy-start.18 = (f32[64]{0:T(128)S(1)}, f32[64]{0:T(128)}, u32[]{:S(2)}) copy-start(f32[64]{0:T(128)} %get-tuple-element.89) | copy-start | bytes 772
  49.9 5.7 %collective-permute-start.6 = (bf16[1,4096]{1,0:T(2,128)(2,1)S(1)}, bf16[1,4096]{1,0:T(2,128)(2,1)S(1)}, u32[]{:S(2)}, u32[]{:S(2)}) collective-permute-start(bf16[1,4096]{1,0:T(2,128)(2,1)S(1)} %slice.974), channel_id=1, source_target_pairs={{0,16},{16,32},{32,48},{48,64},{64,80},{80,96},{96,112},{112,128},... | collective-permute-start | bytes 24584 | tf_op jit(solution)/shard_map/ppermute | solution.py:12
  54.8 9.6 %copy-start.30 = (bf16[64,128]{1,0:T(8,128)(2,1)S(1)}, bf16[64,128]{1,0:T(8,128)(2,1)}, u32[]{:S(2)}) copy-start(bf16[64,128]{1,0:T(8,128)(2,1)} %param.19) | copy-start | bytes 49156
  55.8 7.6 %collective-permute-start.7 = (bf16[17,64]{1,0:T(8,128)(2,1)S(1)}, bf16[17,64]{1,0:T(8,128)(2,1)S(1)}, u32[]{:S(2)}, u32[]{:S(2)}) collective-permute-start(bf16[17,64]{1,0:T(8,128)(2,1)S(1)} %fusion.198), channel_id=1, source_target_pairs={{0,1},{1,2},{2,3},{3,4},{4,5},{5,6},{6,7},{7,8},{8,9},{9,10},{10,1... | collective-permute-start | bytes 6536 | tf_op jit(solution)/shard_map/ppermute | solution.py:12
  58.0 19.3 %copy-start.19 = (f32[128]{0:T(128)S(1)}, f32[128]{0:T(128)}, u32[]{:S(2)}) copy-start(f32[128]{0:T(128)} %get-tuple-element.72) | copy-start | bytes 1540
  58.0 19.3 %copy-start.20 = (f32[128]{0:T(128)S(1)}, f32[128]{0:T(128)}, u32[]{:S(2)}) copy-start(f32[128]{0:T(128)} %get-tuple-element.73) | copy-start | bytes 1540
  58.0 19.3 %copy-start.21 = (f32[128]{0:T(128)S(1)}, f32[128]{0:T(128)}, u32[]{:S(2)}) copy-start(f32[128]{0:T(128)} %get-tuple-element.74) | copy-start | bytes 1540
  58.1 19.3 %copy-start.22 = (f32[128]{0:T(128)S(1)}, f32[128]{0:T(128)}, u32[]{:S(2)}) copy-start(f32[128]{0:T(128)} %get-tuple-element.75) | copy-start | bytes 1540
  58.1 19.3 %copy-start.23 = (f32[128]{0:T(128)S(1)}, f32[128]{0:T(128)}, u32[]{:S(2)}) copy-start(f32[128]{0:T(128)} %get-tuple-element.76) | copy-start | bytes 1540
  58.1 19.3 %copy-start.24 = (f32[128]{0:T(128)S(1)}, f32[128]{0:T(128)}, u32[]{:S(2)}) copy-start(f32[128]{0:T(128)} %get-tuple-element.77) | copy-start | bytes 1540
  58.1 19.3 %copy-start.25 = (f32[128]{0:T(128)S(1)}, f32[128]{0:T(128)}, u32[]{:S(2)}) copy-start(f32[128]{0:T(128)} %get-tuple-element.78) | copy-start | bytes 1540
  58.1 19.3 %copy-start.26 = (f32[128]{0:T(128)S(1)}, f32[128]{0:T(128)}, u32[]{:S(2)}) copy-start(f32[128]{0:T(128)} %get-tuple-element.79) | copy-start | bytes 1540
  58.1 19.3 %copy-start.27 = (f32[128]{0:T(128)S(1)}, f32[128]{0:T(128)}, u32[]{:S(2)}) copy-start(f32[128]{0:T(128)} %get-tuple-element.80) | copy-start | bytes 1540
  58.1 19.3 %copy-start.29 = (bf16[128,256]{1,0:T(8,128)(2,1)S(1)}, bf16[128,256]{1,0:T(8,128)(2,1)}, u32[]{:S(2)}) copy-start(bf16[128,256]{1,0:T(8,128)(2,1)} %param.21) | copy-start | bytes 196612
  64.1 26.8 %copy-start.4 = (f32[1,256]{1,0:T(1,128)S(1)}, f32[1,256]{1,0:T(1,128)}, u32[]{:S(2)}) copy-start(f32[1,256]{1,0:T(1,128)} %get-tuple-element.67) | copy-start | bytes 3076
  64.1 26.9 %copy-start.5 = (f32[1,256]{1,0:T(1,128)S(1)}, f32[1,256]{1,0:T(1,128)}, u32[]{:S(2)}) copy-start(f32[1,256]{1,0:T(1,128)} %get-tuple-element.68) | copy-start | bytes 3076
  64.1 26.9 %copy-start.6 = (f32[1,256]{1,0:T(1,128)S(1)}, f32[1,256]{1,0:T(1,128)}, u32[]{:S(2)}) copy-start(f32[1,256]{1,0:T(1,128)} %get-tuple-element.69) | copy-start | bytes 3076
  64.1 26.9 %copy-start.7 = (f32[1,256]{1,0:T(1,128)S(1)}, f32[1,256]{1,0:T(1,128)}, u32[]{:S(2)}) copy-start(f32[1,256]{1,0:T(1,128)} %get-tuple-element.70) | copy-start | bytes 3076
  64.1 26.9 %copy-start.8 = (f32[1,256]{1,0:T(1,128)S(1)}, f32[1,256]{1,0:T(1,128)}, u32[]{:S(2)}) copy-start(f32[1,256]{1,0:T(1,128)} %get-tuple-element.71) | copy-start | bytes 3076
  64.2 31.2 %copy-start.3 = (f32[4,9,512]{2,0,1:T(4,128)S(1)}, f32[4,9,512]{2,0,1:T(4,128)}, u32[]{:S(2)}) copy-start(f32[4,9,512]{2,0,1:T(4,128)} %param.24) | copy-start | bytes 221188
  64.4 39.9 %copy-start.28 = (bf16[4,512,512]{2,1,0:T(8,128)(2,1)S(1)}, bf16[4,512,512]{2,1,0:T(8,128)(2,1)}, u32[]{:S(2)}) copy-start(bf16[4,512,512]{2,1,0:T(8,128)(2,1)} %param.25) | copy-start | bytes 6291460
  64.9 4.6 %collective-permute-start.8 = (bf16[1,4096]{1,0:T(2,128)(2,1)S(1)}, bf16[1,4096]{1,0:T(2,128)(2,1)S(1)}, u32[]{:S(2)}, u32[]{:S(2)}) collective-permute-start(bf16[1,4096]{1,0:T(2,128)(2,1)S(1)} %bitcast.361), channel_id=1, source_target_pairs={{0,16},{16,32},{32,48},{48,64},{64,80},{80,96},{96,112},{112,128},... | collective-permute-start | bytes 24584 | tf_op jit(solution)/shard_map/ppermute | solution.py:12
  69.5 7.6 %collective-permute-start.9 = (bf16[9,128]{1,0:T(8,128)(2,1)S(1)}, bf16[9,128]{1,0:T(8,128)(2,1)S(1)}, u32[]{:S(2)}, u32[]{:S(2)}) collective-permute-start(bf16[9,128]{1,0:T(8,128)(2,1)S(1)} %fusion.200), channel_id=1, source_target_pairs={{0,1},{1,2},{2,3},{3,4},{4,5},{5,6},{6,7},{7,8},{8,9},{9,10},{10,1... | collective-permute-start | bytes 6920 | tf_op jit(solution)/shard_map/ppermute | solution.py:12
  77.9 5.1 %collective-permute-start.10 = (bf16[1,4096]{1,0:T(2,128)(2,1)S(1)}, bf16[1,4096]{1,0:T(2,128)(2,1)S(1)}, u32[]{:S(2)}, u32[]{:S(2)}) collective-permute-start(bf16[1,4096]{1,0:T(2,128)(2,1)S(1)} %bitcast.362), channel_id=1, source_target_pairs={{0,16},{16,32},{32,48},{48,64},{64,80},{80,96},{96,112},{112,128},... | collective-permute-start | bytes 24584 | tf_op jit(solution)/shard_map/ppermute | solution.py:12
  83.1 7.6 %collective-permute-start.11 = (bf16[5,256]{1,0:T(8,128)(2,1)S(1)}, bf16[5,256]{1,0:T(8,128)(2,1)S(1)}, u32[]{:S(2)}, u32[]{:S(2)}) collective-permute-start(bf16[5,256]{1,0:T(8,128)(2,1)S(1)} %fusion.199), channel_id=1, source_target_pairs={{0,1},{1,2},{2,3},{3,4},{4,5},{5,6},{6,7},{7,8},{8,9},{9,10},{10,1... | collective-permute-start | bytes 7688 | tf_op jit(solution)/shard_map/ppermute | solution.py:12
  91.1 5.0 %collective-permute-start.12 = (bf16[1,8,512]{2,1,0:T(8,128)(2,1)S(1)}, bf16[1,8,512]{2,1,0:T(8,128)(2,1)S(1)}, u32[]{:S(2)}, u32[]{:S(2)}) collective-permute-start(bf16[1,8,512]{2,1,0:T(8,128)(2,1)S(1)} %slice_bitcast_fusion), channel_id=1, source_target_pairs={{0,16},{16,32},{32,48},{48,64},{64,80},{80,96},{96,112},{112,128},... | collective-permute-start | bytes 24584 | tf_op jit(solution)/shard_map/ppermute | solution.py:12
  96.2 7.8 %collective-permute-start.13 = (bf16[3,7,512]{2,1,0:T(8,128)(2,1)S(1)}, bf16[3,7,512]{2,1,0:T(8,128)(2,1)S(1)}, u32[]{:S(2)}, u32[]{:S(2)}) collective-permute-start(bf16[3,7,512]{2,1,0:T(8,128)(2,1)S(1)} %pad_maximum_fusion.6), channel_id=1, source_target_pairs={{0,1},{1,2},{2,3},{3,4},{4,5},{5,6},{6,7},{7,8},{8,9},{9,10},{10,1... | collective-permute-start | bytes 64520 | tf_op jit(solution)/shard_map/ppermute | solution.py:12

commit v2 on v1

--- a/solution.py
+++ b/solution.py
@@ -65,25 +65,58 @@
     return point_flat(total, weight, half_rows, half_cols).astype(jnp.bfloat16)
 
 
+def strided_flat(ext, taps, weight):
+    chans = taps.shape[1]
+    rows = (ext.shape[0] - 1) // 2
+    cols = (ext.shape[1] // chans - 1) // 2
+    tiled = jnp.tile(taps, (1, cols))
+    total = jnp.zeros((rows, cols * chans), jnp.float32)
+    for first in range(3):
+        slab = ext[first : first + 2 * rows : 2]
+        head = slab[:, : 2 * cols * chans].reshape(rows, cols, 2 * chans)
+        tail = slab[:, chans:].reshape(rows, cols, 2 * chans)
+        pieces = (head[:, :, :chans], head[:, :, chans:], tail[:, :, chans:])
+        for second, piece in enumerate(pieces):
+            piece = piece.reshape(rows, cols * chans)
+            total = total + piece.astype(jnp.float32) * tiled[3 * first + second]
+    return point_flat(total, weight, rows, cols).astype(jnp.bfloat16)
+
+
 def local(field, dw0, pw0, dw1, pw1, dw2, pw2, dw3, pw3, dw4, pw4, dwc, pwc):
     chans = dw0.shape[1]
     rows = field.shape[0]
     cols = field.shape[1] // chans
-    grid = field.reshape(rows, cols, chans)
-    padded = padded_2(grid, (("gx", 0), ("gy", 1)), 2)
-    flat_pad = padded.reshape(rows + 4, (cols + 4) * chans)
-    tiled = jnp.tile(dw0, (1, cols))
-    total = jnp.zeros((rows, cols * chans), jnp.float32)
+    depth = 4
+    margin = 2**depth - 1
+    upper = shifted(field[-margin - 2 :], "gx", 1)
+    lower = shifted(field[:2], "gx", -1)
+    stacked = jnp.concatenate([upper, field, lower], axis=0)
+    leftside = shifted(stacked[:, -(margin + 2) * chans :], "gy", 1)
+    rightside = shifted(stacked[:, : 2 * chans], "gy", -1)
+    flat_pad = jnp.concatenate([leftside, stacked, rightside], axis=1)
+    ext_rows = rows + margin
+    ext_cols = cols + margin
+    tiled = jnp.tile(dw0, (1, ext_cols))
+    total = jnp.zeros((ext_rows, ext_cols * chans), jnp.float32)
     for first in range(3):
         for second in range(3):
             piece = flat_pad[
-                2 * first : 2 * first + rows, 2 * second * chans : 2 * second * chans + cols * chans
+                2 * first : 2 * first + ext_rows,
+                2 * second * chans : 2 * second * chans + ext_cols * chans,
             ]
             total = total + piece.astype(jnp.float32) * tiled[3 * first + second]
-    hidden = (field.astype(jnp.float32) + point_flat(total, pw0, rows, cols)).astype(jnp.bfloat16)
-    fine = hidden
+    centre = flat_pad[2 : 2 + ext_rows, 2 * chans : 2 * chans + ext_cols * chans]
+    hidden = (centre.astype(jnp.float32) + point_flat(total, pw0, ext_rows, ext_cols)).astype(
+        jnp.bfloat16
+    )
+    row_ok = (lax.axis_index("gx") > 0) | (lax.broadcasted_iota(jnp.int32, hidden.shape, 0) >= margin)
+    col_ok = (lax.axis_index("gy") > 0) | (
+        lax.broadcasted_iota(jnp.int32, hidden.shape, 1) >= margin * chans
+    )
+    hidden = jnp.where(row_ok & col_ok, hidden, jnp.zeros_like(hidden))
+    fine = hidden[margin:, margin * chans :]
     for taps, weight in ((dw1, pw1), (dw2, pw2), (dw3, pw3), (dw4, pw4)):
-        hidden = down_level(hidden, taps, weight, True, True)
+        hidden = strided_flat(hidden, taps, weight)
     coarse_chans = dwc.shape[2]
     halo = 2 ** (LC - 1) - 1
     grid4 = hidden.reshape(hidden.shape[0], -1, coarse_chans)

time: 176 us -> 142 us (0.81)
  waiting for transfers between devices: 32.9 us -> 5.66 us
  starting transfers between devices: 42.6 us -> 17.7 us
  local copies, waits for them, and re-layouts: 25.2 us -> 40.9 us
  matrix products: 2.91 us -> 7.61 us
  blocking collectives: 63.9 us -> 61.8 us
    ppermute x10 -> x6, waiting for transfers between devices: 28.5 us -> 5.66 us  [shifted(): lax.ppermute(value, axis, [(source, source + steps) for source in range(l...]
    ppermute x10 -> x6, starting transfers between devices: 31.6 us -> 17.7 us  [shifted(): lax.ppermute(value, axis, [(source, source + steps) for source in range(l...]
    ppermute x4 -> x0, starting transfers between devices: 11 us -> none  [the longest x2 5.76 us: padded_2(): lax.ppermute(lax.slice_in_dim(block, 0, width, axis=dim), axis, backward)]
    convert_element_type x16 -> x40, local copies, waits for them, and re-layouts: 1.37 us -> 6.94 us  [the longest x36 6.18 us: strided_flat(): total = total + piece.astype(jnp.float32) * tiled[3 * first + second]]
    slice x47 -> x39, local copies, waits for them, and re-layouts: 9.49 us -> 14.1 us  [the longest x4 5.76 us: strided_flat(): total = total + piece.astype(jnp.float32) * tiled[3 * first + second]]
    ppermute x4 -> x0, waiting for transfers between devices: 4.39 us -> none  [the longest x2 2.64 us: padded_2(): lax.ppermute(lax.slice_in_dim(block, block.shape[dim] - width, None, axis...]
    dot_general x4, matrix products: 0.89 us -> 5.07 us  [strided_cells(): mixed = jnp.dot(flat, weight, preferred_element_type=jnp.float32)]
    unnamed x92 -> x75, local copies, waits for them, and re-layouts: 0.38 us -> 3.73 us
  transfers between devices with their start and end apart: 14 -> 6, of which waited for: 11 -> 3; matrix products, arithmetic and copies ran while one was open for 7% -> 7% of each run, Pallas kernels for 0% -> 0%
where the time goes in v2:
time: 142 us; the launch traced here: 140 us
  blocking collectives  61.8 us (44%)
  local copies, waits for them, and re-layouts  40.9 us (29%)
  starting transfers between devices  17.7 us (12%)
  matrix products  7.61 us (5%)
  waiting for transfers between devices  5.66 us (4%)
  other arithmetic  4.19 us (3%)
  between operations  2.36 us (2%)
    all_gather x1, blocking collectives, local(): hidden = lax.all_gather(hidden, 'gx', axis=0, tiled=True)  40.3 us
    all_gather x1, blocking collectives, local(): hidden = lax.all_gather(hidden, 'gy', axis=1, tiled=True)  21.5 us
    ppermute x6, starting transfers between devices, shifted(): lax.ppermute(value, axis, [(source, source + steps) for source in range(l...  17.7 us
    convert_element_type x36, local copies, waits for them, and re-layouts, strided_flat(): total = total + piece.astype(jnp.float32) * tiled[3 * first + second]  6.18 us
    slice x4, local copies, waits for them, and re-layouts, strided_flat(): total = total + piece.astype(jnp.float32) * tiled[3 * first + second]  5.76 us
    ppermute x6, waiting for transfers between devices, shifted(): lax.ppermute(value, axis, [(source, source + steps) for source in range(l...  5.66 us
    dot_general x4, matrix products, strided_cells(): mixed = jnp.dot(flat, weight, preferred_element_type=jnp.float32)  5.07 us
    unnamed x75, local copies, waits for them, and re-layouts  3.73 us
  transfers between devices with their start and end apart: 6, of which 3 were waited for; matrix products, arithmetic and copies ran while one was open for 7% of the time, Pallas kernels for 0%

profile of v2, /device:TPU:6, one launch (start us, length us, event | category | flops | bytes accessed | tf_op | source)
XLA Modules:
  0.0 140.3 jit_solution(11028981407478511368)
XLA Ops:
  0.7 1.0 slice.912
  1.7 1.8 %collective-permute-start = (bf16[17,4096]{1,0:T(8,128)(2,1)S(1)}, bf16[17,4096]{1,0:T(8,128)(2,1)S(1)}, u32[]{:S(2)}, u32[]{:S(2)}) collective-permute-start(bf16[17,4096]{1,0:T(8,128)(2,1)S(1)} %slice.912), channel_id=1, source_target_pairs={{0,16},{16,32},{32,48},{48,64},{64,80},{80,96},{96,112},{112,128},... | collective-permute-start | bytes 417800 | tf_op jit(solution)/shard_map/ppermute | solution.py:12
  3.5 0.9 slice.913
  4.3 1.3 collective-permute-start.1
  5.6 1.0 slice_bitcast_fusion.54
  6.6 1.6 %slice_bitcast_fusion.45 = (f32[32]{0:T(128)}, f32[32]{0:T(128)}, f32[32]{0:T(128)}, f32[32]{0:T(128)}, f32[32]{0:T(128)}, /*index=5*/f32[32]{0:T(128)}, f32[32]{0:T(128)}, f32[32]{0:T(128)}, f32[32]{0:T(128)}) fusion(f32[9,32]{1,0:T(8,128)} %param.16), kind=kLoop, calls=%fused_computation.242 | loop fusion | bytes 2304 | tf_op jit(solution)/shard_map/slice | solution.py:81
  8.2 1.6 %slice_bitcast_fusion.36 = (f32[64]{0:T(128)}, f32[64]{0:T(128)}, f32[64]{0:T(128)}, f32[64]{0:T(128)}, f32[64]{0:T(128)}, /*index=5*/f32[64]{0:T(128)}, f32[64]{0:T(128)}, f32[64]{0:T(128)}, f32[64]{0:T(128)}) fusion(f32[9,64]{1,0:T(8,128)} %param.18), kind=kLoop, calls=%fused_computation.233 | loop fusion | bytes 4608 | tf_op jit(solution)/shard_map/slice | solution.py:81
  9.8 1.0 fusion.186
  10.8 1.6 %slice_bitcast_fusion.27 = (f32[128]{0:T(128)S(1)}, f32[128]{0:T(128)S(1)}, f32[128]{0:T(128)S(1)}, f32[128]{0:T(128)S(1)}, f32[128]{0:T(128)}, /*index=5*/f32[1...) fusion(f32[9,128]{1,0:T(8,128)} %param.20), kind=kLoop, calls=%fused_computation.224 | loop fusion | bytes 9216 | tf_op jit(solution)/shard_map/slice | solution.py:81
  12.4 1.1 pad_maximum_fusion
  13.6 3.5 %collective-permute-start.2 = (bf16[51,544]{1,0:T(8,128)(2,1)S(1)}, bf16[51,544]{1,0:T(8,128)(2,1)S(1)}, u32[]{:S(2)}, u32[]{:S(2)}) collective-permute-start(bf16[51,544]{1,0:T(8,128)(2,1)S(1)} %slice.1167), channel_id=1, source_target_pairs={{0,1},{1,2},{2,3},{3,4},{4,5},{5,6},{6,7},{7,8},{8,9},{9,10},{10,1... | collective-permute-start | bytes 166472 | tf_op jit(solution)/shard_map/ppermute | solution.py:12
  17.1 0.5 compare_or_fusion
  18.5 4.5 %collective-permute-start.3 = (bf16[51,64]{1,0:T(8,128)(2,1)S(1)}, bf16[51,64]{1,0:T(8,128)(2,1)S(1)}, u32[]{:S(2)}, u32[]{:S(2)}) collective-permute-start(bf16[51,64]{1,0:T(8,128)(2,1)S(1)} %slice.1171), channel_id=1, source_target_pairs={{1,0},{2,1},{3,2},{4,3},{5,4},{6,5},{7,6},{8,7},{9,8},{10,9},{11,1... | collective-permute-start | bytes 19592 | tf_op jit(solution)/shard_map/ppermute | solution.py:12
  23.2 1.1 collective-permute-done.3
  24.4 0.8 concatenate.34
  25.2 1.3 fusion.5
  26.4 1.6 %reshape.640 = bf16[6721,32]{1,0:T(8,128)(2,1)S(1)} reshape(bf16[47,4576]{1,0:T(8,128)(2,1)S(1)} %fusion.5) | data formatting | bytes 860288 | tf_op jit(solution)/shard_map/reshape | solution.py:34
  28.0 1.4 %fusion.13 = f32[6721,32]{0,1:T(8,128)S(1)} fusion(bf16[6721,32]{1,0:T(8,128)(2,1)S(1)} %reshape.640, bf16[32,32]{1,0:T(8,128)(2,1)} %param.15), kind=kOutput, calls=%fused_computation.17 | convolution fusion | flops 15485184 | bytes 1292480 | tf_op jit(solution)/shard_map/dot_general | solution.py:35
  29.5 2.5 %copy.47 = f32[6721,32]{1,0:T(8,128)} copy(f32[6721,32]{0,1:T(8,128)S(1)} %fusion.13) | data formatting | bytes 1720576 | tf_op jit(solution)/shard_map/mul | solution.py:29
  32.0 2.5 %reshape.641 = f32[47,4576]{1,0:T(8,128)S(1)} reshape(f32[6721,32]{1,0:T(8,128)} %copy.47) | data formatting | bytes 1720576 | tf_op jit(solution)/shard_map/reshape | solution.py:36
  34.7 0.4 slice.944
  35.2 0.4 slice.956
  35.6 0.7 slice.968
  36.5 0.3 reshape.642
  38.2 0.3 reshape.644
  39.5 0.9 reshape.677
  41.0 0.9 copy.93
  41.9 1.0 copy.61
  43.4 0.8 reshape.680
  46.1 0.8 reshape.678
  47.5 0.9 copy.95
  48.4 1.0 copy.65
  49.7 0.4 fusion.33
  53.7 0.4 slice.1016
  54.1 0.4 slice.1028
  54.4 0.4 slice.1040
  56.7 3.6 %collective-permute-start.4 = (bf16[1,8,512]{2,1,0:T(8,128)(2,1)S(1)}, bf16[1,8,512]{2,1,0:T(8,128)(2,1)S(1)}, u32[]{:S(2)}, u32[]{:S(2)}) collective-permute-start(bf16[1,8,512]{2,1,0:T(8,128)(2,1)S(1)} %slice_bitcast_fusion), channel_id=1, source_target_pairs={{0,16},{16,32},{32,48},{48,64},{64,80},{80,96},{96,112},{112,128},... | collective-permute-start | bytes 24584 | tf_op jit(solution)/shard_map/ppermute | solution.py:12
  60.4 0.8 collective-permute-done.4
  61.1 3.1 %collective-permute-start.5 = (bf16[3,7,512]{2,1,0:T(8,128)(2,1)S(1)}, bf16[3,7,512]{2,1,0:T(8,128)(2,1)S(1)}, u32[]{:S(2)}, u32[]{:S(2)}) collective-permute-start(bf16[3,7,512]{2,1,0:T(8,128)(2,1)S(1)} %pad_maximum_fusion.1), channel_id=1, source_target_pairs={{0,1},{1,2},{2,3},{3,4},{4,5},{5,6},{6,7},{7,8},{8,9},{9,10},{10,1... | collective-permute-start | bytes 64520 | tf_op jit(solution)/shard_map/ppermute | solution.py:12
  64.3 0.9 slice.1178
  65.2 3.8 %collective-permute-done.5 = bf16[3,7,512]{2,1,0:T(8,128)(2,1)S(1)} collective-permute-done((bf16[3,7,512]{2,1,0:T(8,128)(2,1)S(1)}, bf16[3,7,512]{2,1,0:T(8,128)(2,1)S(1)}, u32[]{:S(2)}, u32[]{:S(2)}) %collective-permute-start.5) | collective-permute-done | bytes 21536 | tf_op jit(solution)/shard_map/ppermute | solution.py:12
  69.2 1.3 fusion.114
  70.4 40.3 %all-gather.2 = bf16[32,7,512]{2,1,0:T(8,128)(2,1)S(1)} all-gather(bf16[1,7,512]{2,1,0:T(8,128)(2,1)S(1)} %fusion.114), channel_id=2, replica_groups=mesh['gx'=32,'gy'=16] {'gx'}, dimensions={0}, use_global_device_ids=true | all-gather | bytes 236544 | tf_op jit(solution)/shard_map/all_gather | solution.py:128
  112.5 1.3 fusion.51
  114.0 1.3 fusion.126
  115.3 21.5 %all-gather.1 = bf16[8,8192]{1,0:T(8,128)(2,1)S(1)} all-gather(bf16[8,512]{1,0:T(8,128)(2,1)S(1)} %fusion.126), channel_id=3, replica_groups=mesh['gx'=32,'gy'=16] {'gy'}, dimensions={1}, use_global_device_ids=true | all-gather | bytes 139264 | tf_op jit(solution)/shard_map/all_gather | solution.py:131
  138.3 1.3 fusion.71
  139.6 0.6 reshape_reshape.3
  (244 shorter events, 15.7 us)
Async XLA Ops:
  0.6 55.9 %copy-start = (bf16[256,512]{1,0:T(8,128)(2,1)S(1)}, bf16[256,512]{1,0:T(8,128)(2,1)}, u32[]{:S(2)}) copy-start(bf16[256,512]{1,0:T(8,128)(2,1)} %param.23) | copy-start | bytes 786436
  0.6 22.3 %copy-start.1 = (bf16[32,4096]{1,0:T(8,128)(2,1)S(1)}, bf16[32,4096]{1,0:T(8,128)(2,1)}, u32[]{:S(2)}) copy-start(bf16[32,4096]{1,0:T(8,128)(2,1)} %param.13) | copy-start | bytes 786436
  1.7 10.7 %collective-permute-start = (bf16[17,4096]{1,0:T(8,128)(2,1)S(1)}, bf16[17,4096]{1,0:T(8,128)(2,1)S(1)}, u32[]{:S(2)}, u32[]{:S(2)}) collective-permute-start(bf16[17,4096]{1,0:T(8,128)(2,1)S(1)} %slice.912), channel_id=1, source_target_pairs={{0,16},{16,32},{32,48},{48,64},{64,80},{80,96},{96,112},{112,128},... | collective-permute-start | bytes 417800 | tf_op jit(solution)/shard_map/ppermute | solution.py:12
  4.3 8.1 %collective-permute-start.1 = (bf16[2,4096]{1,0:T(2,128)(2,1)S(1)}, bf16[2,4096]{1,0:T(2,128)(2,1)S(1)}, u32[]{:S(2)}, u32[]{:S(2)}) collective-permute-start(bf16[2,4096]{1,0:T(2,128)(2,1)S(1)} %slice.913), channel_id=1, source_target_pairs={{16,0},{32,16},{48,32},{64,48},{80,64},{96,80},{112,96},{128,112},... | collective-permute-start | bytes 49160 | tf_op jit(solution)/shard_map/ppermute | solution.py:12
  13.6 9.4 %collective-permute-start.2 = (bf16[51,544]{1,0:T(8,128)(2,1)S(1)}, bf16[51,544]{1,0:T(8,128)(2,1)S(1)}, u32[]{:S(2)}, u32[]{:S(2)}) collective-permute-start(bf16[51,544]{1,0:T(8,128)(2,1)S(1)} %slice.1167), channel_id=1, source_target_pairs={{0,1},{1,2},{2,3},{3,4},{4,5},{5,6},{6,7},{7,8},{8,9},{9,10},{10,1... | collective-permute-start | bytes 166472 | tf_op jit(solution)/shard_map/ppermute | solution.py:12
  18.5 5.9 %collective-permute-start.3 = (bf16[51,64]{1,0:T(8,128)(2,1)S(1)}, bf16[51,64]{1,0:T(8,128)(2,1)S(1)}, u32[]{:S(2)}, u32[]{:S(2)}) collective-permute-start(bf16[51,64]{1,0:T(8,128)(2,1)S(1)} %slice.1171), channel_id=1, source_target_pairs={{1,0},{2,1},{3,2},{4,3},{5,4},{6,5},{7,6},{8,7},{9,8},{10,9},{11,1... | collective-permute-start | bytes 19592 | tf_op jit(solution)/shard_map/ppermute | solution.py:12
  32.0 2.5 %copy-start.32 = (pred[47]{0:T(512)(128)(4,1)S(1)}, pred[47]{0:T(512)(128)(4,1)}, u32[]{:S(2)}) copy-start(pred[47]{0:T(512)(128)(4,1)} %compare_or_fusion) | copy-start | bytes 145
  46.9 2.7 %copy-start.2 = (f32[1633,32]{0,1:T(8,128)S(1)}, f32[1633,32]{0,1:T(8,128)}, u32[]{:S(2)}) copy-start(f32[1633,32]{0,1:T(8,128)} %reshape.677) | copy-start | bytes 627076
  46.9 2.7 %copy-start.3 = (f32[1633,32]{0,1:T(8,128)S(1)}, f32[1633,32]{0,1:T(8,128)}, u32[]{:S(2)}) copy-start(f32[1633,32]{0,1:T(8,128)} %reshape.680) | copy-start | bytes 627076
  46.9 2.7 %copy-start.8 = (bf16[32,64]{1,0:T(8,128)(2,1)S(1)}, bf16[32,64]{1,0:T(8,128)(2,1)}, u32[]{:S(2)}) copy-start(bf16[32,64]{1,0:T(8,128)(2,1)} %param.17) | copy-start | bytes 12292
  46.9 2.7 %copy-start.23 = (f32[32]{0:T(128)S(1)}, f32[32]{0:T(128)}, u32[]{:S(2)}) copy-start(f32[32]{0:T(128)} %get-tuple-element.107) | copy-start | bytes 388
  46.9 2.7 %copy-start.24 = (f32[32]{0:T(128)S(1)}, f32[32]{0:T(128)}, u32[]{:S(2)}) copy-start(f32[32]{0:T(128)} %get-tuple-element.108) | copy-start | bytes 388
  47.0 2.7 %copy-start.25 = (f32[32]{0:T(128)S(1)}, f32[32]{0:T(128)}, u32[]{:S(2)}) copy-start(f32[32]{0:T(128)} %get-tuple-element.109) | copy-start | bytes 388
  47.0 2.7 %copy-start.26 = (f32[32]{0:T(128)S(1)}, f32[32]{0:T(128)}, u32[]{:S(2)}) copy-start(f32[32]{0:T(128)} %get-tuple-element.110) | copy-start | bytes 388
  47.0 2.7 %copy-start.27 = (f32[32]{0:T(128)S(1)}, f32[32]{0:T(128)}, u32[]{:S(2)}) copy-start(f32[32]{0:T(128)} %get-tuple-element.111) | copy-start | bytes 388
  47.0 2.7 %copy-start.28 = (f32[32]{0:T(128)S(1)}, f32[32]{0:T(128)}, u32[]{:S(2)}) copy-start(f32[32]{0:T(128)} %get-tuple-element.112) | copy-start | bytes 388
  47.0 2.7 %copy-start.29 = (f32[32]{0:T(128)S(1)}, f32[32]{0:T(128)}, u32[]{:S(2)}) copy-start(f32[32]{0:T(128)} %get-tuple-element.113) | copy-start | bytes 388
  47.0 2.7 %copy-start.30 = (f32[32]{0:T(128)S(1)}, f32[32]{0:T(128)}, u32[]{:S(2)}) copy-start(f32[32]{0:T(128)} %get-tuple-element.114) | copy-start | bytes 388
  47.0 2.7 %copy-start.31 = (f32[32]{0:T(128)S(1)}, f32[32]{0:T(128)}, u32[]{:S(2)}) copy-start(f32[32]{0:T(128)} %get-tuple-element.115) | copy-start | bytes 388
  47.3 2.4 %copy-start.4 = (f32[1633,32]{0,1:T(8,128)S(1)}, f32[1633,32]{0,1:T(8,128)}, u32[]{:S(2)}) copy-start(f32[1633,32]{0,1:T(8,128)} %reshape.678) | copy-start | bytes 627076
  52.3 0.8 copy-start.7
  52.3 0.8 copy-start.14
  52.3 0.8 copy-start.15
  52.3 0.8 copy-start.16
  52.3 0.8 copy-start.17
  52.4 0.8 copy-start.18
  52.4 0.8 copy-start.19
  52.4 0.8 copy-start.20
  52.4 0.8 copy-start.21
  52.4 0.8 copy-start.22
  54.8 0.8 copy-start.6
  54.9 0.8 copy-start.9
  54.9 0.8 copy-start.10
  54.9 0.8 copy-start.11
  54.9 0.8 copy-start.12
  54.9 0.8 copy-start.13
  55.2 5.1 %copy-start.5 = (f32[4,9,512]{2,0,1:T(4,128)S(1)}, f32[4,9,512]{2,0,1:T(4,128)}, u32[]{:S(2)}) copy-start(f32[4,9,512]{2,0,1:T(4,128)} %param.24) | copy-start | bytes 221188
  56.7 4.4 %collective-permute-start.4 = (bf16[1,8,512]{2,1,0:T(8,128)(2,1)S(1)}, bf16[1,8,512]{2,1,0:T(8,128)(2,1)S(1)}, u32[]{:S(2)}, u32[]{:S(2)}) collective-permute-start(bf16[1,8,512]{2,1,0:T(8,128)(2,1)S(1)} %slice_bitcast_fusion), channel_id=1, source_target_pairs={{0,16},{16,32},{32,48},{48,64},{64,80},{80,96},{96,112},{112,128},... | collective-permute-start | bytes 24584 | tf_op jit(solution)/shard_map/ppermute | solution.py:12
  61.1 7.8 %collective-permute-start.5 = (bf16[3,7,512]{2,1,0:T(8,128)(2,1)S(1)}, bf16[3,7,512]{2,1,0:T(8,128)(2,1)S(1)}, u32[]{:S(2)}, u32[]{:S(2)}) collective-permute-start(bf16[3,7,512]{2,1,0:T(8,128)(2,1)S(1)} %pad_maximum_fusion.1), channel_id=1, source_target_pairs={{0,1},{1,2},{2,3},{3,4},{4,5},{5,6},{6,7},{7,8},{8,9},{9,10},{10,1... | collective-permute-start | bytes 64520 | tf_op jit(solution)/shard_map/ppermute | solution.py:12

commit v3 on v2

--- a/solution.py
+++ b/solution.py
@@ -125,12 +125,29 @@
     leftside = shifted(extended[:, -halo:], "gy", 1)
     extended = jnp.concatenate([leftside, extended], axis=1)
     hidden = strided_cells(extended, dwc[0], pwc[0])
-    hidden = lax.all_gather(hidden, "gx", axis=0, tiled=True)
+    hidden = doubling_gather(hidden, "gx", 0)
     for level in range(1, LC - 1):
         hidden = strided_cells(pad_top(hidden), dwc[level], pwc[level])
-    hidden = lax.all_gather(hidden, "gy", axis=1, tiled=True)
+    hidden = doubling_gather(hidden, "gy", 1)
     hidden = strided_cells(pad_left(pad_top(hidden)), dwc[LC - 1], pwc[LC - 1])
     return (fine, hidden.reshape(hidden.shape[0], -1))
+
+
+def doubling_gather(block, axis, dim):
+    count = lax.axis_size(axis)
+    index = lax.axis_index(axis)
+    span = 1
+    while span < count:
+        pairs = [(source, source ^ span) for source in range(count)]
+        other = lax.ppermute(block, axis, pairs)
+        later = (index // span) % 2 == 1
+        block = jnp.where(
+            later,
+            jnp.concatenate([other, block], axis=dim),
+            jnp.concatenate([block, other], axis=dim),
+        )
+        span *= 2
+    return block
 
 
 def pad_top(cells):

time: 142 us -> 162 us (1.14)
  blocking collectives: 61.8 us -> 0 us
  starting transfers between devices: 17.7 us -> 65.3 us
  waiting for transfers between devices: 5.66 us -> 39.4 us
    all_gather x2 -> x0, blocking collectives: 61.8 us -> none  [the longest x1 40.3 us: local(): hidden = lax.all_gather(hidden, 'gx', axis=0, tiled=True)]
    ppermute x0 -> x9, starting transfers between devices: none -> 47.8 us  [doubling_gather(): other = lax.ppermute(block, axis, pairs)]
    ppermute x0 -> x9, waiting for transfers between devices: none -> 32.6 us  [doubling_gather(): other = lax.ppermute(block, axis, pairs)]
  transfers between devices with their start and end apart: 6 -> 15, of which waited for: 3 -> 12; matrix products, arithmetic and copies ran while one was open for 7% -> 6% of each run, Pallas kernels for 0% -> 0%
where the time goes in v3:
time: 162 us; the launch traced here: 161 us
  starting transfers between devices  65.3 us (40%)
  local copies, waits for them, and re-layouts  40.9 us (25%)
  waiting for transfers between devices  39.4 us (24%)
  matrix products  7.61 us (5%)
  other arithmetic  4.67 us (3%)
  between operations  2.7 us (2%)
    ppermute x9, starting transfers between devices, doubling_gather(): other = lax.ppermute(block, axis, pairs)  47.8 us
    ppermute x9, waiting for transfers between devices, doubling_gather(): other = lax.ppermute(block, axis, pairs)  32.6 us
    ppermute x6, starting transfers between devices, shifted(): lax.ppermute(value, axis, [(source, source + steps) for source in range(l...  17.5 us
    ppermute x6, waiting for transfers between devices, shifted(): lax.ppermute(value, axis, [(source, source + steps) for source in range(l...  6.78 us
    convert_element_type x36, local copies, waits for them, and re-layouts, strided_flat(): total = total + piece.astype(jnp.float32) * tiled[3 * first + second]  6.15 us
    slice x4, local copies, waits for them, and re-layouts, strided_flat(): total = total + piece.astype(jnp.float32) * tiled[3 * first + second]  5.78 us
    dot_general x4, matrix products, strided_cells(): mixed = jnp.dot(flat, weight, preferred_element_type=jnp.float32)  5.07 us
    unnamed x75, local copies, waits for them, and re-layouts  3.75 us
  transfers between devices with their start and end apart: 15, of which 12 were waited for; matrix products, arithmetic and copies ran while one was open for 6% of the time, Pallas kernels for 0%

profile of v3, /device:TPU:6, one launch (start us, length us, event | category | flops | bytes accessed | tf_op | source)
XLA Modules:
  0.0 160.5 jit_solution(115916308534896943)
XLA Ops:
  0.7 1.0 slice.912
  1.7 1.8 %collective-permute-start = (bf16[17,4096]{1,0:T(8,128)(2,1)S(1)}, bf16[17,4096]{1,0:T(8,128)(2,1)S(1)}, u32[]{:S(2)}, u32[]{:S(2)}) collective-permute-start(bf16[17,4096]{1,0:T(8,128)(2,1)S(1)} %slice.912), channel_id=1, source_target_pairs={{0,16},{16,32},{32,48},{48,64},{64,80},{80,96},{96,112},{112,128},... | collective-permute-start | bytes 417800 | tf_op jit(solution)/shard_map/ppermute | solution.py:12
  3.5 0.9 slice.913
  4.3 1.3 collective-permute-start.1
  5.6 1.0 slice_bitcast_fusion.54
  6.6 1.6 slice_bitcast_fusion.45
  8.2 1.6 slice_bitcast_fusion.36
  9.8 1.0 fusion.189
  10.8 1.6 slice_bitcast_fusion.27
  12.4 1.1 pad_maximum_fusion
  13.6 3.5 %collective-permute-start.2 = (bf16[51,544]{1,0:T(8,128)(2,1)S(1)}, bf16[51,544]{1,0:T(8,128)(2,1)S(1)}, u32[]{:S(2)}, u32[]{:S(2)}) collective-permute-start(bf16[51,544]{1,0:T(8,128)(2,1)S(1)} %slice.1167), channel_id=1, source_target_pairs={{0,1},{1,2},{2,3},{3,4},{4,5},{5,6},{6,7},{7,8},{8,9},{9,10},{10,1... | collective-permute-start | bytes 166472 | tf_op jit(solution)/shard_map/ppermute | solution.py:12
  18.5 4.5 %collective-permute-start.3 = (bf16[51,64]{1,0:T(8,128)(2,1)S(1)}, bf16[51,64]{1,0:T(8,128)(2,1)S(1)}, u32[]{:S(2)}, u32[]{:S(2)}) collective-permute-start(bf16[51,64]{1,0:T(8,128)(2,1)S(1)} %slice.1171), channel_id=1, source_target_pairs={{1,0},{2,1},{3,2},{4,3},{5,4},{6,5},{7,6},{8,7},{9,8},{10,9},{11,1... | collective-permute-start | bytes 19592 | tf_op jit(solution)/shard_map/ppermute | solution.py:12
  23.3 1.1 collective-permute-done.3
  25.2 1.3 fusion.5
  26.5 1.6 reshape.640
  28.1 1.4 fusion.13
  29.5 2.5 %copy.55 = f32[6721,32]{1,0:T(8,128)} copy(f32[6721,32]{0,1:T(8,128)S(1)} %fusion.13) | data formatting | bytes 1720576 | tf_op jit(solution)/shard_map/mul | solution.py:29
  32.0 2.5 %reshape.641 = f32[47,4576]{1,0:T(8,128)S(1)} reshape(f32[6721,32]{1,0:T(8,128)} %copy.55) | data formatting | bytes 1720576 | tf_op jit(solution)/shard_map/reshape | solution.py:36
  41.0 0.9 copy.95
  41.9 1.0 copy.69
  46.1 0.8 reshape.678
  47.6 0.9 copy.97
  48.5 1.0 copy.73
  56.7 3.6 %collective-permute-start.4 = (bf16[1,8,512]{2,1,0:T(8,128)(2,1)S(1)}, bf16[1,8,512]{2,1,0:T(8,128)(2,1)S(1)}, u32[]{:S(2)}, u32[]{:S(2)}) collective-permute-start(bf16[1,8,512]{2,1,0:T(8,128)(2,1)S(1)} %slice_bitcast_fusion), channel_id=1, source_target_pairs={{0,16},{16,32},{32,48},{48,64},{64,80},{80,96},{96,112},{112,128},... | collective-permute-start | bytes 24584 | tf_op jit(solution)/shard_map/ppermute | solution.py:12
  61.2 2.9 %collective-permute-start.5 = (bf16[3,7,512]{2,1,0:T(8,128)(2,1)S(1)}, bf16[3,7,512]{2,1,0:T(8,128)(2,1)S(1)}, u32[]{:S(2)}, u32[]{:S(2)}) collective-permute-start(bf16[3,7,512]{2,1,0:T(8,128)(2,1)S(1)} %pad_maximum_fusion.1), channel_id=1, source_target_pairs={{0,1},{1,2},{2,3},{3,4},{4,5},{5,6},{6,7},{7,8},{8,9},{9,10},{10,1... | collective-permute-start | bytes 64520 | tf_op jit(solution)/shard_map/ppermute | solution.py:12
  64.1 4.9 %collective-permute-done.5 = bf16[3,7,512]{2,1,0:T(8,128)(2,1)S(1)} collective-permute-done((bf16[3,7,512]{2,1,0:T(8,128)(2,1)S(1)}, bf16[3,7,512]{2,1,0:T(8,128)(2,1)S(1)}, u32[]{:S(2)}, u32[]{:S(2)}) %collective-permute-start.5) | collective-permute-done | bytes 21536 | tf_op jit(solution)/shard_map/ppermute | solution.py:12
  69.2 1.3 fusion.114
  70.5 4.4 %collective-permute-start.6 = (bf16[1,7,512]{2,0,1:T(2,128)(2,1)S(1)}, bf16[1,7,512]{2,0,1:T(2,128)(2,1)S(1)}, u32[]{:S(2)}, u32[]{:S(2)}) collective-permute-start(bf16[1,7,512]{2,0,1:T(2,128)(2,1)S(1)} %copy.75), channel_id=1, source_target_pairs={{0,16},{16,0},{32,48},{48,32},{64,80},{80,64},{96,112},{112,96},{1... | collective-permute-start | bytes 21512 | tf_op jit(solution)/shard_map/ppermute | solution.py:142
  75.5 5.3 %collective-permute-start.7 = (bf16[2,7,512]{2,0,1:T(2,128)(2,1)S(1)}, bf16[2,7,512]{2,0,1:T(2,128)(2,1)S(1)}, u32[]{:S(2)}, u32[]{:S(2)}) collective-permute-start(bf16[2,7,512]{2,0,1:T(2,128)(2,1)S(1)} %broadcast_select_fusion.1), channel_id=1, source_target_pairs={{0,32},{16,48},{32,0},{48,16},{64,96},{80,112},{96,64},{112,80},{1... | collective-permute-start | bytes 43016 | tf_op jit(solution)/shard_map/ppermute | solution.py:142
  80.8 1.6 %collective-permute-done.7 = bf16[2,7,512]{2,0,1:T(2,128)(2,1)S(1)} collective-permute-done((bf16[2,7,512]{2,0,1:T(2,128)(2,1)S(1)}, bf16[2,7,512]{2,0,1:T(2,128)(2,1)S(1)}, u32[]{:S(2)}, u32[]{:S(2)}) %collective-permute-start.7) | collective-permute-done | bytes 14368 | tf_op jit(solution)/shard_map/ppermute | solution.py:142
  82.6 6.1 %collective-permute-start.8 = (bf16[4,7,512]{2,0,1:T(4,128)(2,1)S(1)}, bf16[4,7,512]{2,0,1:T(4,128)(2,1)S(1)}, u32[]{:S(2)}, u32[]{:S(2)}) collective-permute-start(bf16[4,7,512]{2,0,1:T(4,128)(2,1)S(1)} %maximum_select_fusion.6), channel_id=1, source_target_pairs={{0,64},{16,80},{32,96},{48,112},{64,0},{80,16},{96,32},{112,48},{1... | collective-permute-start | bytes 86024 | tf_op jit(solution)/shard_map/ppermute | solution.py:142
  88.7 2.1 %collective-permute-done.8 = bf16[4,7,512]{2,0,1:T(4,128)(2,1)S(1)} collective-permute-done((bf16[4,7,512]{2,0,1:T(4,128)(2,1)S(1)}, bf16[4,7,512]{2,0,1:T(4,128)(2,1)S(1)}, u32[]{:S(2)}, u32[]{:S(2)}) %collective-permute-start.8) | collective-permute-done | bytes 28704 | tf_op jit(solution)/shard_map/ppermute | solution.py:142
  90.9 10.0 %collective-permute-start.9 = (bf16[8,7,512]{2,0,1:T(8,128)(2,1)S(1)}, bf16[8,7,512]{2,0,1:T(8,128)(2,1)S(1)}, u32[]{:S(2)}, u32[]{:S(2)}) collective-permute-start(bf16[8,7,512]{2,0,1:T(8,128)(2,1)S(1)} %maximum_select_fusion.4), channel_id=1, source_target_pairs={{0,128},{16,144},{32,160},{48,176},{64,192},{80,208},{96,224},{112... | collective-permute-start | bytes 172040 | tf_op jit(solution)/shard_map/ppermute | solution.py:142
  101.0 3.9 %collective-permute-done.9 = bf16[8,7,512]{2,0,1:T(8,128)(2,1)S(1)} collective-permute-done((bf16[8,7,512]{2,0,1:T(8,128)(2,1)S(1)}, bf16[8,7,512]{2,0,1:T(8,128)(2,1)S(1)}, u32[]{:S(2)}, u32[]{:S(2)}) %collective-permute-start.9) | collective-permute-done | bytes 57376 | tf_op jit(solution)/shard_map/ppermute | solution.py:142
  104.9 13.4 %collective-permute-start.10 = (bf16[16,7,512]{2,0,1:T(8,128)(2,1)S(1)}, bf16[16,7,512]{2,0,1:T(8,128)(2,1)S(1)}, u32[]{:S(2)}, u32[]{:S(2)}) collective-permute-start(bf16[16,7,512]{2,0,1:T(8,128)(2,1)S(1)} %maximum_select_fusion.2), channel_id=1, source_target_pairs={{0,256},{16,272},{32,288},{48,304},{64,320},{80,336},{96,352},{112... | collective-permute-start | bytes 344072 | tf_op jit(solution)/shard_map/ppermute | solution.py:142
  118.4 7.6 %collective-permute-done.10 = bf16[16,7,512]{2,0,1:T(8,128)(2,1)S(1)} collective-permute-done((bf16[16,7,512]{2,0,1:T(8,128)(2,1)S(1)}, bf16[16,7,512]{2,0,1:T(8,128)(2,1)S(1)}, u32[]{:S(2)}, u32[]{:S(2)}) %collective-permute-start.10) | collective-permute-done | bytes 114720 | tf_op jit(solution)/shard_map/ppermute | solution.py:142
  127.8 1.3 fusion.51
  129.3 1.3 fusion.129
  130.6 1.9 %collective-permute-start.11 = (bf16[8,1,512]{2,1,0:T(2,128)(2,1)S(1)}, bf16[8,1,512]{2,1,0:T(2,128)(2,1)S(1)}, u32[]{:S(2)}, u32[]{:S(2)}) collective-permute-start(bf16[8,1,512]{2,1,0:T(2,128)(2,1)S(1)} %copy.86), channel_id=1, source_target_pairs={{0,1},{1,0},{2,3},{3,2},{4,5},{5,4},{6,7},{7,6},{8,9},{9,8},{10,11... | collective-permute-start | bytes 24584 | tf_op jit(solution)/shard_map/ppermute | solution.py:142
  132.5 3.7 %collective-permute-done.11 = bf16[8,1,512]{2,1,0:T(2,128)(2,1)S(1)} collective-permute-done((bf16[8,1,512]{2,1,0:T(2,128)(2,1)S(1)}, bf16[8,1,512]{2,1,0:T(2,128)(2,1)S(1)}, u32[]{:S(2)}, u32[]{:S(2)}) %collective-permute-start.11) | collective-permute-done | bytes 8224 | tf_op jit(solution)/shard_map/ppermute | solution.py:142
  136.3 1.9 %collective-permute-start.12 = (bf16[8,2,512]{2,1,0:T(2,128)(2,1)S(1)}, bf16[8,2,512]{2,1,0:T(2,128)(2,1)S(1)}, u32[]{:S(2)}, u32[]{:S(2)}) collective-permute-start(bf16[8,2,512]{2,1,0:T(2,128)(2,1)S(1)} %broadcast_select_fusion), channel_id=1, source_target_pairs={{0,2},{1,3},{2,0},{3,1},{4,6},{5,7},{6,4},{7,5},{8,10},{9,11},{10,... | collective-permute-start | bytes 49160 | tf_op jit(solution)/shard_map/ppermute | solution.py:142
  138.3 5.2 %collective-permute-done.12 = bf16[8,2,512]{2,1,0:T(2,128)(2,1)S(1)} collective-permute-done((bf16[8,2,512]{2,1,0:T(2,128)(2,1)S(1)}, bf16[8,2,512]{2,1,0:T(2,128)(2,1)S(1)}, u32[]{:S(2)}, u32[]{:S(2)}) %collective-permute-start.12) | collective-permute-done | bytes 16416 | tf_op jit(solution)/shard_map/ppermute | solution.py:142
  143.5 2.7 %collective-permute-start.13 = (bf16[8,4,512]{2,1,0:T(4,128)(2,1)S(1)}, bf16[8,4,512]{2,1,0:T(4,128)(2,1)S(1)}, u32[]{:S(2)}, u32[]{:S(2)}) collective-permute-start(bf16[8,4,512]{2,1,0:T(4,128)(2,1)S(1)} %maximum_select_fusion.5), channel_id=1, source_target_pairs={{0,4},{1,5},{2,6},{3,7},{4,0},{5,1},{6,2},{7,3},{8,12},{9,13},{10,... | collective-permute-start | bytes 98312 | tf_op jit(solution)/shard_map/ppermute | solution.py:142
  146.3 3.0 %collective-permute-done.13 = bf16[8,4,512]{2,1,0:T(4,128)(2,1)S(1)} collective-permute-done((bf16[8,4,512]{2,1,0:T(4,128)(2,1)S(1)}, bf16[8,4,512]{2,1,0:T(4,128)(2,1)S(1)}, u32[]{:S(2)}, u32[]{:S(2)}) %collective-permute-start.13) | collective-permute-done | bytes 32800 | tf_op jit(solution)/shard_map/ppermute | solution.py:142
  149.4 1.9 %collective-permute-start.14 = (bf16[8,8,512]{2,1,0:T(8,128)(2,1)S(1)}, bf16[8,8,512]{2,1,0:T(8,128)(2,1)S(1)}, u32[]{:S(2)}, u32[]{:S(2)}) collective-permute-start(bf16[8,8,512]{2,1,0:T(8,128)(2,1)S(1)} %maximum_select_fusion.3), channel_id=1, source_target_pairs={{0,8},{1,9},{2,10},{3,11},{4,12},{5,13},{6,14},{7,15},{8,0},{9,1},... | collective-permute-start | bytes 196616 | tf_op jit(solution)/shard_map/ppermute | solution.py:142
  151.3 0.9 slice.1178
  152.2 4.8 %collective-permute-done.14 = bf16[8,8,512]{2,1,0:T(8,128)(2,1)S(1)} collective-permute-done((bf16[8,8,512]{2,1,0:T(8,128)(2,1)S(1)}, bf16[8,8,512]{2,1,0:T(8,128)(2,1)S(1)}, u32[]{:S(2)}, u32[]{:S(2)}) %collective-permute-start.14) | collective-permute-done | bytes 65568 | tf_op jit(solution)/shard_map/ppermute | solution.py:142
  158.6 1.3 fusion.71
  (269 shorter events, 25.0 us)
Async XLA Ops:
  0.6 55.9 %copy-start = (bf16[256,512]{1,0:T(8,128)(2,1)S(1)}, bf16[256,512]{1,0:T(8,128)(2,1)}, u32[]{:S(2)}) copy-start(bf16[256,512]{1,0:T(8,128)(2,1)} %param.23) | copy-start | bytes 786436
  0.6 22.3 %copy-start.1 = (bf16[32,4096]{1,0:T(8,128)(2,1)S(1)}, bf16[32,4096]{1,0:T(8,128)(2,1)}, u32[]{:S(2)}) copy-start(bf16[32,4096]{1,0:T(8,128)(2,1)} %param.13) | copy-start | bytes 786436
  1.7 10.7 %collective-permute-start = (bf16[17,4096]{1,0:T(8,128)(2,1)S(1)}, bf16[17,4096]{1,0:T(8,128)(2,1)S(1)}, u32[]{:S(2)}, u32[]{:S(2)}) collective-permute-start(bf16[17,4096]{1,0:T(8,128)(2,1)S(1)} %slice.912), channel_id=1, source_target_pairs={{0,16},{16,32},{32,48},{48,64},{64,80},{80,96},{96,112},{112,128},... | collective-permute-start | bytes 417800 | tf_op jit(solution)/shard_map/ppermute | solution.py:12
  4.3 8.1 %collective-permute-start.1 = (bf16[2,4096]{1,0:T(2,128)(2,1)S(1)}, bf16[2,4096]{1,0:T(2,128)(2,1)S(1)}, u32[]{:S(2)}, u32[]{:S(2)}) collective-permute-start(bf16[2,4096]{1,0:T(2,128)(2,1)S(1)} %slice.913), channel_id=1, source_target_pairs={{16,0},{32,16},{48,32},{64,48},{80,64},{96,80},{112,96},{128,112},... | collective-permute-start | bytes 49160 | tf_op jit(solution)/shard_map/ppermute | solution.py:12
  13.6 9.4 %collective-permute-start.2 = (bf16[51,544]{1,0:T(8,128)(2,1)S(1)}, bf16[51,544]{1,0:T(8,128)(2,1)S(1)}, u32[]{:S(2)}, u32[]{:S(2)}) collective-permute-start(bf16[51,544]{1,0:T(8,128)(2,1)S(1)} %slice.1167), channel_id=1, source_target_pairs={{0,1},{1,2},{2,3},{3,4},{4,5},{5,6},{6,7},{7,8},{8,9},{9,10},{10,1... | collective-permute-start | bytes 166472 | tf_op jit(solution)/shard_map/ppermute | solution.py:12
  18.5 5.9 %collective-permute-start.3 = (bf16[51,64]{1,0:T(8,128)(2,1)S(1)}, bf16[51,64]{1,0:T(8,128)(2,1)S(1)}, u32[]{:S(2)}, u32[]{:S(2)}) collective-permute-start(bf16[51,64]{1,0:T(8,128)(2,1)S(1)} %slice.1171), channel_id=1, source_target_pairs={{1,0},{2,1},{3,2},{4,3},{5,4},{6,5},{7,6},{8,7},{9,8},{10,9},{11,1... | collective-permute-start | bytes 19592 | tf_op jit(solution)/shard_map/ppermute | solution.py:12
  32.0 2.5 %copy-start.32 = (pred[47]{0:T(512)(128)(4,1)S(1)}, pred[47]{0:T(512)(128)(4,1)}, u32[]{:S(2)}) copy-start(pred[47]{0:T(512)(128)(4,1)} %compare_or_fusion) | copy-start | bytes 145
  46.9 2.7 %copy-start.2 = (f32[1633,32]{0,1:T(8,128)S(1)}, f32[1633,32]{0,1:T(8,128)}, u32[]{:S(2)}) copy-start(f32[1633,32]{0,1:T(8,128)} %reshape.677) | copy-start | bytes 627076
  47.0 2.7 %copy-start.3 = (f32[1633,32]{0,1:T(8,128)S(1)}, f32[1633,32]{0,1:T(8,128)}, u32[]{:S(2)}) copy-start(f32[1633,32]{0,1:T(8,128)} %reshape.680) | copy-start | bytes 627076
  47.0 2.7 %copy-start.8 = (bf16[32,64]{1,0:T(8,128)(2,1)S(1)}, bf16[32,64]{1,0:T(8,128)(2,1)}, u32[]{:S(2)}) copy-start(bf16[32,64]{1,0:T(8,128)(2,1)} %param.17) | copy-start | bytes 12292
  47.0 2.7 %copy-start.23 = (f32[32]{0:T(128)S(1)}, f32[32]{0:T(128)}, u32[]{:S(2)}) copy-start(f32[32]{0:T(128)} %get-tuple-element.107) | copy-start | bytes 388
  47.0 2.7 %copy-start.24 = (f32[32]{0:T(128)S(1)}, f32[32]{0:T(128)}, u32[]{:S(2)}) copy-start(f32[32]{0:T(128)} %get-tuple-element.108) | copy-start | bytes 388
  47.0 2.7 %copy-start.25 = (f32[32]{0:T(128)S(1)}, f32[32]{0:T(128)}, u32[]{:S(2)}) copy-start(f32[32]{0:T(128)} %get-tuple-element.109) | copy-start | bytes 388
  47.0 2.7 %copy-start.26 = (f32[32]{0:T(128)S(1)}, f32[32]{0:T(128)}, u32[]{:S(2)}) copy-start(f32[32]{0:T(128)} %get-tuple-element.110) | copy-start | bytes 388
  47.0 2.7 %copy-start.27 = (f32[32]{0:T(128)S(1)}, f32[32]{0:T(128)}, u32[]{:S(2)}) copy-start(f32[32]{0:T(128)} %get-tuple-element.111) | copy-start | bytes 388
  47.0 2.7 %copy-start.28 = (f32[32]{0:T(128)S(1)}, f32[32]{0:T(128)}, u32[]{:S(2)}) copy-start(f32[32]{0:T(128)} %get-tuple-element.112) | copy-start | bytes 388
  47.0 2.7 %copy-start.29 = (f32[32]{0:T(128)S(1)}, f32[32]{0:T(128)}, u32[]{:S(2)}) copy-start(f32[32]{0:T(128)} %get-tuple-element.113) | copy-start | bytes 388
  47.0 2.7 %copy-start.30 = (f32[32]{0:T(128)S(1)}, f32[32]{0:T(128)}, u32[]{:S(2)}) copy-start(f32[32]{0:T(128)} %get-tuple-element.114) | copy-start | bytes 388
  47.0 2.7 %copy-start.31 = (f32[32]{0:T(128)S(1)}, f32[32]{0:T(128)}, u32[]{:S(2)}) copy-start(f32[32]{0:T(128)} %get-tuple-element.115) | copy-start | bytes 388
  47.4 2.4 %copy-start.4 = (f32[1633,32]{0,1:T(8,128)S(1)}, f32[1633,32]{0,1:T(8,128)}, u32[]{:S(2)}) copy-start(f32[1633,32]{0,1:T(8,128)} %reshape.678) | copy-start | bytes 627076
  52.3 0.8 copy-start.7
  52.4 0.8 copy-start.14
  52.4 0.8 copy-start.15
  52.4 0.8 copy-start.16
  52.4 0.8 copy-start.17
  52.4 0.8 copy-start.18
  52.4 0.8 copy-start.19
  52.4 0.8 copy-start.20
  52.4 0.8 copy-start.21
  52.4 0.8 copy-start.22
  54.9 0.8 copy-start.6
  54.9 0.8 copy-start.9
  54.9 0.8 copy-start.10
  54.9 0.8 copy-start.11
  54.9 0.8 copy-start.12
  54.9 0.8 copy-start.13
  55.2 8.9 %copy-start.5 = (f32[4,9,512]{2,0,1:T(4,128)S(1)}, f32[4,9,512]{2,0,1:T(4,128)}, u32[]{:S(2)}) copy-start(f32[4,9,512]{2,0,1:T(4,128)} %param.24) | copy-start | bytes 221188
  56.7 4.4 %collective-permute-start.4 = (bf16[1,8,512]{2,1,0:T(8,128)(2,1)S(1)}, bf16[1,8,512]{2,1,0:T(8,128)(2,1)S(1)}, u32[]{:S(2)}, u32[]{:S(2)}) collective-permute-start(bf16[1,8,512]{2,1,0:T(8,128)(2,1)S(1)} %slice_bitcast_fusion), channel_id=1, source_target_pairs={{0,16},{16,32},{32,48},{48,64},{64,80},{80,96},{96,112},{112,128},... | collective-permute-start | bytes 24584 | tf_op jit(solution)/shard_map/ppermute | solution.py:12
  61.2 7.8 %collective-permute-start.5 = (bf16[3,7,512]{2,1,0:T(8,128)(2,1)S(1)}, bf16[3,7,512]{2,1,0:T(8,128)(2,1)S(1)}, u32[]{:S(2)}, u32[]{:S(2)}) collective-permute-start(bf16[3,7,512]{2,1,0:T(8,128)(2,1)S(1)} %pad_maximum_fusion.1), channel_id=1, source_target_pairs={{0,1},{1,2},{2,3},{3,4},{4,5},{5,6},{6,7},{7,8},{8,9},{9,10},{10,1... | collective-permute-start | bytes 64520 | tf_op jit(solution)/shard_map/ppermute | solution.py:12
  70.5 5.0 %collective-permute-start.6 = (bf16[1,7,512]{2,0,1:T(2,128)(2,1)S(1)}, bf16[1,7,512]{2,0,1:T(2,128)(2,1)S(1)}, u32[]{:S(2)}, u32[]{:S(2)}) collective-permute-start(bf16[1,7,512]{2,0,1:T(2,128)(2,1)S(1)} %copy.75), channel_id=1, source_target_pairs={{0,16},{16,0},{32,48},{48,32},{64,80},{80,64},{96,112},{112,96},{1... | collective-permute-start | bytes 21512 | tf_op jit(solution)/shard_map/ppermute | solution.py:142
  75.5 7.0 %collective-permute-start.7 = (bf16[2,7,512]{2,0,1:T(2,128)(2,1)S(1)}, bf16[2,7,512]{2,0,1:T(2,128)(2,1)S(1)}, u32[]{:S(2)}, u32[]{:S(2)}) collective-permute-start(bf16[2,7,512]{2,0,1:T(2,128)(2,1)S(1)} %broadcast_select_fusion.1), channel_id=1, source_target_pairs={{0,32},{16,48},{32,0},{48,16},{64,96},{80,112},{96,64},{112,80},{1... | collective-permute-start | bytes 43016 | tf_op jit(solution)/shard_map/ppermute | solution.py:142
  82.6 8.2 %collective-permute-start.8 = (bf16[4,7,512]{2,0,1:T(4,128)(2,1)S(1)}, bf16[4,7,512]{2,0,1:T(4,128)(2,1)S(1)}, u32[]{:S(2)}, u32[]{:S(2)}) collective-permute-start(bf16[4,7,512]{2,0,1:T(4,128)(2,1)S(1)} %maximum_select_fusion.6), channel_id=1, source_target_pairs={{0,64},{16,80},{32,96},{48,112},{64,0},{80,16},{96,32},{112,48},{1... | collective-permute-start | bytes 86024 | tf_op jit(solution)/shard_map/ppermute | solution.py:142
  90.9 14.0 %collective-permute-start.9 = (bf16[8,7,512]{2,0,1:T(8,128)(2,1)S(1)}, bf16[8,7,512]{2,0,1:T(8,128)(2,1)S(1)}, u32[]{:S(2)}, u32[]{:S(2)}) collective-permute-start(bf16[8,7,512]{2,0,1:T(8,128)(2,1)S(1)} %maximum_select_fusion.4), channel_id=1, source_target_pairs={{0,128},{16,144},{32,160},{48,176},{64,192},{80,208},{96,224},{112... | collective-permute-start | bytes 172040 | tf_op jit(solution)/shard_map/ppermute | solution.py:142
  104.9 21.1 %collective-permute-start.10 = (bf16[16,7,512]{2,0,1:T(8,128)(2,1)S(1)}, bf16[16,7,512]{2,0,1:T(8,128)(2,1)S(1)}, u32[]{:S(2)}, u32[]{:S(2)}) collective-permute-start(bf16[16,7,512]{2,0,1:T(8,128)(2,1)S(1)} %maximum_select_fusion.2), channel_id=1, source_target_pairs={{0,256},{16,272},{32,288},{48,304},{64,320},{80,336},{96,352},{112... | collective-permute-start | bytes 344072 | tf_op jit(solution)/shard_map/ppermute | solution.py:142
  130.6 5.6 %collective-permute-start.11 = (bf16[8,1,512]{2,1,0:T(2,128)(2,1)S(1)}, bf16[8,1,512]{2,1,0:T(2,128)(2,1)S(1)}, u32[]{:S(2)}, u32[]{:S(2)}) collective-permute-start(bf16[8,1,512]{2,1,0:T(2,128)(2,1)S(1)} %copy.86), channel_id=1, source_target_pairs={{0,1},{1,0},{2,3},{3,2},{4,5},{5,4},{6,7},{7,6},{8,9},{9,8},{10,11... | collective-permute-start | bytes 24584 | tf_op jit(solution)/shard_map/ppermute | solution.py:142
  136.3 7.1 %collective-permute-start.12 = (bf16[8,2,512]{2,1,0:T(2,128)(2,1)S(1)}, bf16[8,2,512]{2,1,0:T(2,128)(2,1)S(1)}, u32[]{:S(2)}, u32[]{:S(2)}) collective-permute-start(bf16[8,2,512]{2,1,0:T(2,128)(2,1)S(1)} %broadcast_select_fusion), channel_id=1, source_target_pairs={{0,2},{1,3},{2,0},{3,1},{4,6},{5,7},{6,4},{7,5},{8,10},{9,11},{10,... | collective-permute-start | bytes 49160 | tf_op jit(solution)/shard_map/ppermute | solution.py:142
  143.5 5.8 %collective-permute-start.13 = (bf16[8,4,512]{2,1,0:T(4,128)(2,1)S(1)}, bf16[8,4,512]{2,1,0:T(4,128)(2,1)S(1)}, u32[]{:S(2)}, u32[]{:S(2)}) collective-permute-start(bf16[8,4,512]{2,1,0:T(4,128)(2,1)S(1)} %maximum_select_fusion.5), channel_id=1, source_target_pairs={{0,4},{1,5},{2,6},{3,7},{4,0},{5,1},{6,2},{7,3},{8,12},{9,13},{10,... | collective-permute-start | bytes 98312 | tf_op jit(solution)/shard_map/ppermute | solution.py:142
  149.4 7.7 %collective-permute-start.14 = (bf16[8,8,512]{2,1,0:T(8,128)(2,1)S(1)}, bf16[8,8,512]{2,1,0:T(8,128)(2,1)S(1)}, u32[]{:S(2)}, u32[]{:S(2)}) collective-permute-start(bf16[8,8,512]{2,1,0:T(8,128)(2,1)S(1)} %maximum_select_fusion.3), channel_id=1, source_target_pairs={{0,8},{1,9},{2,10},{3,11},{4,12},{5,13},{6,14},{7,15},{8,0},{9,1},... | collective-permute-start | bytes 196616 | tf_op jit(solution)/shard_map/ppermute | solution.py:142

commit v4 on v2

--- a/solution.py
+++ b/solution.py
@@ -4,17 +4,26 @@
 from jax.sharding import PartitionSpec as P
 
 LC = 4
+ROW_AXES = ("zh", "zl", "core")
+COL_AXES = ("x", "y")
 
 
 def shifted(value, axis, steps):
-    count = lax.axis_size(axis)
+    count = axis_count(axis)
     leading, last = (max(0, -steps), min(count, count - steps))
     return lax.ppermute(value, axis, [(source, source + steps) for source in range(leading, last)])
 
 
+def axis_count(axes):
+    count = 1
+    for axis in axes:
+        count *= lax.axis_size(axis)
+    return count
+
+
 def padded_2(block, sides, width):
     for axis, dim in sides:
-        count = lax.axis_size(axis)
+        count = axis_count(axis)
         forward = [(i, i + 1) for i in range(count - 1)]
         backward = [(target, source) for source, target in forward]
         low = lax.ppermute(
@@ -43,12 +52,12 @@
     half_rows = rows // 2
     half_cols = cols // 2
     if split_rows:
-        upper = shifted(field[-1:], "gx", 1)
+        upper = shifted(field[-1:], ROW_AXES, 1)
     else:
         upper = jnp.zeros((1, cols * chans), jnp.bfloat16)
     extended = jnp.concatenate([upper, field], axis=0)
     if split_cols:
-        leftside = shifted(extended[:, -chans:], "gy", 1)
+        leftside = shifted(extended[:, -chans:], COL_AXES, 1)
     else:
         leftside = jnp.zeros((rows + 1, chans), jnp.bfloat16)
     tiled = jnp.tile(taps, (1, half_cols))
@@ -88,11 +97,11 @@
     cols = field.shape[1] // chans
     depth = 4
     margin = 2**depth - 1
-    upper = shifted(field[-margin - 2 :], "gx", 1)
-    lower = shifted(field[:2], "gx", -1)
+    upper = shifted(field[-margin - 2 :], ROW_AXES, 1)
+    lower = shifted(field[:2], ROW_AXES, -1)
     stacked = jnp.concatenate([upper, field, lower], axis=0)
-    leftside = shifted(stacked[:, -(margin + 2) * chans :], "gy", 1)
-    rightside = shifted(stacked[:, : 2 * chans], "gy", -1)
+    leftside = shifted(stacked[:, -(margin + 2) * chans :], COL_AXES, 1)
+    rightside = shifted(stacked[:, : 2 * chans], COL_AXES, -1)
     flat_pad = jnp.concatenate([leftside, stacked, rightside], axis=1)
     ext_rows = rows + margin
     ext_cols = cols + margin
@@ -109,8 +118,8 @@
     hidden = (centre.astype(jnp.float32) + point_flat(total, pw0, ext_rows, ext_cols)).astype(
         jnp.bfloat16
     )
-    row_ok = (lax.axis_index("gx") > 0) | (lax.broadcasted_iota(jnp.int32, hidden.shape, 0) >= margin)
-    col_ok = (lax.axis_index("gy") > 0) | (
+    row_ok = (lax.axis_index(ROW_AXES) > 0) | (lax.broadcasted_iota(jnp.int32, hidden.shape, 0) >= margin)
+    col_ok = (lax.axis_index(COL_AXES) > 0) | (
         lax.broadcasted_iota(jnp.int32, hidden.shape, 1) >= margin * chans
     )
     hidden = jnp.where(row_ok & col_ok, hidden, jnp.zeros_like(hidden))
@@ -120,15 +129,17 @@
     coarse_chans = dwc.shape[2]
     halo = 2 ** (LC - 1) - 1
     grid4 = hidden.reshape(hidden.shape[0], -1, coarse_chans)
-    upper = shifted(grid4[-1:], "gx", 1)
+    upper = shifted(grid4[-1:], ROW_AXES, 1)
     extended = jnp.concatenate([upper, grid4], axis=0)
-    leftside = shifted(extended[:, -halo:], "gy", 1)
+    leftside = shifted(extended[:, -halo:], COL_AXES, 1)
     extended = jnp.concatenate([leftside, extended], axis=1)
     hidden = strided_cells(extended, dwc[0], pwc[0])
-    hidden = lax.all_gather(hidden, "gx", axis=0, tiled=True)
+    for axis in reversed(ROW_AXES):
+        hidden = lax.all_gather(hidden, axis, axis=0, tiled=True)
     for level in range(1, LC - 1):
         hidden = strided_cells(pad_top(hidden), dwc[level], pwc[level])
-    hidden = lax.all_gather(hidden, "gy", axis=1, tiled=True)
+    for axis in reversed(COL_AXES):
+        hidden = lax.all_gather(hidden, axis, axis=1, tiled=True)
     hidden = strided_cells(pad_left(pad_top(hidden)), dwc[LC - 1], pwc[LC - 1])
     return (fine, hidden.reshape(hidden.shape[0], -1))
 
@@ -155,7 +166,11 @@
 
 
 def solution(mesh):
-    placed = (P("gx", "gy"), P(), P(), P(), P(), P(), P(), P(), P(), P(), P(), P(), P())
+    rows, cols = mesh.devices.shape
+    split = mesh.devices.reshape(rows // 8, 4, 2, cols // 4, 4)
+    fine_mesh = jax.sharding.Mesh(split, ROW_AXES + COL_AXES)
+    grid = P(ROW_AXES, COL_AXES)
+    placed = (grid,) + (P(),) * 12
     return jax.shard_map(
-        local, mesh=mesh, in_specs=placed, out_specs=(P("gx", "gy"), P()), check_vma=False
+        local, mesh=fine_mesh, in_specs=placed, out_specs=(grid, P()), check_vma=False
     )

time: 142 us -> 152 us (1.070)
  blocking collectives: 61.8 us -> 72.4 us
    all_gather x2 -> x5, blocking collectives: 61.8 us -> 72.4 us  [the longest x3 48.5 us: local(): hidden = lax.all_gather(hidden, axis, axis=0, tiled=True)]
where the time goes in v4:
time: 152 us; the launch traced here: 151 us
  blocking collectives  72.4 us (48%)
  local copies, waits for them, and re-layouts  40.9 us (27%)
  starting transfers between devices  17.7 us (12%)
  matrix products  7.61 us (5%)
  waiting for transfers between devices  5.66 us (4%)
  other arithmetic  4.19 us (3%)
  between operations  2.35 us (2%)
    all_gather x3, blocking collectives, local(): hidden = lax.all_gather(hidden, axis, axis=0, tiled=True)  48.5 us
    all_gather x2, blocking collectives, local(): hidden = lax.all_gather(hidden, axis, axis=1, tiled=True)  23.9 us
    ppermute x6, starting transfers between devices, shifted(): lax.ppermute(value, axis, [(source, source + steps) for source in range(l...  17.7 us
    convert_element_type x36, local copies, waits for them, and re-layouts, strided_flat(): total = total + piece.astype(jnp.float32) * tiled[3 * first + second]  6.18 us
    slice x4, local copies, waits for them, and re-layouts, strided_flat(): total = total + piece.astype(jnp.float32) * tiled[3 * first + second]  5.76 us
    ppermute x6, waiting for transfers between devices, shifted(): lax.ppermute(value, axis, [(source, source + steps) for source in range(l...  5.66 us
    dot_general x4, matrix products, strided_cells(): mixed = jnp.dot(flat, weight, preferred_element_type=jnp.float32)  5.07 us
    unnamed x75, local copies, waits for them, and re-layouts  3.73 us
  transfers between devices with their start and end apart: 6, of which 3 were waited for; matrix products, arithmetic and copies ran while one was open for 7% of the time, Pallas kernels for 0%

profile of v4, /device:TPU:6, one launch (start us, length us, event | category | flops | bytes accessed | tf_op | source)
XLA Modules:
  0.0 150.8 jit_solution(1149958784928321987)
XLA Ops:
  0.7 1.0 slice.912
  1.7 1.8 %collective-permute-start = (bf16[17,4096]{1,0:T(8,128)(2,1)S(1)}, bf16[17,4096]{1,0:T(8,128)(2,1)S(1)}, u32[]{:S(2)}, u32[]{:S(2)}) collective-permute-start(bf16[17,4096]{1,0:T(8,128)(2,1)S(1)} %slice.912), channel_id=1, source_target_pairs={{0,16},{16,32},{32,48},{48,64},{64,80},{80,96},{96,112},{112,128},... | collective-permute-start | bytes 417800 | tf_op jit(solution)/shard_map/ppermute | solution.py:14
  3.5 0.9 slice.913
  4.3 1.3 collective-permute-start.1
  5.6 1.0 slice_bitcast_fusion.54
  6.6 1.6 %slice_bitcast_fusion.45 = (f32[32]{0:T(128)}, f32[32]{0:T(128)}, f32[32]{0:T(128)}, f32[32]{0:T(128)}, f32[32]{0:T(128)}, /*index=5*/f32[32]{0:T(128)}, f32[32]{0:T(128)}, f32[32]{0:T(128)}, f32[32]{0:T(128)}) fusion(f32[9,32]{1,0:T(8,128)} %param.16), kind=kLoop, calls=%fused_computation.242 | loop fusion | bytes 2304 | tf_op jit(solution)/shard_map/slice | solution.py:90
  8.2 1.6 %slice_bitcast_fusion.36 = (f32[64]{0:T(128)}, f32[64]{0:T(128)}, f32[64]{0:T(128)}, f32[64]{0:T(128)}, f32[64]{0:T(128)}, /*index=5*/f32[64]{0:T(128)}, f32[64]{0:T(128)}, f32[64]{0:T(128)}, f32[64]{0:T(128)}) fusion(f32[9,64]{1,0:T(8,128)} %param.18), kind=kLoop, calls=%fused_computation.233 | loop fusion | bytes 4608 | tf_op jit(solution)/shard_map/slice | solution.py:90
  9.8 1.0 fusion.186
  10.8 1.6 %slice_bitcast_fusion.27 = (f32[128]{0:T(128)S(1)}, f32[128]{0:T(128)S(1)}, f32[128]{0:T(128)S(1)}, f32[128]{0:T(128)S(1)}, f32[128]{0:T(128)}, /*index=5*/f32[1...) fusion(f32[9,128]{1,0:T(8,128)} %param.20), kind=kLoop, calls=%fused_computation.224 | loop fusion | bytes 9216 | tf_op jit(solution)/shard_map/slice | solution.py:90
  12.4 1.1 pad_maximum_fusion
  13.6 3.5 %collective-permute-start.2 = (bf16[51,544]{1,0:T(8,128)(2,1)S(1)}, bf16[51,544]{1,0:T(8,128)(2,1)S(1)}, u32[]{:S(2)}, u32[]{:S(2)}) collective-permute-start(bf16[51,544]{1,0:T(8,128)(2,1)S(1)} %slice.1167), channel_id=1, source_target_pairs={{0,1},{1,2},{2,3},{3,4},{4,5},{5,6},{6,7},{7,8},{8,9},{9,10},{10,1... | collective-permute-start | bytes 166472 | tf_op jit(solution)/shard_map/ppermute | solution.py:14
  17.1 0.5 compare_or_fusion
  18.5 4.5 %collective-permute-start.3 = (bf16[51,64]{1,0:T(8,128)(2,1)S(1)}, bf16[51,64]{1,0:T(8,128)(2,1)S(1)}, u32[]{:S(2)}, u32[]{:S(2)}) collective-permute-start(bf16[51,64]{1,0:T(8,128)(2,1)S(1)} %slice.1171), channel_id=1, source_target_pairs={{1,0},{2,1},{3,2},{4,3},{5,4},{6,5},{7,6},{8,7},{9,8},{10,9},{11,1... | collective-permute-start | bytes 19592 | tf_op jit(solution)/shard_map/ppermute | solution.py:14
  23.3 1.1 collective-permute-done.3
  24.4 0.8 concatenate.34
  25.2 1.3 fusion.5
  26.4 1.6 %reshape.640 = bf16[6721,32]{1,0:T(8,128)(2,1)S(1)} reshape(bf16[47,4576]{1,0:T(8,128)(2,1)S(1)} %fusion.5) | data formatting | bytes 860288 | tf_op jit(solution)/shard_map/reshape | solution.py:43
  28.0 1.4 fusion.13
  29.5 2.5 %copy.45 = f32[6721,32]{1,0:T(8,128)} copy(f32[6721,32]{0,1:T(8,128)S(1)} %fusion.13) | data formatting | bytes 1720576 | tf_op jit(solution)/shard_map/mul | solution.py:38
  32.0 2.5 %reshape.641 = f32[47,4576]{1,0:T(8,128)S(1)} reshape(f32[6721,32]{1,0:T(8,128)} %copy.45) | data formatting | bytes 1720576 | tf_op jit(solution)/shard_map/reshape | solution.py:45
  34.7 0.4 slice.944
  35.2 0.4 slice.956
  35.6 0.7 slice.968
  39.5 0.9 reshape.677
  41.0 0.9 copy.85
  41.9 1.0 copy.59
  43.4 0.8 reshape.680
  46.1 0.8 reshape.678
  47.5 0.9 copy.87
  48.4 1.0 copy.63
  49.7 0.4 fusion.33
  53.7 0.4 slice.1016
  54.4 0.4 slice.1040
  56.7 3.6 %collective-permute-start.4 = (bf16[1,8,512]{2,1,0:T(8,128)(2,1)S(1)}, bf16[1,8,512]{2,1,0:T(8,128)(2,1)S(1)}, u32[]{:S(2)}, u32[]{:S(2)}) collective-permute-start(bf16[1,8,512]{2,1,0:T(8,128)(2,1)S(1)} %slice_bitcast_fusion), channel_id=1, source_target_pairs={{0,16},{16,32},{32,48},{48,64},{64,80},{80,96},{96,112},{112,128},... | collective-permute-start | bytes 24584 | tf_op jit(solution)/shard_map/ppermute | solution.py:14
  60.4 0.8 collective-permute-done.4
  61.1 3.1 %collective-permute-start.5 = (bf16[3,7,512]{2,1,0:T(8,128)(2,1)S(1)}, bf16[3,7,512]{2,1,0:T(8,128)(2,1)S(1)}, u32[]{:S(2)}, u32[]{:S(2)}) collective-permute-start(bf16[3,7,512]{2,1,0:T(8,128)(2,1)S(1)} %pad_maximum_fusion.1), channel_id=1, source_target_pairs={{0,1},{1,2},{2,3},{3,4},{4,5},{5,6},{6,7},{7,8},{8,9},{9,10},{10,1... | collective-permute-start | bytes 64520 | tf_op jit(solution)/shard_map/ppermute | solution.py:14
  64.3 0.9 slice.1178
  65.2 3.8 %collective-permute-done.5 = bf16[3,7,512]{2,1,0:T(8,128)(2,1)S(1)} collective-permute-done((bf16[3,7,512]{2,1,0:T(8,128)(2,1)S(1)}, bf16[3,7,512]{2,1,0:T(8,128)(2,1)S(1)}, u32[]{:S(2)}, u32[]{:S(2)}) %collective-permute-start.5) | collective-permute-done | bytes 21536 | tf_op jit(solution)/shard_map/ppermute | solution.py:14
  69.2 1.3 fusion.114
  70.4 3.7 %all-gather.2 = bf16[2,7,512]{2,1,0:T(8,128)(2,1)S(1)} all-gather(bf16[1,7,512]{2,1,0:T(8,128)(2,1)S(1)} %fusion.114), channel_id=2, replica_groups=mesh['zh'=4,'zl'=4,'core'=2,'x'=4,'y'=4] {'core'}, dimensions={0}, use_global_device_ids=true | all-gather | bytes 21504 | tf_op jit(solution)/shard_map/all_gather | solution.py:138
  74.1 16.4 %all_gather.16 = bf16[8,7,512]{2,1,0:T(8,128)(2,1)S(1)} all-gather(bf16[2,7,512]{2,1,0:T(8,128)(2,1)S(1)} %all-gather.2), channel_id=1, replica_groups=mesh['zh'=4,'zl'=4,'core'=2,'x'=4,'y'=4] {'zl'}, dimensions={0}, use_global_device_ids=true | all-gather | bytes 71680 | tf_op jit(solution)/shard_map/all_gather | solution.py:138
  90.6 28.3 %all_gather.17 = bf16[32,7,512]{2,0,1:T(8,128)(2,1)S(1)} all-gather(bf16[8,7,512]{2,0,1:T(8,128)(2,1)S(1)} %copy.65), channel_id=1, replica_groups=mesh['zh'=4,'zl'=4,'core'=2,'x'=4,'y'=4] {'zh'}, dimensions={0}, use_global_device_ids=true | all-gather | bytes 286720 | tf_op jit(solution)/shard_map/all_gather | solution.py:138
  120.6 1.3 fusion.51
  122.1 1.3 fusion.126
  123.4 11.9 %all-gather.1 = bf16[8,2048]{1,0:T(8,128)(2,1)S(1)} all-gather(bf16[8,512]{1,0:T(8,128)(2,1)S(1)} %fusion.126), channel_id=3, replica_groups=mesh['zh'=4,'zl'=4,'core'=2,'x'=4,'y'=4] {'y'}, dimensions={1}, use_global_device_ids=true | all-gather | bytes 40960 | tf_op jit(solution)/shard_map/all_gather | solution.py:142
  135.3 12.0 %all_gather.19 = bf16[8,16,512]{2,0,1:T(8,128)(2,1)S(1)} all-gather(bf16[8,4,512]{2,0,1:T(8,128)(2,1)S(1)} %bitcast.261), channel_id=1, replica_groups=mesh['zh'=4,'zl'=4,'core'=2,'x'=4,'y'=4] {'x'}, dimensions={1}, use_global_device_ids=true | all-gather | bytes 163840 | tf_op jit(solution)/shard_map/all_gather | solution.py:142
  148.8 1.3 fusion.71
  150.1 0.6 reshape_reshape.3
  (247 shorter events, 16.7 us)
Async XLA Ops:
  0.6 55.9 %copy-start = (bf16[256,512]{1,0:T(8,128)(2,1)S(1)}, bf16[256,512]{1,0:T(8,128)(2,1)}, u32[]{:S(2)}) copy-start(bf16[256,512]{1,0:T(8,128)(2,1)} %param.23) | copy-start | bytes 786436
  0.6 22.3 %copy-start.1 = (bf16[32,4096]{1,0:T(8,128)(2,1)S(1)}, bf16[32,4096]{1,0:T(8,128)(2,1)}, u32[]{:S(2)}) copy-start(bf16[32,4096]{1,0:T(8,128)(2,1)} %param.13) | copy-start | bytes 786436
  1.7 10.7 %collective-permute-start = (bf16[17,4096]{1,0:T(8,128)(2,1)S(1)}, bf16[17,4096]{1,0:T(8,128)(2,1)S(1)}, u32[]{:S(2)}, u32[]{:S(2)}) collective-permute-start(bf16[17,4096]{1,0:T(8,128)(2,1)S(1)} %slice.912), channel_id=1, source_target_pairs={{0,16},{16,32},{32,48},{48,64},{64,80},{80,96},{96,112},{112,128},... | collective-permute-start | bytes 417800 | tf_op jit(solution)/shard_map/ppermute | solution.py:14
  4.3 8.1 %collective-permute-start.1 = (bf16[2,4096]{1,0:T(2,128)(2,1)S(1)}, bf16[2,4096]{1,0:T(2,128)(2,1)S(1)}, u32[]{:S(2)}, u32[]{:S(2)}) collective-permute-start(bf16[2,4096]{1,0:T(2,128)(2,1)S(1)} %slice.913), channel_id=1, source_target_pairs={{16,0},{32,16},{48,32},{64,48},{80,64},{96,80},{112,96},{128,112},... | collective-permute-start | bytes 49160 | tf_op jit(solution)/shard_map/ppermute | solution.py:14
  13.6 9.4 %collective-permute-start.2 = (bf16[51,544]{1,0:T(8,128)(2,1)S(1)}, bf16[51,544]{1,0:T(8,128)(2,1)S(1)}, u32[]{:S(2)}, u32[]{:S(2)}) collective-permute-start(bf16[51,544]{1,0:T(8,128)(2,1)S(1)} %slice.1167), channel_id=1, source_target_pairs={{0,1},{1,2},{2,3},{3,4},{4,5},{5,6},{6,7},{7,8},{8,9},{9,10},{10,1... | collective-permute-start | bytes 166472 | tf_op jit(solution)/shard_map/ppermute | solution.py:14
  18.5 5.9 %collective-permute-start.3 = (bf16[51,64]{1,0:T(8,128)(2,1)S(1)}, bf16[51,64]{1,0:T(8,128)(2,1)S(1)}, u32[]{:S(2)}, u32[]{:S(2)}) collective-permute-start(bf16[51,64]{1,0:T(8,128)(2,1)S(1)} %slice.1171), channel_id=1, source_target_pairs={{1,0},{2,1},{3,2},{4,3},{5,4},{6,5},{7,6},{8,7},{9,8},{10,9},{11,1... | collective-permute-start | bytes 19592 | tf_op jit(solution)/shard_map/ppermute | solution.py:14
  32.0 2.5 %copy-start.32 = (pred[47]{0:T(512)(128)(4,1)S(1)}, pred[47]{0:T(512)(128)(4,1)}, u32[]{:S(2)}) copy-start(pred[47]{0:T(512)(128)(4,1)} %compare_or_fusion) | copy-start | bytes 145
  46.9 2.7 %copy-start.2 = (f32[1633,32]{0,1:T(8,128)S(1)}, f32[1633,32]{0,1:T(8,128)}, u32[]{:S(2)}) copy-start(f32[1633,32]{0,1:T(8,128)} %reshape.677) | copy-start | bytes 627076
  46.9 2.7 %copy-start.3 = (f32[1633,32]{0,1:T(8,128)S(1)}, f32[1633,32]{0,1:T(8,128)}, u32[]{:S(2)}) copy-start(f32[1633,32]{0,1:T(8,128)} %reshape.680) | copy-start | bytes 627076
  46.9 2.7 %copy-start.8 = (bf16[32,64]{1,0:T(8,128)(2,1)S(1)}, bf16[32,64]{1,0:T(8,128)(2,1)}, u32[]{:S(2)}) copy-start(bf16[32,64]{1,0:T(8,128)(2,1)} %param.17) | copy-start | bytes 12292
  46.9 2.7 %copy-start.23 = (f32[32]{0:T(128)S(1)}, f32[32]{0:T(128)}, u32[]{:S(2)}) copy-start(f32[32]{0:T(128)} %get-tuple-element.107) | copy-start | bytes 388
  46.9 2.7 %copy-start.24 = (f32[32]{0:T(128)S(1)}, f32[32]{0:T(128)}, u32[]{:S(2)}) copy-start(f32[32]{0:T(128)} %get-tuple-element.108) | copy-start | bytes 388
  47.0 2.7 %copy-start.25 = (f32[32]{0:T(128)S(1)}, f32[32]{0:T(128)}, u32[]{:S(2)}) copy-start(f32[32]{0:T(128)} %get-tuple-element.109) | copy-start | bytes 388
  47.0 2.7 %copy-start.26 = (f32[32]{0:T(128)S(1)}, f32[32]{0:T(128)}, u32[]{:S(2)}) copy-start(f32[32]{0:T(128)} %get-tuple-element.110) | copy-start | bytes 388
  47.0 2.7 %copy-start.27 = (f32[32]{0:T(128)S(1)}, f32[32]{0:T(128)}, u32[]{:S(2)}) copy-start(f32[32]{0:T(128)} %get-tuple-element.111) | copy-start | bytes 388
  47.0 2.7 %copy-start.28 = (f32[32]{0:T(128)S(1)}, f32[32]{0:T(128)}, u32[]{:S(2)}) copy-start(f32[32]{0:T(128)} %get-tuple-element.112) | copy-start | bytes 388
  47.0 2.7 %copy-start.29 = (f32[32]{0:T(128)S(1)}, f32[32]{0:T(128)}, u32[]{:S(2)}) copy-start(f32[32]{0:T(128)} %get-tuple-element.113) | copy-start | bytes 388
  47.0 2.7 %copy-start.30 = (f32[32]{0:T(128)S(1)}, f32[32]{0:T(128)}, u32[]{:S(2)}) copy-start(f32[32]{0:T(128)} %get-tuple-element.114) | copy-start | bytes 388
  47.0 2.7 %copy-start.31 = (f32[32]{0:T(128)S(1)}, f32[32]{0:T(128)}, u32[]{:S(2)}) copy-start(f32[32]{0:T(128)} %get-tuple-element.115) | copy-start | bytes 388
  47.3 2.4 %copy-start.4 = (f32[1633,32]{0,1:T(8,128)S(1)}, f32[1633,32]{0,1:T(8,128)}, u32[]{:S(2)}) copy-start(f32[1633,32]{0,1:T(8,128)} %reshape.678) | copy-start | bytes 627076
  52.3 0.8 copy-start.7
  52.3 0.8 copy-start.14
  52.3 0.8 copy-start.15
  52.3 0.8 copy-start.16
  52.4 0.8 copy-start.17
  52.4 0.8 copy-start.18
  52.4 0.8 copy-start.19
  52.4 0.8 copy-start.20
  52.4 0.8 copy-start.21
  52.4 0.8 copy-start.22
  54.8 0.8 copy-start.6
  54.9 0.8 copy-start.9
  54.9 0.8 copy-start.10
  54.9 0.8 copy-start.11
  54.9 0.8 copy-start.12
  54.9 0.8 copy-start.13
  55.2 5.1 %copy-start.5 = (f32[4,9,512]{2,0,1:T(4,128)S(1)}, f32[4,9,512]{2,0,1:T(4,128)}, u32[]{:S(2)}) copy-start(f32[4,9,512]{2,0,1:T(4,128)} %param.24) | copy-start | bytes 221188
  56.7 4.4 %collective-permute-start.4 = (bf16[1,8,512]{2,1,0:T(8,128)(2,1)S(1)}, bf16[1,8,512]{2,1,0:T(8,128)(2,1)S(1)}, u32[]{:S(2)}, u32[]{:S(2)}) collective-permute-start(bf16[1,8,512]{2,1,0:T(8,128)(2,1)S(1)} %slice_bitcast_fusion), channel_id=1, source_target_pairs={{0,16},{16,32},{32,48},{48,64},{64,80},{80,96},{96,112},{112,128},... | collective-permute-start | bytes 24584 | tf_op jit(solution)/shard_map/ppermute | solution.py:14
  61.1 7.8 %collective-permute-start.5 = (bf16[3,7,512]{2,1,0:T(8,128)(2,1)S(1)}, bf16[3,7,512]{2,1,0:T(8,128)(2,1)S(1)}, u32[]{:S(2)}, u32[]{:S(2)}) collective-permute-start(bf16[3,7,512]{2,1,0:T(8,128)(2,1)S(1)} %pad_maximum_fusion.1), channel_id=1, source_target_pairs={{0,1},{1,2},{2,3},{3,4},{4,5},{5,6},{6,7},{7,8},{8,9},{9,10},{10,1... | collective-permute-start | bytes 64520 | tf_op jit(solution)/shard_map/ppermute | solution.py:14

commit v5 on v2

--- a/solution.py
+++ b/solution.py
@@ -23,6 +23,17 @@
         high = lax.ppermute(lax.slice_in_dim(block, 0, width, axis=dim), axis, backward)
         block = jnp.concatenate([low, block, high], axis=dim)
     return block
+
+
+def moved(value, down, right):
+    rows = lax.axis_size("gx")
+    cols = lax.axis_size("gy")
+    pairs = []
+    for row in range(rows):
+        for col in range(cols):
+            if 0 <= row + down < rows and 0 <= col + right < cols:
+                pairs.append((row * cols + col, (row + down) * cols + col + right))
+    return lax.ppermute(value, ("gx", "gy"), pairs)
 
 
 def gelu_tanh(value):
@@ -88,12 +99,24 @@
     cols = field.shape[1] // chans
     depth = 4
     margin = 2**depth - 1
-    upper = shifted(field[-margin - 2 :], "gx", 1)
-    lower = shifted(field[:2], "gx", -1)
-    stacked = jnp.concatenate([upper, field, lower], axis=0)
-    leftside = shifted(stacked[:, -(margin + 2) * chans :], "gy", 1)
-    rightside = shifted(stacked[:, : 2 * chans], "gy", -1)
-    flat_pad = jnp.concatenate([leftside, stacked, rightside], axis=1)
+    top = margin + 2
+    edges = {}
+    for down, row_part in ((1, field[-top:]), (0, field), (-1, field[:2])):
+        for right, width in ((1, top), (0, None), (-1, 2)):
+            if width is None:
+                part = row_part
+            elif right == 1:
+                part = row_part[:, -width * chans :]
+            else:
+                part = row_part[:, : width * chans]
+            edges[down, right] = part if down == right == 0 else moved(part, down, right)
+    flat_pad = jnp.concatenate(
+        [
+            jnp.concatenate([edges[down, right] for right in (1, 0, -1)], axis=1)
+            for down in (1, 0, -1)
+        ],
+        axis=0,
+    )
     ext_rows = rows + margin
     ext_cols = cols + margin
     tiled = jnp.tile(dw0, (1, ext_cols))

time: 142 us -> 152 us (1.070)
  starting transfers between devices: 17.7 us -> 30.9 us
  matrix products: 7.61 us -> 5.34 us
    ppermute x0 -> x8, starting transfers between devices: none -> 25.8 us  [moved(): return lax.ppermute(value, ('gx', 'gy'), pairs)]
    ppermute x6 -> x2, starting transfers between devices: 17.7 us -> 5.03 us  [shifted(): lax.ppermute(value, axis, [(source, source + steps) for source in range(l...]
    slice x4 -> x8, local copies, waits for them, and re-layouts: 1.99 us -> 6.45 us  [the longest x3 2.48 us: local(): part = row_part[:, -width * chans:]]
    convert_element_type x36, local copies, waits for them, and re-layouts: 6.18 us -> 2.94 us  [strided_flat(): total = total + piece.astype(jnp.float32) * tiled[3 * first + second]]
    dot_general x4, matrix products: 5.07 us -> 1.94 us  [strided_cells(): mixed = jnp.dot(flat, weight, preferred_element_type=jnp.float32)]
    unnamed x75 -> x61, local copies, waits for them, and re-layouts: 3.73 us -> 2.36 us
    ppermute x6 -> x2, waiting for transfers between devices: 5.66 us -> 5.75 us  [shifted(): lax.ppermute(value, axis, [(source, source + steps) for source in range(l...]
  transfers between devices with their start and end apart: 6 -> 10, of which waited for: 3 -> 3; matrix products, arithmetic and copies ran while one was open for 7% -> 10% of each run, Pallas kernels for 0% -> 0%
where the time goes in v5:
time: 152 us; the launch traced here: 149 us
  blocking collectives  60.5 us (40%)
  local copies, waits for them, and re-layouts  41.5 us (27%)
  starting transfers between devices  30.9 us (20%)
  waiting for transfers between devices  6.05 us (4%)
  matrix products  5.34 us (4%)
  other arithmetic  2.93 us (2%)
  between operations  2.38 us (2%)
    all_gather x1, blocking collectives, local(): hidden = lax.all_gather(hidden, 'gx', axis=0, tiled=True)  39 us
    ppermute x8, starting transfers between devices, moved(): return lax.ppermute(value, ('gx', 'gy'), pairs)  25.8 us
    all_gather x1, blocking collectives, local(): hidden = lax.all_gather(hidden, 'gy', axis=1, tiled=True)  21.5 us
    slice x4, local copies, waits for them, and re-layouts, strided_flat(): total = total + piece.astype(jnp.float32) * tiled[3 * first + second]  5.77 us
    ppermute x2, waiting for transfers between devices, shifted(): lax.ppermute(value, axis, [(source, source + steps) for source in range(l...  5.75 us
    ppermute x2, starting transfers between devices, shifted(): lax.ppermute(value, axis, [(source, source + steps) for source in range(l...  5.03 us
    slice x12, local copies, waits for them, and re-layouts, strided_flat(): slab = ext[first:first + 2 * rows:2]  3.67 us
    dot_general x5, matrix products, point_flat(): mixed = jnp.dot(flat, weight, preferred_element_type=jnp.float32)  3.41 us
  transfers between devices with their start and end apart: 10, of which 3 were waited for; matrix products, arithmetic and copies ran while one was open for 10% of the time, Pallas kernels for 0%

profile of v5, /device:TPU:6, one launch (start us, length us, event | category | flops | bytes accessed | tf_op | source)
XLA Modules:
  0.0 149.5 jit_solution(3928388793844755777)
XLA Ops:
  0.7 1.0 slice.929
  1.7 1.8 %collective-permute-start.1 = (bf16[17,4096]{1,0:T(8,128)(2,1)S(1)}, bf16[17,4096]{1,0:T(8,128)(2,1)S(1)}, u32[]{:S(2)}, u32[]{:S(2)}) collective-permute-start(bf16[17,4096]{1,0:T(8,128)(2,1)S(1)} %slice.929), channel_id=1, source_target_pairs={{0,16},{1,17},{2,18},{3,19},{4,20},{5,21},{6,22},{7,23},{8,24},{9,... | collective-permute-start | bytes 417800 | tf_op jit(solution)/shard_map/ppermute | solution.py:36
  3.5 0.8 slice.928
  4.3 5.3 %collective-permute-start = (bf16[17,544]{1,0:T(8,128)(2,1)S(1)}, bf16[17,544]{1,0:T(8,128)(2,1)S(1)}, u32[]{:S(2)}, u32[]{:S(2)}) collective-permute-start(bf16[17,544]{1,0:T(8,128)(2,1)S(1)} %slice.928), channel_id=1, source_target_pairs={{0,17},{1,18},{2,19},{3,20},{4,21},{5,22},{6,23},{7,24},{8,25},{9,... | collective-permute-start | bytes 55496 | tf_op jit(solution)/shard_map/ppermute | solution.py:36
  9.6 0.9 slice.952
  10.4 1.3 collective-permute-start.6
  11.7 0.8 slice.951
  12.5 1.3 collective-permute-start.5
  13.8 0.7 slice.953
  14.5 1.3 collective-permute-start.7
  15.8 1.0 slice_bitcast_fusion.54
  16.8 1.6 %slice_bitcast_fusion.45 = (f32[32]{0:T(128)}, f32[32]{0:T(128)}, f32[32]{0:T(128)}, f32[32]{0:T(128)}, f32[32]{0:T(128)}, /*index=5*/f32[32]{0:T(128)}, f32[32]{0:T(128)}, f32[32]{0:T(128)}, f32[32]{0:T(128)}) fusion(f32[9,32]{1,0:T(8,128)} %param.16), kind=kLoop, calls=%fused_computation.257 | loop fusion | bytes 2304 | tf_op jit(solution)/shard_map/slice | solution.py:92
  18.4 1.6 %slice_bitcast_fusion.36 = (f32[64]{0:T(128)}, f32[64]{0:T(128)}, f32[64]{0:T(128)}, f32[64]{0:T(128)}, f32[64]{0:T(128)}, /*index=5*/f32[64]{0:T(128)}, f32[64]{0:T(128)}, f32[64]{0:T(128)}, f32[64]{0:T(128)}) fusion(f32[9,64]{1,0:T(8,128)} %param.18), kind=kLoop, calls=%fused_computation.248 | loop fusion | bytes 4608 | tf_op jit(solution)/shard_map/slice | solution.py:92
  19.9 1.6 %slice_bitcast_fusion.27 = (f32[128]{0:T(128)S(1)}, f32[128]{0:T(128)}, f32[128]{0:T(128)}, f32[128]{0:T(128)}, f32[128]{0:T(128)}, /*index=5*/f32[128]{0:T(128)}, f32[128]{0:T(128)}, f32[128]{0:T(128)}, f32[128]{0:T(128)}) fusion(f32[9,128]{1,0:T(8,128)} %param.20), kind=kLoop, calls=%fused_computation.239 | loop fusion | bytes 9216 | tf_op jit(solution)/shard_map/slice | solution.py:92
  21.5 1.0 fusion.191
  22.6 0.7 slice.930
  23.3 0.9 slice.931
  24.1 0.7 slice.932
  24.8 7.0 %collective-permute-start.2 = (bf16[17,64]{1,0:T(8,128)(2,1)S(1)}, bf16[17,64]{1,0:T(8,128)(2,1)S(1)}, u32[]{:S(2)}, u32[]{:S(2)}) collective-permute-start(bf16[17,64]{1,0:T(8,128)(2,1)S(1)} %slice.930), channel_id=1, source_target_pairs={{1,16},{2,17},{3,18},{4,19},{5,20},{6,21},{7,22},{8,23},{9,24},{10... | collective-permute-start | bytes 6536 | tf_op jit(solution)/shard_map/ppermute | solution.py:36
  31.8 1.9 %collective-permute-start.3 = (bf16[32,544]{1,0:T(8,128)(2,1)S(1)}, bf16[32,544]{1,0:T(8,128)(2,1)S(1)}, u32[]{:S(2)}, u32[]{:S(2)}) collective-permute-start(bf16[32,544]{1,0:T(8,128)(2,1)S(1)} %slice.931), channel_id=1, source_target_pairs={{0,1},{1,2},{2,3},{3,4},{4,5},{5,6},{6,7},{7,8},{8,9},{9,10},{10,1... | collective-permute-start | bytes 104456 | tf_op jit(solution)/shard_map/ppermute | solution.py:36
  33.8 6.0 %collective-permute-start.4 = (bf16[32,64]{1,0:T(8,128)(2,1)S(1)}, bf16[32,64]{1,0:T(8,128)(2,1)S(1)}, u32[]{:S(2)}, u32[]{:S(2)}) collective-permute-start(bf16[32,64]{1,0:T(8,128)(2,1)S(1)} %slice.932), channel_id=1, source_target_pairs={{1,0},{2,1},{3,2},{4,3},{5,4},{6,5},{7,6},{8,7},{9,8},{10,9},{11,1... | collective-permute-start | bytes 12296 | tf_op jit(solution)/shard_map/ppermute | solution.py:36
  41.8 1.6 %fusion.5 = bf16[47,4576]{1,0:T(8,128)(2,1)S(1)} fusion(bf16[32,4704]{1,0:T(8,128)(2,1)S(1)} %concatenate.39, bf16[17,4704]{1,0:T(8,128)(2,1)S(1)} %concatenate.38, bf16[51,4704]{1,0:T(8,128)(2,1)S(1)} %pad_maximum_fusion, f32[4576]{0:T(1024)S(1)} %tile.78, f32[4576]{0:T(1024)S(1)} %tile.76, f32[4576]{0:T(1024)S(1)} %tile.74, f32[4576]{0:T(1024)S(1)} %tile.72, ...), kind=kLoop, calls=%fused_computation.13 | loop fusion | flops 9678240 | bytes 2346304 | tf_op jit(solution)/shard_map/convert_element_type | solution.py:45
  43.5 1.6 %reshape.640 = bf16[6721,32]{1,0:T(8,128)(2,1)S(1)} reshape(bf16[47,4576]{1,0:T(8,128)(2,1)S(1)} %fusion.5) | data formatting | bytes 860288 | tf_op jit(solution)/shard_map/reshape | solution.py:45
  45.1 1.7 %fusion.13 = f32[6721,32]{0,1:T(8,128)} fusion(bf16[6721,32]{1,0:T(8,128)(2,1)S(1)} %reshape.640, bf16[32,32]{1,0:T(8,128)(2,1)S(1)} %copy-done.25), kind=kOutput, calls=%fused_computation.22 | convolution fusion | flops 15485184 | bytes 1292480 | tf_op jit(solution)/shard_map/dot_general | solution.py:46
  46.7 3.3 %copy.47 = f32[6721,32]{1,0:T(8,128)} copy(f32[6721,32]{0,1:T(8,128)} %fusion.13) | data formatting | bytes 1720576 | tf_op jit(solution)/shard_map/mul | solution.py:40
  50.0 2.4 %reshape.641 = f32[47,4576]{1,0:T(8,128)S(1)} reshape(f32[6721,32]{1,0:T(8,128)} %copy.47) | data formatting | bytes 1720576 | tf_op jit(solution)/shard_map/reshape | solution.py:47
  52.5 0.4 and_select_fusion
  52.9 0.4 slice.964
  53.3 0.4 slice.976
  53.8 0.6 slice.988
  54.5 0.3 reshape.642
  56.1 0.3 reshape.644
  57.4 0.8 reshape.677
  60.9 0.3 reshape.645
  61.9 0.3 reshape.647
  62.9 1.1 fusion.38
  67.6 0.4 slice.1036
  68.0 0.4 slice.1048
  68.4 0.6 slice.1060
  70.8 3.1 %collective-permute-start.8 = (bf16[1,8,512]{2,1,0:T(8,128)(2,1)S(1)}, bf16[1,8,512]{2,1,0:T(8,128)(2,1)S(1)}, u32[]{:S(2)}, u32[]{:S(2)}) collective-permute-start(bf16[1,8,512]{2,1,0:T(8,128)(2,1)S(1)} %slice_bitcast_fusion), channel_id=1, source_target_pairs={{0,16},{16,32},{32,48},{48,64},{64,80},{80,96},{96,112},{112,128},... | collective-permute-start | bytes 24584 | tf_op jit(solution)/shard_map/ppermute | solution.py:12
  74.0 0.8 collective-permute-done.8
  74.8 1.9 %collective-permute-start.9 = (bf16[3,7,512]{2,1,0:T(8,128)(2,1)S(1)}, bf16[3,7,512]{2,1,0:T(8,128)(2,1)S(1)}, u32[]{:S(2)}, u32[]{:S(2)}) collective-permute-start(bf16[3,7,512]{2,1,0:T(8,128)(2,1)S(1)} %pad_maximum_fusion.2), channel_id=1, source_target_pairs={{0,1},{1,2},{2,3},{3,4},{4,5},{5,6},{6,7},{7,8},{8,9},{9,10},{10,1... | collective-permute-start | bytes 64520 | tf_op jit(solution)/shard_map/ppermute | solution.py:12
  76.8 0.9 slice.1200
  77.6 5.0 %collective-permute-done.9 = bf16[3,7,512]{2,1,0:T(8,128)(2,1)S(1)} collective-permute-done((bf16[3,7,512]{2,1,0:T(8,128)(2,1)S(1)}, bf16[3,7,512]{2,1,0:T(8,128)(2,1)S(1)}, u32[]{:S(2)}, u32[]{:S(2)}) %collective-permute-start.9) | collective-permute-done | bytes 21536 | tf_op jit(solution)/shard_map/ppermute | solution.py:12
  82.8 1.3 fusion.119
  84.1 39.0 %all-gather.2 = bf16[32,7,512]{2,1,0:T(8,128)(2,1)S(1)} all-gather(bf16[1,7,512]{2,1,0:T(8,128)(2,1)S(1)} %fusion.119), channel_id=2, replica_groups=mesh['gx'=32,'gy'=16] {'gx'}, dimensions={0}, use_global_device_ids=true | all-gather | bytes 236544 | tf_op jit(solution)/shard_map/all_gather | solution.py:151
  125.5 21.5 %all-gather.1 = bf16[8,8192]{1,0:T(8,128)(2,1)S(1)} all-gather(bf16[8,512]{1,0:T(8,128)(2,1)S(1)} %fusion.131), channel_id=3, replica_groups=mesh['gx'=32,'gy'=16] {'gy'}, dimensions={1}, use_global_device_ids=true | all-gather | bytes 139264 | tf_op jit(solution)/shard_map/all_gather | solution.py:154
  148.9 0.6 reshape_reshape.3
  (243 shorter events, 17.0 us)
Async XLA Ops:
  0.6 70.0 %copy-start = (bf16[256,512]{1,0:T(8,128)(2,1)S(1)}, bf16[256,512]{1,0:T(8,128)(2,1)}, u32[]{:S(2)}) copy-start(bf16[256,512]{1,0:T(8,128)(2,1)} %param.23) | copy-start | bytes 786436
  0.6 40.5 %copy-start.1 = (bf16[32,4096]{1,0:T(8,128)(2,1)S(1)}, bf16[32,4096]{1,0:T(8,128)(2,1)}, u32[]{:S(2)}) copy-start(bf16[32,4096]{1,0:T(8,128)(2,1)} %param.13) | copy-start | bytes 786436
  1.7 39.8 %collective-permute-start.1 = (bf16[17,4096]{1,0:T(8,128)(2,1)S(1)}, bf16[17,4096]{1,0:T(8,128)(2,1)S(1)}, u32[]{:S(2)}, u32[]{:S(2)}) collective-permute-start(bf16[17,4096]{1,0:T(8,128)(2,1)S(1)} %slice.929), channel_id=1, source_target_pairs={{0,16},{1,17},{2,18},{3,19},{4,20},{5,21},{6,22},{7,23},{8,24},{9,... | collective-permute-start | bytes 417800 | tf_op jit(solution)/shard_map/ppermute | solution.py:36
  4.3 37.1 %collective-permute-start = (bf16[17,544]{1,0:T(8,128)(2,1)S(1)}, bf16[17,544]{1,0:T(8,128)(2,1)S(1)}, u32[]{:S(2)}, u32[]{:S(2)}) collective-permute-start(bf16[17,544]{1,0:T(8,128)(2,1)S(1)} %slice.928), channel_id=1, source_target_pairs={{0,17},{1,18},{2,19},{3,20},{4,21},{5,22},{6,23},{7,24},{8,25},{9,... | collective-permute-start | bytes 55496 | tf_op jit(solution)/shard_map/ppermute | solution.py:36
  10.4 23.3 %collective-permute-start.6 = (bf16[2,4096]{1,0:T(2,128)(2,1)S(1)}, bf16[2,4096]{1,0:T(2,128)(2,1)S(1)}, u32[]{:S(2)}, u32[]{:S(2)}) collective-permute-start(bf16[2,4096]{1,0:T(2,128)(2,1)S(1)} %slice.952), channel_id=1, source_target_pairs={{16,0},{17,1},{18,2},{19,3},{20,4},{21,5},{22,6},{23,7},{24,8},{25... | collective-permute-start | bytes 49160 | tf_op jit(solution)/shard_map/ppermute | solution.py:36
  12.5 19.3 %collective-permute-start.5 = (bf16[2,544]{1,0:T(2,128)(2,1)S(1)}, bf16[2,544]{1,0:T(2,128)(2,1)S(1)}, u32[]{:S(2)}, u32[]{:S(2)}) collective-permute-start(bf16[2,544]{1,0:T(2,128)(2,1)S(1)} %slice.951), channel_id=1, source_target_pairs={{16,1},{17,2},{18,3},{19,4},{20,5},{21,6},{22,7},{23,8},{24,9},{25... | collective-permute-start | bytes 6536 | tf_op jit(solution)/shard_map/ppermute | solution.py:36
  14.5 10.3 %collective-permute-start.7 = (bf16[2,64]{1,0:T(2,128)(2,1)S(1)}, bf16[2,64]{1,0:T(2,128)(2,1)S(1)}, u32[]{:S(2)}, u32[]{:S(2)}) collective-permute-start(bf16[2,64]{1,0:T(2,128)(2,1)S(1)} %slice.953), channel_id=1, source_target_pairs={{17,0},{18,1},{19,2},{20,3},{21,4},{22,5},{23,6},{24,7},{25,8},{26... | collective-permute-start | bytes 776 | tf_op jit(solution)/shard_map/ppermute | solution.py:36
  24.8 16.6 %collective-permute-start.2 = (bf16[17,64]{1,0:T(8,128)(2,1)S(1)}, bf16[17,64]{1,0:T(8,128)(2,1)S(1)}, u32[]{:S(2)}, u32[]{:S(2)}) collective-permute-start(bf16[17,64]{1,0:T(8,128)(2,1)S(1)} %slice.930), channel_id=1, source_target_pairs={{1,16},{2,17},{3,18},{4,19},{5,20},{6,21},{7,22},{8,23},{9,24},{10... | collective-permute-start | bytes 6536 | tf_op jit(solution)/shard_map/ppermute | solution.py:36
  31.8 9.3 %collective-permute-start.3 = (bf16[32,544]{1,0:T(8,128)(2,1)S(1)}, bf16[32,544]{1,0:T(8,128)(2,1)S(1)}, u32[]{:S(2)}, u32[]{:S(2)}) collective-permute-start(bf16[32,544]{1,0:T(8,128)(2,1)S(1)} %slice.931), channel_id=1, source_target_pairs={{0,1},{1,2},{2,3},{3,4},{4,5},{5,6},{6,7},{7,8},{8,9},{9,10},{10,1... | collective-permute-start | bytes 104456 | tf_op jit(solution)/shard_map/ppermute | solution.py:36
  33.8 7.4 %collective-permute-start.4 = (bf16[32,64]{1,0:T(8,128)(2,1)S(1)}, bf16[32,64]{1,0:T(8,128)(2,1)S(1)}, u32[]{:S(2)}, u32[]{:S(2)}) collective-permute-start(bf16[32,64]{1,0:T(8,128)(2,1)S(1)} %slice.932), channel_id=1, source_target_pairs={{1,0},{2,1},{3,2},{4,3},{5,4},{6,5},{7,6},{8,7},{9,8},{10,9},{11,1... | collective-permute-start | bytes 12296 | tf_op jit(solution)/shard_map/ppermute | solution.py:36
  41.8 3.3 %copy-start.25 = (bf16[32,32]{1,0:T(8,128)(2,1)S(1)}, bf16[32,32]{1,0:T(8,128)(2,1)}, u32[]{:S(2)}) copy-start(bf16[32,32]{1,0:T(8,128)(2,1)} %param.15) | copy-start | bytes 6148
  61.7 1.2 copy-start.2
  61.7 1.2 copy-start.6
  66.2 0.8 copy-start.5
  66.2 0.8 copy-start.15
  66.2 0.8 copy-start.16
  66.2 0.8 copy-start.17
  66.2 0.8 copy-start.18
  66.2 0.8 copy-start.19
  66.2 0.8 copy-start.20
  66.2 0.8 copy-start.21
  66.2 0.8 copy-start.22
  66.3 0.8 copy-start.23
  67.4 2.4 %copy-start.4 = (bf16[128,256]{1,0:T(8,128)(2,1)S(1)}, bf16[128,256]{1,0:T(8,128)(2,1)}, u32[]{:S(2)}) copy-start(bf16[128,256]{1,0:T(8,128)(2,1)} %param.21) | copy-start | bytes 196612
  67.4 2.4 %copy-start.7 = (f32[128]{0:T(128)S(1)}, f32[128]{0:T(128)}, u32[]{:S(2)}) copy-start(f32[128]{0:T(128)} %get-tuple-element.90) | copy-start | bytes 1540
  67.4 2.4 %copy-start.8 = (f32[128]{0:T(128)S(1)}, f32[128]{0:T(128)}, u32[]{:S(2)}) copy-start(f32[128]{0:T(128)} %get-tuple-element.91) | copy-start | bytes 1540
  67.4 2.4 %copy-start.9 = (f32[128]{0:T(128)S(1)}, f32[128]{0:T(128)}, u32[]{:S(2)}) copy-start(f32[128]{0:T(128)} %get-tuple-element.92) | copy-start | bytes 1540
  67.4 2.4 %copy-start.10 = (f32[128]{0:T(128)S(1)}, f32[128]{0:T(128)}, u32[]{:S(2)}) copy-start(f32[128]{0:T(128)} %get-tuple-element.93) | copy-start | bytes 1540
  67.4 2.4 %copy-start.11 = (f32[128]{0:T(128)S(1)}, f32[128]{0:T(128)}, u32[]{:S(2)}) copy-start(f32[128]{0:T(128)} %get-tuple-element.94) | copy-start | bytes 1540
  67.5 2.4 %copy-start.12 = (f32[128]{0:T(128)S(1)}, f32[128]{0:T(128)}, u32[]{:S(2)}) copy-start(f32[128]{0:T(128)} %get-tuple-element.95) | copy-start | bytes 1540
  67.5 2.4 %copy-start.13 = (f32[128]{0:T(128)S(1)}, f32[128]{0:T(128)}, u32[]{:S(2)}) copy-start(f32[128]{0:T(128)} %get-tuple-element.96) | copy-start | bytes 1540
  67.5 2.4 %copy-start.14 = (f32[128]{0:T(128)S(1)}, f32[128]{0:T(128)}, u32[]{:S(2)}) copy-start(f32[128]{0:T(128)} %get-tuple-element.97) | copy-start | bytes 1540
  69.2 4.8 %copy-start.3 = (f32[4,9,512]{2,0,1:T(4,128)S(1)}, f32[4,9,512]{2,0,1:T(4,128)}, u32[]{:S(2)}) copy-start(f32[4,9,512]{2,0,1:T(4,128)} %param.24) | copy-start | bytes 221188
  70.8 3.9 %collective-permute-start.8 = (bf16[1,8,512]{2,1,0:T(8,128)(2,1)S(1)}, bf16[1,8,512]{2,1,0:T(8,128)(2,1)S(1)}, u32[]{:S(2)}, u32[]{:S(2)}) collective-permute-start(bf16[1,8,512]{2,1,0:T(8,128)(2,1)S(1)} %slice_bitcast_fusion), channel_id=1, source_target_pairs={{0,16},{16,32},{32,48},{48,64},{64,80},{80,96},{96,112},{112,128},... | collective-permute-start | bytes 24584 | tf_op jit(solution)/shard_map/ppermute | solution.py:12
  74.8 7.8 %collective-permute-start.9 = (bf16[3,7,512]{2,1,0:T(8,128)(2,1)S(1)}, bf16[3,7,512]{2,1,0:T(8,128)(2,1)S(1)}, u32[]{:S(2)}, u32[]{:S(2)}) collective-permute-start(bf16[3,7,512]{2,1,0:T(8,128)(2,1)S(1)} %pad_maximum_fusion.2), channel_id=1, source_target_pairs={{0,1},{1,2},{2,3},{3,4},{4,5},{5,6},{6,7},{7,8},{8,9},{9,10},{10,1... | collective-permute-start | bytes 64520 | tf_op jit(solution)/shard_map/ppermute | solution.py:12
  76.8 48.1 %copy-start.24 = (bf16[4,512,512]{2,1,0:T(8,128)(2,1)S(1)}, bf16[4,512,512]{2,1,0:T(8,128)(2,1)}, u32[]{:S(2)}) copy-start(bf16[4,512,512]{2,1,0:T(8,128)(2,1)} %param.25) | copy-start | bytes 6291460

commit v6 on v2

--- a/solution.py
+++ b/solution.py
@@ -1,6 +1,10 @@
+import functools
+
 import jax
 import jax.numpy as jnp
 from jax import lax
+from jax.experimental import pallas as pl
+from jax.experimental.pallas import tpu as pltpu
 from jax.sharding import PartitionSpec as P
 
 LC = 4
@@ -82,6 +86,59 @@
     return point_flat(total, weight, rows, cols).astype(jnp.bfloat16)
 
 
+def pair_kernel(even_ref, odd_ref, near_ref, far_ref, w_ref, o_ref, *, rows, chans, chunk, width):
+    lanes = even_ref.shape[1]
+    total = None
+    for first in range(3):
+        if first == 1:
+            slab = odd_ref[...]
+        else:
+            slab = even_ref[pl.ds(first // 2, rows), :]
+        ahead = pltpu.roll(slab, lanes - 2 * chans, 1)
+        term = slab * near_ref[first : first + 1, :] + ahead * far_ref[first : first + 1, :]
+        total = term if total is None else total + term
+    weight = w_ref[...]
+    for index in range(lanes // chunk):
+        part = jnp.dot(
+            total[:, index * chunk : (index + 1) * chunk],
+            weight,
+            preferred_element_type=jnp.float32,
+        )
+        o_ref[:, index * width : (index + 1) * width] = gelu_tanh(part).astype(o_ref.dtype)
+
+
+def strided_kernel(ext, taps, weight):
+    chans = taps.shape[1]
+    outs = weight.shape[1]
+    rows = (ext.shape[0] - 1) // 2
+    cols = (ext.shape[1] // chans - 1) // 2
+    pairs = cols + 1
+    if pairs * 2 * chans % 128:
+        pairs += 1
+    padded_rows = -(-rows // 8) * 8
+    lanes = pairs * 2 * chans
+    source = jnp.pad(
+        ext.astype(jnp.float32),
+        ((0, 2 * padded_rows + 1 - ext.shape[0]), (0, lanes - ext.shape[1])),
+    )
+    zero = jnp.zeros_like(taps[0])
+    near = jnp.stack(
+        [jnp.tile(jnp.concatenate([taps[3 * a], taps[3 * a + 1]]), pairs) for a in range(3)]
+    )
+    far = jnp.stack([jnp.tile(jnp.concatenate([taps[3 * a + 2], zero]), pairs) for a in range(3)])
+    chunk = max(128, 2 * chans)
+    group = chunk // (2 * chans)
+    doubled = jnp.concatenate([weight, weight], axis=0).astype(jnp.float32)
+    block = jnp.kron(jnp.eye(group, dtype=jnp.float32), doubled)
+    width = group * outs
+    body = functools.partial(pair_kernel, rows=padded_rows, chans=chans, chunk=chunk, width=width)
+    result = pl.pallas_call(
+        body,
+        out_shape=jax.ShapeDtypeStruct((padded_rows, pairs * outs), jnp.bfloat16),
+    )(source[0::2], source[1::2], near, far, block)
+    return result[:rows, : cols * outs]
+
+
 def local(field, dw0, pw0, dw1, pw1, dw2, pw2, dw3, pw3, dw4, pw4, dwc, pwc):
     chans = dw0.shape[1]
     rows = field.shape[0]
@@ -116,7 +173,7 @@
     hidden = jnp.where(row_ok & col_ok, hidden, jnp.zeros_like(hidden))
     fine = hidden[margin:, margin * chans :]
     for taps, weight in ((dw1, pw1), (dw2, pw2), (dw3, pw3), (dw4, pw4)):
-        hidden = strided_flat(hidden, taps, weight)
+        hidden = strided_kernel(hidden, taps, weight)
     coarse_chans = dwc.shape[2]
     halo = 2 ** (LC - 1) - 1
     grid4 = hidden.reshape(hidden.shape[0], -1, coarse_chans)

time: 142 us -> 144 us (1.014)
  Pallas kernels: 0 us -> 9.89 us
  local copies, waits for them, and re-layouts: 40.9 us -> 32.8 us
  other arithmetic: 4.19 us -> 11.7 us
  matrix products: 7.61 us -> 1.64 us
    pallas_call x0 -> x4, Pallas kernels: none -> 9.89 us  [strided_kernel(): pl.pallas_call(body, out_shape=jax.ShapeDtypeStruct((padded_rows, pairs *...]
    convert_element_type x40 -> x0, local copies, waits for them, and re-layouts: 6.94 us -> none  [the longest x36 6.18 us: strided_flat(): total = total + piece.astype(jnp.float32) * tiled[3 * first + second]]
    another operation x0 -> x7, other arithmetic: none -> 4.83 us  [the longest x4 2.82 us: strided_kernel(): jnp.stack([jnp.tile(jnp.concatenate([taps[3 * a], taps[3 * a + 1]]), pair...]
    dot_general x4, matrix products: 5.07 us -> 0.89 us  [strided_cells(): mixed = jnp.dot(flat, weight, preferred_element_type=jnp.float32)]
    unnamed x75 -> x51, local copies, waits for them, and re-layouts: 3.73 us -> 0.45 us
    squeeze x0 -> x3, local copies, waits for them, and re-layouts: none -> 2.95 us  [strided_kernel(): taps[3 * a + 2]]
    reshape x21 -> x0, local copies, waits for them, and re-layouts: 2.91 us -> none  [the longest x12 1.47 us: strided_flat(): tail = slab[:, chans:].reshape(rows, cols, 2 * chans)]
    convert_element_type x12 -> x5, other arithmetic: 0.64 us -> 3.24 us  [the longest x4 3.24 us: strided_kernel(): doubled = jnp.concatenate([weight, weight], axis=0).astype(jnp.float32)]
  transfers between devices with their start and end apart: 6 -> 6, of which waited for: 3 -> 2; matrix products, arithmetic and copies ran while one was open for 7% -> 13% of each run, Pallas kernels for 0% -> 0%
where the time goes in v6:
time: 144 us; the launch traced here: 142 us
  blocking collectives  61.9 us (43%)
  local copies, waits for them, and re-layouts  32.8 us (23%)
  starting transfers between devices  17.5 us (12%)
  other arithmetic  11.7 us (8%)
  Pallas kernels  9.89 us (7%)
  waiting for transfers between devices  5.14 us (4%)
  between operations  1.77 us (1%)
  matrix products  1.64 us (1%)
    all_gather x1, blocking collectives, local(): hidden = lax.all_gather(hidden, 'gx', axis=0, tiled=True)  40.4 us
    all_gather x1, blocking collectives, local(): hidden = lax.all_gather(hidden, 'gy', axis=1, tiled=True)  21.5 us
    ppermute x6, starting transfers between devices, shifted(): lax.ppermute(value, axis, [(source, source + steps) for source in range(l...  17.5 us
    pallas_call x4, Pallas kernels, strided_kernel(): pl.pallas_call(body, out_shape=jax.ShapeDtypeStruct((padded_rows, pairs *...  9.89 us
    ppermute x6, waiting for transfers between devices, shifted(): lax.ppermute(value, axis, [(source, source + steps) for source in range(l...  5.14 us
    slice x4, local copies, waits for them, and re-layouts, strided_kernel(): source[0::2]  4.57 us
    slice x4, local copies, waits for them, and re-layouts, strided_kernel(): source[1::2]  3.69 us
    convert_element_type x4, other arithmetic, strided_kernel(): doubled = jnp.concatenate([weight, weight], axis=0).astype(jnp.float32)  3.24 us
  transfers between devices with their start and end apart: 6, of which 2 were waited for; matrix products, arithmetic and copies ran while one was open for 13% of the time, Pallas kernels for 0%

profile of v6, /device:TPU:6, one launch (start us, length us, event | category | flops | bytes accessed | tf_op | source)
XLA Modules:
  0.0 142.3 jit_solution(5682020808837073360)
XLA Ops:
  0.7 1.0 slice.588
  1.7 1.8 %collective-permute-start = (bf16[17,4096]{1,0:T(8,128)(2,1)S(1)}, bf16[17,4096]{1,0:T(8,128)(2,1)S(1)}, u32[]{:S(2)}, u32[]{:S(2)}) collective-permute-start(bf16[17,4096]{1,0:T(8,128)(2,1)S(1)} %slice.588), channel_id=1, source_target_pairs={{0,16},{16,32},{32,48},{48,64},{64,80},{80,96},{96,112},{112,128},... | collective-permute-start | bytes 417800 | tf_op jit(solution)/shard_map/ppermute | solution.py:16
  3.5 0.9 slice.589
  4.3 1.3 collective-permute-start.1
  5.6 1.0 slice_bitcast_fusion.35
  6.6 1.0 slice_bitcast_fusion.20
  8.4 0.8 maximum_convert_fusion.3
  9.2 1.0 slice_bitcast_fusion.11
  10.5 1.0 slice_bitcast_fusion.2
  11.8 0.7 maximum_convert_fusion.1.w_ref
  12.9 1.1 maximum_convert_fusion.w_ref
  14.2 0.7 pad_maximum_fusion.1.near_ref
  14.9 0.7 pad_maximum_fusion.2.far_ref
  15.5 0.7 pad_maximum_fusion.3.near_ref
  18.2 0.8 pad_maximum_fusion.7
  19.9 3.5 %collective-permute-start.2 = (bf16[51,544]{1,0:T(8,128)(2,1)S(1)}, bf16[51,544]{1,0:T(8,128)(2,1)S(1)}, u32[]{:S(2)}, u32[]{:S(2)}) collective-permute-start(bf16[51,544]{1,0:T(8,128)(2,1)S(1)} %slice.747), channel_id=1, source_target_pairs={{0,1},{1,2},{2,3},{3,4},{4,5},{5,6},{6,7},{7,8},{8,9},{9,10},{10,1... | collective-permute-start | bytes 166472 | tf_op jit(solution)/shard_map/ppermute | solution.py:16
  24.3 0.7 mul.622.w_ref
  25.0 4.5 %collective-permute-start.3 = (bf16[51,64]{1,0:T(8,128)(2,1)S(1)}, bf16[51,64]{1,0:T(8,128)(2,1)S(1)}, u32[]{:S(2)}, u32[]{:S(2)}) collective-permute-start(bf16[51,64]{1,0:T(8,128)(2,1)S(1)} %slice.751), channel_id=1, source_target_pairs={{1,0},{2,1},{3,2},{4,3},{5,4},{6,5},{7,6},{8,7},{9,8},{10,9},{11,1... | collective-permute-start | bytes 19592 | tf_op jit(solution)/shard_map/ppermute | solution.py:16
  29.8 1.1 collective-permute-done.3
  30.9 0.8 concatenate.128
  31.7 1.3 fusion.5
  33.0 1.6 %reshape.266 = bf16[6721,32]{1,0:T(8,128)(2,1)S(1)} reshape(bf16[47,4576]{1,0:T(8,128)(2,1)S(1)} %fusion.5) | data formatting | bytes 860288 | tf_op jit(solution)/shard_map/reshape | solution.py:38
  34.6 0.7 fusion.13
  35.3 2.6 %copy.28 = f32[6721,32]{1,0:T(8,128)} copy(f32[6721,32]{0,1:T(8,128)S(1)} %fusion.13) | data formatting | bytes 1720576 | tf_op jit(solution)/shard_map/mul | solution.py:33
  37.9 2.4 %reshape.267 = f32[47,4576]{1,0:T(8,128)S(1)} reshape(f32[6721,32]{1,0:T(8,128)} %copy.28) | data formatting | bytes 1720576 | tf_op jit(solution)/shard_map/reshape | solution.py:40
  40.7 1.5 %slice.620.even_ref = f32[25,4608]{1,0:T(8,128)} slice(f32[49,4608]{1,0:T(8,128)S(1)} %pad_convert_fusion), slice={[0:49:2], [0:4608:1]} | slice | bytes 921600 | tf_op jit(solution)/shard_map/slice | solution.py:138
  42.2 1.5 %slice.621.odd_ref = f32[24,4608]{1,0:T(8,128)} slice(f32[49,4608]{1,0:T(8,128)S(1)} %pad_convert_fusion), slice={[1:49:2], [0:4608:1]} | slice | bytes 884736 | tf_op jit(solution)/shard_map/slice | solution.py:138
  43.7 2.5 %shard_map.140 = bf16[24,4608]{1,0:T(8,128)(2,1)} custom-call(f32[25,4608]{1,0:T(8,128)} %slice.620.even_ref, f32[24,4608]{1,0:T(8,128)} %slice.621.odd_ref, f32[3,4608]{1,0:T(4,128)} %pad_maximum_fusion.1.near_ref, f32[3,4608]{1,0:T(4,128)} %pad_maximum_fusion.2.far_ref, f32[128,128]{1,0:T(8,128)} %mul.622.w_ref), custom_call_target="tpu_custom_call" | custom-call | tf_op jit(solution)/shard_map/pallas_call | solution.py:135
  46.3 1.0 pad_convert_fusion.1
  47.3 1.5 %slice.632.even_ref = f32[17,4608]{1,0:T(8,128)} slice(f32[33,4608]{1,0:T(8,128)S(1)} %pad_convert_fusion.1), slice={[0:33:2], [0:4608:1]} | slice | bytes 626688 | tf_op jit(solution)/shard_map/slice | solution.py:138
  48.7 0.8 slice.633.odd_ref
  49.5 2.2 %shard_map.141 = bf16[16,4608]{1,0:T(8,128)(2,1)} custom-call(f32[17,4608]{1,0:T(8,128)} %slice.632.even_ref, f32[16,4608]{1,0:T(8,128)} %slice.633.odd_ref, f32[3,4608]{1,0:T(4,128)} %pad_maximum_fusion.3.near_ref, f32[3,4608]{1,0:T(4,128)} %pad_maximum_fusion.4.far_ref, f32[128,128]{1,0:T(8,128)} %maximum_convert_fusion.2.w_ref), custom_call_target="tpu_custom_call" | custom-call | tf_op jit(solution)/shard_map/pallas_call | solution.py:135
  51.8 0.9 slice.760
  52.7 0.8 slice.644.even_ref
  53.5 0.7 slice.645.odd_ref
  54.2 2.2 %shard_map.142 = bf16[8,4608]{1,0:T(8,128)(2,1)} custom-call(f32[9,4608]{1,0:T(8,128)} %slice.644.even_ref, f32[8,4608]{1,0:T(8,128)} %slice.645.odd_ref, f32[3,4608]{1,0:T(4,128)} %pad_maximum_fusion.5.near_ref, f32[3,4608]{1,0:T(4,128)} %pad_maximum_fusion.6.far_ref, f32[256,256]{1,0:T(8,128)} %maximum_convert_fusion.1.w_ref), custom_call_target="tpu_custom_call" | custom-call | tf_op jit(solution)/shard_map/pallas_call | solution.py:135
  56.5 0.9 slice.761
  57.4 0.8 slice.656.even_ref
  58.2 0.7 slice.657.odd_ref
  59.0 2.8 %shard_map.143 = bf16[8,4608]{1,0:T(8,128)(2,1)} custom-call(f32[9,4608]{1,0:T(8,128)} %slice.656.even_ref, f32[8,4608]{1,0:T(8,128)} %slice.657.odd_ref, f32[3,4608]{1,0:T(4,128)} %get-tuple-element.91.near_ref, f32[3,4608]{1,0:T(4,128)} %get-tuple-element.92.far_ref, f32[512,512]{1,0:T(8,128)} %maximum_convert_fusion.w_ref), custom_call_target="tpu_custom_call" | custom-call | tf_op jit(solution)/shard_map/pallas_call | solution.py:135
  61.8 0.9 slice_reduce_fusion
  62.7 3.6 %collective-permute-start.4 = (bf16[1,8,512]{2,1,0:T(8,128)(2,1)S(1)}, bf16[1,8,512]{2,1,0:T(8,128)(2,1)S(1)}, u32[]{:S(2)}, u32[]{:S(2)}) collective-permute-start(bf16[1,8,512]{2,1,0:T(8,128)(2,1)S(1)} %slice.668), channel_id=1, source_target_pairs={{0,16},{16,32},{32,48},{48,64},{64,80},{80,96},{96,112},{112,128},... | collective-permute-start | bytes 24584 | tf_op jit(solution)/shard_map/ppermute | solution.py:16
  66.4 0.9 slice.763
  67.3 2.9 %collective-permute-start.5 = (bf16[3,7,512]{2,1,0:T(8,128)(2,1)S(1)}, bf16[3,7,512]{2,1,0:T(8,128)(2,1)S(1)}, u32[]{:S(2)}, u32[]{:S(2)}) collective-permute-start(bf16[3,7,512]{2,1,0:T(8,128)(2,1)S(1)} %slice.764), channel_id=1, source_target_pairs={{0,1},{1,2},{2,3},{3,4},{4,5},{5,6},{6,7},{7,8},{8,9},{9,10},{10,1... | collective-permute-start | bytes 64520 | tf_op jit(solution)/shard_map/ppermute | solution.py:16
  70.3 0.9 slice.758
  71.1 4.0 %collective-permute-done.5 = bf16[3,7,512]{2,1,0:T(8,128)(2,1)S(1)} collective-permute-done((bf16[3,7,512]{2,1,0:T(8,128)(2,1)S(1)}, bf16[3,7,512]{2,1,0:T(8,128)(2,1)S(1)}, u32[]{:S(2)}, u32[]{:S(2)}) %collective-permute-start.5) | collective-permute-done | bytes 21536 | tf_op jit(solution)/shard_map/ppermute | solution.py:16
  75.5 40.4 %all-gather.2 = bf16[32,7,512]{2,1,0:T(8,128)(2,1)S(1)} all-gather(bf16[1,7,512]{2,1,0:T(8,128)(2,1)S(1)} %fusion.72), channel_id=2, replica_groups=mesh['gx'=32,'gy'=16] {'gx'}, dimensions={0}, use_global_device_ids=true | all-gather | bytes 236544 | tf_op jit(solution)/shard_map/all_gather | solution.py:185
  118.4 21.5 %all-gather.1 = bf16[8,8192]{1,0:T(8,128)(2,1)S(1)} all-gather(bf16[8,512]{1,0:T(8,128)(2,1)S(1)} %fusion.84), channel_id=3, replica_groups=mesh['gx'=32,'gy'=16] {'gy'}, dimensions={1}, use_global_device_ids=true | all-gather | bytes 139264 | tf_op jit(solution)/shard_map/all_gather | solution.py:188
  (182 shorter events, 11.1 us)
Async XLA Ops:
  0.6 34.0 %copy-start = (bf16[32,32]{1,0:T(8,128)(2,1)S(1)}, bf16[32,32]{1,0:T(8,128)(2,1)}, u32[]{:S(2)}) copy-start(bf16[32,32]{1,0:T(8,128)(2,1)} %param.15) | copy-start | bytes 6148
  0.6 11.2 %copy-start.4 = (bf16[128,256]{1,0:T(8,128)(2,1)S(1)}, bf16[128,256]{1,0:T(8,128)(2,1)}, u32[]{:S(2)}) copy-start(bf16[128,256]{1,0:T(8,128)(2,1)} %param.21) | copy-start | bytes 196612
  0.7 11.9 %copy-start.6 = (f32[9,256]{1,0:T(8,128)S(1)}, f32[9,256]{1,0:T(8,128)}, u32[]{:S(2)}) copy-start(f32[9,256]{1,0:T(8,128)} %param.22) | copy-start | bytes 27652
  0.7 12.2 %copy-start.2 = (bf16[256,512]{1,0:T(8,128)(2,1)S(1)}, bf16[256,512]{1,0:T(8,128)(2,1)}, u32[]{:S(2)}) copy-start(bf16[256,512]{1,0:T(8,128)(2,1)} %param.23) | copy-start | bytes 786436
  1.7 17.9 %collective-permute-start = (bf16[17,4096]{1,0:T(8,128)(2,1)S(1)}, bf16[17,4096]{1,0:T(8,128)(2,1)S(1)}, u32[]{:S(2)}, u32[]{:S(2)}) collective-permute-start(bf16[17,4096]{1,0:T(8,128)(2,1)S(1)} %slice.588), channel_id=1, source_target_pairs={{0,16},{16,32},{32,48},{48,64},{64,80},{80,96},{96,112},{112,128},... | collective-permute-start | bytes 417800 | tf_op jit(solution)/shard_map/ppermute | solution.py:16
  4.3 15.3 %collective-permute-start.1 = (bf16[2,4096]{1,0:T(2,128)(2,1)S(1)}, bf16[2,4096]{1,0:T(2,128)(2,1)S(1)}, u32[]{:S(2)}, u32[]{:S(2)}) collective-permute-start(bf16[2,4096]{1,0:T(2,128)(2,1)S(1)} %slice.589), channel_id=1, source_target_pairs={{16,0},{32,16},{48,32},{64,48},{80,64},{96,80},{112,96},{128,112},... | collective-permute-start | bytes 49160 | tf_op jit(solution)/shard_map/ppermute | solution.py:16
  11.8 7.2 %copy-start.5 = (bf16[64,128]{1,0:T(8,128)(2,1)S(1)}, bf16[64,128]{1,0:T(8,128)(2,1)}, u32[]{:S(2)}) copy-start(bf16[64,128]{1,0:T(8,128)(2,1)} %param.19) | copy-start | bytes 49156
  12.6 7.1 %copy-start.1 = (bf16[32,4096]{1,0:T(8,128)(2,1)S(1)}, bf16[32,4096]{1,0:T(8,128)(2,1)}, u32[]{:S(2)}) copy-start(bf16[32,4096]{1,0:T(8,128)(2,1)} %param.13) | copy-start | bytes 786436
  19.9 9.6 %collective-permute-start.2 = (bf16[51,544]{1,0:T(8,128)(2,1)S(1)}, bf16[51,544]{1,0:T(8,128)(2,1)S(1)}, u32[]{:S(2)}, u32[]{:S(2)}) collective-permute-start(bf16[51,544]{1,0:T(8,128)(2,1)S(1)} %slice.747), channel_id=1, source_target_pairs={{0,1},{1,2},{2,3},{3,4},{4,5},{5,6},{6,7},{7,8},{8,9},{9,10},{10,1... | collective-permute-start | bytes 166472 | tf_op jit(solution)/shard_map/ppermute | solution.py:16
  25.0 5.9 %collective-permute-start.3 = (bf16[51,64]{1,0:T(8,128)(2,1)S(1)}, bf16[51,64]{1,0:T(8,128)(2,1)S(1)}, u32[]{:S(2)}, u32[]{:S(2)}) collective-permute-start(bf16[51,64]{1,0:T(8,128)(2,1)S(1)} %slice.751), channel_id=1, source_target_pairs={{1,0},{2,1},{3,2},{4,3},{5,4},{6,5},{7,6},{8,7},{9,8},{10,9},{11,1... | collective-permute-start | bytes 19592 | tf_op jit(solution)/shard_map/ppermute | solution.py:16
  56.5 9.8 %copy-start.3 = (f32[4,9,512]{2,0,1:T(4,128)S(1)}, f32[4,9,512]{2,0,1:T(4,128)}, u32[]{:S(2)}) copy-start(f32[4,9,512]{2,0,1:T(4,128)} %param.24) | copy-start | bytes 221188
  57.4 17.9 %copy-start.7 = (bf16[4,512,512]{2,1,0:T(8,128)(2,1)S(1)}, bf16[4,512,512]{2,1,0:T(8,128)(2,1)}, u32[]{:S(2)}) copy-start(bf16[4,512,512]{2,1,0:T(8,128)(2,1)} %param.25) | copy-start | bytes 6291460
  62.7 4.5 %collective-permute-start.4 = (bf16[1,8,512]{2,1,0:T(8,128)(2,1)S(1)}, bf16[1,8,512]{2,1,0:T(8,128)(2,1)S(1)}, u32[]{:S(2)}, u32[]{:S(2)}) collective-permute-start(bf16[1,8,512]{2,1,0:T(8,128)(2,1)S(1)} %slice.668), channel_id=1, source_target_pairs={{0,16},{16,32},{32,48},{48,64},{64,80},{80,96},{96,112},{112,128},... | collective-permute-start | bytes 24584 | tf_op jit(solution)/shard_map/ppermute | solution.py:16
  67.3 7.8 %collective-permute-start.5 = (bf16[3,7,512]{2,1,0:T(8,128)(2,1)S(1)}, bf16[3,7,512]{2,1,0:T(8,128)(2,1)S(1)}, u32[]{:S(2)}, u32[]{:S(2)}) collective-permute-start(bf16[3,7,512]{2,1,0:T(8,128)(2,1)S(1)} %slice.764), channel_id=1, source_target_pairs={{0,1},{1,2},{2,3},{3,4},{4,5},{5,6},{6,7},{7,8},{8,9},{9,10},{10,1... | collective-permute-start | bytes 64520 | tf_op jit(solution)/shard_map/ppermute | solution.py:16

commit v7 on v6

--- a/solution.py
+++ b/solution.py
@@ -88,22 +88,19 @@
 
 def pair_kernel(even_ref, odd_ref, near_ref, far_ref, w_ref, o_ref, *, rows, chans, chunk, width):
     lanes = even_ref.shape[1]
-    total = None
-    for first in range(3):
-        if first == 1:
-            slab = odd_ref[...]
-        else:
-            slab = even_ref[pl.ds(first // 2, rows), :]
-        ahead = pltpu.roll(slab, lanes - 2 * chans, 1)
-        term = slab * near_ref[first : first + 1, :] + ahead * far_ref[first : first + 1, :]
-        total = term if total is None else total + term
+    slabs = [even_ref[pl.ds(0, rows), :], odd_ref[...], even_ref[pl.ds(1, rows), :]]
+    aheads = [pltpu.roll(slab, lanes - 2 * chans, 1) for slab in slabs]
     weight = w_ref[...]
     for index in range(lanes // chunk):
-        part = jnp.dot(
-            total[:, index * chunk : (index + 1) * chunk],
-            weight,
-            preferred_element_type=jnp.float32,
-        )
+        window = slice(index * chunk, (index + 1) * chunk)
+        total = None
+        for first in range(3):
+            term = (
+                slabs[first][:, window] * near_ref[first : first + 1, :]
+                + aheads[first][:, window] * far_ref[first : first + 1, :]
+            )
+            total = term if total is None else total + term
+        part = jnp.dot(total.astype(jnp.bfloat16), weight, preferred_element_type=jnp.float32)
         o_ref[:, index * width : (index + 1) * width] = gelu_tanh(part).astype(o_ref.dtype)
 
 
@@ -121,15 +118,16 @@
         ext.astype(jnp.float32),
         ((0, 2 * padded_rows + 1 - ext.shape[0]), (0, lanes - ext.shape[1])),
     )
-    zero = jnp.zeros_like(taps[0])
-    near = jnp.stack(
-        [jnp.tile(jnp.concatenate([taps[3 * a], taps[3 * a + 1]]), pairs) for a in range(3)]
-    )
-    far = jnp.stack([jnp.tile(jnp.concatenate([taps[3 * a + 2], zero]), pairs) for a in range(3)])
     chunk = max(128, 2 * chans)
     group = chunk // (2 * chans)
-    doubled = jnp.concatenate([weight, weight], axis=0).astype(jnp.float32)
-    block = jnp.kron(jnp.eye(group, dtype=jnp.float32), doubled)
+    grouped = taps.reshape(3, 3, chans)
+    near = jnp.tile(grouped[:, :2].reshape(3, 2 * chans), (1, group))
+    far = jnp.tile(
+        jnp.concatenate([grouped[:, 2:], jnp.zeros_like(grouped[:, 2:])], axis=1).reshape(3, 2 * chans),
+        (1, group),
+    )
+    doubled = jnp.concatenate([weight, weight], axis=0)
+    block = jnp.kron(jnp.eye(group, dtype=weight.dtype), doubled) if group > 1 else doubled
     width = group * outs
     body = functools.partial(pair_kernel, rows=padded_rows, chans=chans, chunk=chunk, width=width)
     result = pl.pallas_call(

time: 144 us -> 143 us (level)
  other arithmetic: 11.7 us -> 8.94 us
  local copies, waits for them, and re-layouts: 32.8 us -> 34.8 us
    concatenate x9 -> x4, other arithmetic: 0.34 us -> 5.63 us  [strided_kernel(): doubled = jnp.concatenate([weight, weight], axis=0)]
    another operation x7 -> x0, other arithmetic: 4.83 us -> none  [the longest x4 2.82 us: strided_kernel(): jnp.stack([jnp.tile(jnp.concatenate([taps[3 * a], taps[3 * a + 1]]), pair...]
    convert_element_type x5 -> x1, other arithmetic: 3.24 us -> 0.01 us  [strided_kernel(): jnp.eye(group, dtype=weight.dtype)]
    squeeze x3 -> x0, local copies, waits for them, and re-layouts: 2.95 us -> none  [strided_kernel(): taps[3 * a + 2]]
    another operation x13 -> x9, local copies, waits for them, and re-layouts: 0.6 us -> 3.44 us  [the longest x5 2.02 us: strided_kernel(): jnp.tile(jnp.concatenate([grouped[:, 2:], jnp.zeros_like(grouped[:, 2:])]...]
    reshape x0 -> x4, local copies, waits for them, and re-layouts: none -> 1.45 us  [strided_kernel(): grouped = taps.reshape(3, 3, chans)]
  transfers between devices with their start and end apart: 6 -> 6, of which waited for: 2 -> 2; matrix products, arithmetic and copies ran while one was open for 13% -> 12% of each run, Pallas kernels for 0% -> 0%
where the time goes in v7:
time: 143 us; the launch traced here: 141 us
  blocking collectives  61.7 us (43%)
  local copies, waits for them, and re-layouts  34.8 us (24%)
  starting transfers between devices  17.5 us (12%)
  Pallas kernels  9.52 us (7%)
  other arithmetic  8.94 us (6%)
  waiting for transfers between devices  5.14 us (4%)
  matrix products  1.64 us (1%)
    all_gather x1, blocking collectives, local(): hidden = lax.all_gather(hidden, 'gx', axis=0, tiled=True)  40.2 us
    all_gather x1, blocking collectives, local(): hidden = lax.all_gather(hidden, 'gy', axis=1, tiled=True)  21.5 us
    ppermute x6, starting transfers between devices, shifted(): lax.ppermute(value, axis, [(source, source + steps) for source in range(l...  17.5 us
    pallas_call x4, Pallas kernels, strided_kernel(): pl.pallas_call(body, out_shape=jax.ShapeDtypeStruct((padded_rows, pairs *...  9.52 us
    concatenate x4, other arithmetic, strided_kernel(): doubled = jnp.concatenate([weight, weight], axis=0)  5.63 us
    ppermute x6, waiting for transfers between devices, shifted(): lax.ppermute(value, axis, [(source, source + steps) for source in range(l...  5.14 us
    slice x4, local copies, waits for them, and re-layouts, strided_kernel(): source[0::2]  4.59 us
    slice x4, local copies, waits for them, and re-layouts, strided_kernel(): source[1::2]  3.7 us
  transfers between devices with their start and end apart: 6, of which 2 were waited for; matrix products, arithmetic and copies ran while one was open for 12% of the time, Pallas kernels for 0%

profile of v7, /device:TPU:6, one launch (start us, length us, event | category | flops | bytes accessed | tf_op | source)
XLA Modules:
  0.0 140.6 jit_solution(16903876221473547405)
XLA Ops:
  0.7 1.0 slice.504
  1.7 1.8 %collective-permute-start = (bf16[17,4096]{1,0:T(8,128)(2,1)S(1)}, bf16[17,4096]{1,0:T(8,128)(2,1)S(1)}, u32[]{:S(2)}, u32[]{:S(2)}) collective-permute-start(bf16[17,4096]{1,0:T(8,128)(2,1)S(1)} %slice.504), channel_id=1, source_target_pairs={{0,16},{16,32},{32,48},{48,64},{64,80},{80,96},{96,112},{112,128},... | collective-permute-start | bytes 417800 | tf_op jit(solution)/shard_map/ppermute | solution.py:16
  3.5 0.9 slice.505
  4.3 1.3 collective-permute-start.1
  5.6 0.7 reshape.220
  6.3 0.7 reshape.221
  7.1 1.0 slice_bitcast_fusion.10
  8.1 0.8 pad_maximum_fusion.5
  8.9 1.4 pad_maximum_fusion.4.w_ref
  10.3 1.6 %pad_maximum_fusion.2.w_ref = bf16[256,256]{1,0:T(8,128)(2,1)} fusion(bf16[128,256]{1,0:T(8,128)(2,1)} %param.21), kind=kLoop, calls=%fused_computation.38 | loop fusion | flops 262144 | bytes 196608 | tf_op jit(solution)/shard_map/concatenate | solution.py:129
  11.8 1.9 %pad_maximum_fusion.w_ref = bf16[512,512]{1,0:T(8,128)(2,1)} fusion(bf16[256,512]{1,0:T(8,128)(2,1)} %param.23), kind=kLoop, calls=%fused_computation.19 | loop fusion | flops 1048576 | bytes 786432 | tf_op jit(solution)/shard_map/concatenate | solution.py:129
  14.7 3.5 %collective-permute-start.2 = (bf16[51,544]{1,0:T(8,128)(2,1)S(1)}, bf16[51,544]{1,0:T(8,128)(2,1)S(1)}, u32[]{:S(2)}, u32[]{:S(2)}) collective-permute-start(bf16[51,544]{1,0:T(8,128)(2,1)S(1)} %slice.635), channel_id=1, source_target_pairs={{0,1},{1,2},{2,3},{3,4},{4,5},{5,6},{6,7},{7,8},{8,9},{9,10},{10,1... | collective-permute-start | bytes 166472 | tf_op jit(solution)/shard_map/ppermute | solution.py:16
  19.3 0.7 tile.84.far_ref
  20.0 0.7 tile.81.near_ref
  20.7 0.7 mul.589.w_ref
  21.4 0.7 tile_reshape.21.far_ref
  22.1 0.7 tile_reshape.20.near_ref
  24.0 4.5 %collective-permute-start.3 = (bf16[51,64]{1,0:T(8,128)(2,1)S(1)}, bf16[51,64]{1,0:T(8,128)(2,1)S(1)}, u32[]{:S(2)}, u32[]{:S(2)}) collective-permute-start(bf16[51,64]{1,0:T(8,128)(2,1)S(1)} %slice.639), channel_id=1, source_target_pairs={{1,0},{2,1},{3,2},{4,3},{5,4},{6,5},{7,6},{8,7},{9,8},{10,9},{11,1... | collective-permute-start | bytes 19592 | tf_op jit(solution)/shard_map/ppermute | solution.py:16
  28.7 1.1 collective-permute-done.3
  29.8 0.8 concatenate.58
  30.6 1.3 fusion.5
  31.9 1.6 %reshape.216 = bf16[6721,32]{1,0:T(8,128)(2,1)S(1)} reshape(bf16[47,4576]{1,0:T(8,128)(2,1)S(1)} %fusion.5) | data formatting | bytes 860288 | tf_op jit(solution)/shard_map/reshape | solution.py:38
  33.5 0.7 fusion.13
  34.3 2.5 %copy.28 = f32[6721,32]{1,0:T(8,128)} copy(f32[6721,32]{0,1:T(8,128)S(1)} %fusion.13) | data formatting | bytes 1720576 | tf_op jit(solution)/shard_map/mul | solution.py:33
  36.8 2.4 %reshape.217 = f32[47,4576]{1,0:T(8,128)S(1)} reshape(f32[6721,32]{1,0:T(8,128)} %copy.28) | data formatting | bytes 1720576 | tf_op jit(solution)/shard_map/reshape | solution.py:40
  39.6 1.5 %slice.536.even_ref = f32[25,4608]{1,0:T(8,128)} slice(f32[49,4608]{1,0:T(8,128)S(1)} %pad_convert_fusion), slice={[0:49:2], [0:4608:1]} | slice | bytes 921600 | tf_op jit(solution)/shard_map/slice | solution.py:136
  41.1 1.5 %slice.537.odd_ref = f32[24,4608]{1,0:T(8,128)} slice(f32[49,4608]{1,0:T(8,128)S(1)} %pad_convert_fusion), slice={[1:49:2], [0:4608:1]} | slice | bytes 884736 | tf_op jit(solution)/shard_map/slice | solution.py:136
  42.6 2.5 %shard_map.140 = bf16[24,4608]{1,0:T(8,128)(2,1)} custom-call(f32[25,4608]{1,0:T(8,128)} %slice.536.even_ref, f32[24,4608]{1,0:T(8,128)} %slice.537.odd_ref, f32[3,128]{1,0:T(4,128)} %tile.81.near_ref, f32[3,128]{1,0:T(4,128)} %tile.84.far_ref, bf16[128,128]{1,0:T(8,128)(2,1)} %mul.589.w_ref), custom_call_target="tpu_custom_call" | custom-call | tf_op jit(solution)/shard_map/pallas_call | solution.py:133
  45.1 1.0 pad_convert_fusion.1
  46.1 1.5 %slice.541.even_ref = f32[17,4608]{1,0:T(8,128)} slice(f32[33,4608]{1,0:T(8,128)S(1)} %pad_convert_fusion.1), slice={[0:33:2], [0:4608:1]} | slice | bytes 626688 | tf_op jit(solution)/shard_map/slice | solution.py:136
  47.6 0.8 slice.542.odd_ref
  48.4 2.2 %shard_map.141 = bf16[16,4608]{1,0:T(8,128)(2,1)} custom-call(f32[17,4608]{1,0:T(8,128)} %slice.541.even_ref, f32[16,4608]{1,0:T(8,128)} %slice.542.odd_ref, f32[3,128]{1,0:T(4,128)} %tile_reshape.20.near_ref, f32[3,128]{1,0:T(4,128)} %tile_reshape.21.far_ref, bf16[128,128]{1,0:T(8,128)(2,1)} %pad_maximum_fusion.4.w_ref), custom_call_target="tpu_custom_call" | custom-call | tf_op jit(solution)/shard_map/pallas_call | solution.py:133
  50.6 0.9 slice.652
  51.6 0.8 slice.546.even_ref
  52.4 0.7 slice.547.odd_ref
  53.1 2.1 %shard_map.142 = bf16[8,4608]{1,0:T(8,128)(2,1)} custom-call(f32[9,4608]{1,0:T(8,128)} %slice.546.even_ref, f32[8,4608]{1,0:T(8,128)} %slice.547.odd_ref, f32[3,256]{1,0:T(4,128)} %get-tuple-element.48.near_ref, f32[3,256]{1,0:T(4,128)} %get-tuple-element.47.far_ref, bf16[256,256]{1,0:T(8,128)(2,1)} %pad_maximum_fusion.2.w_ref), custom_call_target="tpu_custom_call" | custom-call | tf_op jit(solution)/shard_map/pallas_call | solution.py:133
  55.2 0.9 slice.655
  56.1 0.8 slice.551.even_ref
  56.9 0.7 slice.552.odd_ref
  57.6 2.6 %shard_map.143 = bf16[8,4608]{1,0:T(8,128)(2,1)} custom-call(f32[9,4608]{1,0:T(8,128)} %slice.551.even_ref, f32[8,4608]{1,0:T(8,128)} %slice.552.odd_ref, f32[3,512]{1,0:T(4,128)} %bitcast.121, f32[3,512]{1,0:T(4,128)} %bitcast.120, bf16[512,512]{1,0:T(8,128)(2,1)} %pad_maximum_fusion.w_ref), custom_call_target="tpu_custom_call" | custom-call | tf_op jit(solution)/shard_map/pallas_call | solution.py:133
  60.3 0.9 slice_reduce_fusion
  61.2 3.6 %collective-permute-start.4 = (bf16[1,8,512]{2,1,0:T(8,128)(2,1)S(1)}, bf16[1,8,512]{2,1,0:T(8,128)(2,1)S(1)}, u32[]{:S(2)}, u32[]{:S(2)}) collective-permute-start(bf16[1,8,512]{2,1,0:T(8,128)(2,1)S(1)} %slice.556), channel_id=1, source_target_pairs={{0,16},{16,32},{32,48},{48,64},{64,80},{80,96},{96,112},{112,128},... | collective-permute-start | bytes 24584 | tf_op jit(solution)/shard_map/ppermute | solution.py:16
  64.8 0.9 slice.659
  65.7 2.9 %collective-permute-start.5 = (bf16[3,7,512]{2,1,0:T(8,128)(2,1)S(1)}, bf16[3,7,512]{2,1,0:T(8,128)(2,1)S(1)}, u32[]{:S(2)}, u32[]{:S(2)}) collective-permute-start(bf16[3,7,512]{2,1,0:T(8,128)(2,1)S(1)} %slice.660), channel_id=1, source_target_pairs={{0,1},{1,2},{2,3},{3,4},{4,5},{5,6},{6,7},{7,8},{8,9},{9,10},{10,1... | collective-permute-start | bytes 64520 | tf_op jit(solution)/shard_map/ppermute | solution.py:16
  68.7 0.9 slice.646
  69.6 4.0 %collective-permute-done.5 = bf16[3,7,512]{2,1,0:T(8,128)(2,1)S(1)} collective-permute-done((bf16[3,7,512]{2,1,0:T(8,128)(2,1)S(1)}, bf16[3,7,512]{2,1,0:T(8,128)(2,1)S(1)}, u32[]{:S(2)}, u32[]{:S(2)}) %collective-permute-start.5) | collective-permute-done | bytes 21536 | tf_op jit(solution)/shard_map/ppermute | solution.py:16
  74.0 40.2 %all-gather.2 = bf16[32,7,512]{2,1,0:T(8,128)(2,1)S(1)} all-gather(bf16[1,7,512]{2,1,0:T(8,128)(2,1)S(1)} %fusion.72), channel_id=2, replica_groups=mesh['gx'=32,'gy'=16] {'gx'}, dimensions={0}, use_global_device_ids=true | all-gather | bytes 236544 | tf_op jit(solution)/shard_map/all_gather | solution.py:183
  116.7 21.5 %all-gather.1 = bf16[8,8192]{1,0:T(8,128)(2,1)S(1)} all-gather(bf16[8,512]{1,0:T(8,128)(2,1)S(1)} %fusion.84), channel_id=3, replica_groups=mesh['gx'=32,'gy'=16] {'gy'}, dimensions={1}, use_global_device_ids=true | all-gather | bytes 139264 | tf_op jit(solution)/shard_map/all_gather | solution.py:186
  (126 shorter events, 9.1 us)
Async XLA Ops:
  0.6 32.9 %copy-start = (bf16[32,32]{1,0:T(8,128)(2,1)S(1)}, bf16[32,32]{1,0:T(8,128)(2,1)}, u32[]{:S(2)}) copy-start(bf16[32,32]{1,0:T(8,128)(2,1)} %param.15) | copy-start | bytes 6148
  0.6 13.8 %copy-start.1 = (bf16[32,4096]{1,0:T(8,128)(2,1)S(1)}, bf16[32,4096]{1,0:T(8,128)(2,1)}, u32[]{:S(2)}) copy-start(bf16[32,4096]{1,0:T(8,128)(2,1)} %param.13) | copy-start | bytes 786436
  0.7 17.5 %copy-start.3 = (f32[9,32]{1,0:T(8,128)S(1)}, f32[9,32]{1,0:T(8,128)}, u32[]{:S(2)}) copy-start(f32[9,32]{1,0:T(8,128)} %param.16) | copy-start | bytes 3460
  0.7 17.6 %copy-start.4 = (f32[9,64]{1,0:T(8,128)S(1)}, f32[9,64]{1,0:T(8,128)}, u32[]{:S(2)}) copy-start(f32[9,64]{1,0:T(8,128)} %param.18) | copy-start | bytes 6916
  1.7 12.8 %collective-permute-start = (bf16[17,4096]{1,0:T(8,128)(2,1)S(1)}, bf16[17,4096]{1,0:T(8,128)(2,1)S(1)}, u32[]{:S(2)}, u32[]{:S(2)}) collective-permute-start(bf16[17,4096]{1,0:T(8,128)(2,1)S(1)} %slice.504), channel_id=1, source_target_pairs={{0,16},{16,32},{32,48},{48,64},{64,80},{80,96},{96,112},{112,128},... | collective-permute-start | bytes 417800 | tf_op jit(solution)/shard_map/ppermute | solution.py:16
  4.3 10.1 %collective-permute-start.1 = (bf16[2,4096]{1,0:T(2,128)(2,1)S(1)}, bf16[2,4096]{1,0:T(2,128)(2,1)S(1)}, u32[]{:S(2)}, u32[]{:S(2)}) collective-permute-start(bf16[2,4096]{1,0:T(2,128)(2,1)S(1)} %slice.505), channel_id=1, source_target_pairs={{16,0},{32,16},{48,32},{64,48},{80,64},{96,80},{112,96},{128,112},... | collective-permute-start | bytes 49160 | tf_op jit(solution)/shard_map/ppermute | solution.py:16
  14.7 13.7 %collective-permute-start.2 = (bf16[51,544]{1,0:T(8,128)(2,1)S(1)}, bf16[51,544]{1,0:T(8,128)(2,1)S(1)}, u32[]{:S(2)}, u32[]{:S(2)}) collective-permute-start(bf16[51,544]{1,0:T(8,128)(2,1)S(1)} %slice.635), channel_id=1, source_target_pairs={{0,1},{1,2},{2,3},{3,4},{4,5},{5,6},{6,7},{7,8},{8,9},{9,10},{10,1... | collective-permute-start | bytes 166472 | tf_op jit(solution)/shard_map/ppermute | solution.py:16
  24.0 5.9 %collective-permute-start.3 = (bf16[51,64]{1,0:T(8,128)(2,1)S(1)}, bf16[51,64]{1,0:T(8,128)(2,1)S(1)}, u32[]{:S(2)}, u32[]{:S(2)}) collective-permute-start(bf16[51,64]{1,0:T(8,128)(2,1)S(1)} %slice.639), channel_id=1, source_target_pairs={{1,0},{2,1},{3,2},{4,3},{5,4},{6,5},{7,6},{8,7},{9,8},{10,9},{11,1... | collective-permute-start | bytes 19592 | tf_op jit(solution)/shard_map/ppermute | solution.py:16
  52.4 12.4 %copy-start.2 = (f32[4,9,512]{2,0,1:T(4,128)S(1)}, f32[4,9,512]{2,0,1:T(4,128)}, u32[]{:S(2)}) copy-start(f32[4,9,512]{2,0,1:T(4,128)} %param.24) | copy-start | bytes 221188
  56.1 17.7 %copy-start.5 = (bf16[4,512,512]{2,1,0:T(8,128)(2,1)S(1)}, bf16[4,512,512]{2,1,0:T(8,128)(2,1)}, u32[]{:S(2)}) copy-start(bf16[4,512,512]{2,1,0:T(8,128)(2,1)} %param.25) | copy-start | bytes 6291460
  61.2 4.5 %collective-permute-start.4 = (bf16[1,8,512]{2,1,0:T(8,128)(2,1)S(1)}, bf16[1,8,512]{2,1,0:T(8,128)(2,1)S(1)}, u32[]{:S(2)}, u32[]{:S(2)}) collective-permute-start(bf16[1,8,512]{2,1,0:T(8,128)(2,1)S(1)} %slice.556), channel_id=1, source_target_pairs={{0,16},{16,32},{32,48},{48,64},{64,80},{80,96},{96,112},{112,128},... | collective-permute-start | bytes 24584 | tf_op jit(solution)/shard_map/ppermute | solution.py:16
  65.7 7.8 %collective-permute-start.5 = (bf16[3,7,512]{2,1,0:T(8,128)(2,1)S(1)}, bf16[3,7,512]{2,1,0:T(8,128)(2,1)S(1)}, u32[]{:S(2)}, u32[]{:S(2)}) collective-permute-start(bf16[3,7,512]{2,1,0:T(8,128)(2,1)S(1)} %slice.660), channel_id=1, source_target_pairs={{0,1},{1,2},{2,3},{3,4},{4,5},{5,6},{6,7},{7,8},{8,9},{9,10},{10,1... | collective-permute-start | bytes 64520 | tf_op jit(solution)/shard_map/ppermute | solution.py:16

commit v8 on v7

--- a/solution.py
+++ b/solution.py
@@ -104,9 +104,23 @@
         o_ref[:, index * width : (index + 1) * width] = gelu_tanh(part).astype(o_ref.dtype)
 
 
-def strided_kernel(ext, taps, weight):
+def prepare(taps, weight):
     chans = taps.shape[1]
-    outs = weight.shape[1]
+    chunk = max(128, 2 * chans)
+    group = chunk // (2 * chans)
+    grouped = taps.reshape(3, 3, chans)
+    near = jnp.tile(grouped[:, :2].reshape(3, 2 * chans), (1, group))
+    far = jnp.tile(
+        jnp.concatenate([grouped[:, 2:], jnp.zeros_like(grouped[:, 2:])], axis=1).reshape(3, 2 * chans),
+        (1, group),
+    )
+    doubled = jnp.concatenate([weight, weight], axis=0)
+    block = jnp.kron(jnp.eye(group, dtype=weight.dtype), doubled) if group > 1 else doubled
+    return near, far, block
+
+
+def strided_kernel(ext, chans, outs, prepared):
+    near, far, block = prepared
     rows = (ext.shape[0] - 1) // 2
     cols = (ext.shape[1] // chans - 1) // 2
     pairs = cols + 1
@@ -120,14 +134,6 @@
     )
     chunk = max(128, 2 * chans)
     group = chunk // (2 * chans)
-    grouped = taps.reshape(3, 3, chans)
-    near = jnp.tile(grouped[:, :2].reshape(3, 2 * chans), (1, group))
-    far = jnp.tile(
-        jnp.concatenate([grouped[:, 2:], jnp.zeros_like(grouped[:, 2:])], axis=1).reshape(3, 2 * chans),
-        (1, group),
-    )
-    doubled = jnp.concatenate([weight, weight], axis=0)
-    block = jnp.kron(jnp.eye(group, dtype=weight.dtype), doubled) if group > 1 else doubled
     width = group * outs
     body = functools.partial(pair_kernel, rows=padded_rows, chans=chans, chunk=chunk, width=width)
     result = pl.pallas_call(
@@ -146,6 +152,8 @@
     upper = shifted(field[-margin - 2 :], "gx", 1)
     lower = shifted(field[:2], "gx", -1)
     stacked = jnp.concatenate([upper, field, lower], axis=0)
+    params = ((dw1, pw1), (dw2, pw2), (dw3, pw3), (dw4, pw4))
+    params, stacked = lax.optimization_barrier((params, stacked))
     leftside = shifted(stacked[:, -(margin + 2) * chans :], "gy", 1)
     rightside = shifted(stacked[:, : 2 * chans], "gy", -1)
     flat_pad = jnp.concatenate([leftside, stacked, rightside], axis=1)
@@ -170,8 +178,9 @@
     )
     hidden = jnp.where(row_ok & col_ok, hidden, jnp.zeros_like(hidden))
     fine = hidden[margin:, margin * chans :]
-    for taps, weight in ((dw1, pw1), (dw2, pw2), (dw3, pw3), (dw4, pw4)):
-        hidden = strided_kernel(hidden, taps, weight)
+    for taps, weight in params:
+        prepared = prepare(taps, weight)
+        hidden = strided_kernel(hidden, taps.shape[1], weight.shape[1], prepared)
     coarse_chans = dwc.shape[2]
     halo = 2 ** (LC - 1) - 1
     grid4 = hidden.reshape(hidden.shape[0], -1, coarse_chans)

time: 143 us -> 138 us (0.965)
  other arithmetic: 8.94 us -> 6.71 us
  blocking collectives: 61.7 us -> 59.7 us
  local copies, waits for them, and re-layouts: 34.8 us -> 33 us
  waiting for transfers between devices: 5.14 us -> 6.66 us
    concatenate x5 -> x4, other arithmetic: 5.9 us -> 2.16 us  [prepare(): doubled = jnp.concatenate([weight, weight], axis=0)]
    all_gather x1, blocking collectives: 40.2 us -> 38.2 us  [local(): hidden = lax.all_gather(hidden, 'gx', axis=0, tiled=True)]
    ppermute x6, waiting for transfers between devices: 5.14 us -> 6.66 us  [shifted(): lax.ppermute(value, axis, [(source, source + steps) for source in range(l...]
  transfers between devices with their start and end apart: 6 -> 6, of which waited for: 2 -> 2; matrix products, arithmetic and copies ran while one was open for 12% -> 9% of each run, Pallas kernels for 0% -> 0%
where the time goes in v8:
time: 138 us; the launch traced here: 136 us
  blocking collectives  59.7 us (43%)
  local copies, waits for them, and re-layouts  33 us (24%)
  starting transfers between devices  16.7 us (12%)
  Pallas kernels  9.65 us (7%)
  other arithmetic  6.71 us (5%)
  waiting for transfers between devices  6.66 us (5%)
  matrix products  2.54 us (2%)
  between operations  1.48 us (1%)
    all_gather x1, blocking collectives, local(): hidden = lax.all_gather(hidden, 'gx', axis=0, tiled=True)  38.2 us
    all_gather x1, blocking collectives, local(): hidden = lax.all_gather(hidden, 'gy', axis=1, tiled=True)  21.5 us
    ppermute x6, starting transfers between devices, shifted(): lax.ppermute(value, axis, [(source, source + steps) for source in range(l...  16.7 us
    pallas_call x4, Pallas kernels, strided_kernel(): pl.pallas_call(body, out_shape=jax.ShapeDtypeStruct((padded_rows, pairs *...  9.65 us
    ppermute x6, waiting for transfers between devices, shifted(): lax.ppermute(value, axis, [(source, source + steps) for source in range(l...  6.66 us
    slice x4, local copies, waits for them, and re-layouts, strided_kernel(): source[0::2]  4.54 us
    slice x4, local copies, waits for them, and re-layouts, strided_kernel(): source[1::2]  3.68 us
    slice x36, local copies, waits for them, and re-layouts, strided_cells(): piece = padded[first:first + 2 * rows:2, second:second + 2 * cols:2]  3.02 us
  transfers between devices with their start and end apart: 6, of which 2 were waited for; matrix products, arithmetic and copies ran while one was open for 9% of the time, Pallas kernels for 0%

profile of v8, /device:TPU:6, one launch (start us, length us, event | category | flops | bytes accessed | tf_op | source)
XLA Modules:
  0.0 136.5 jit_solution(11117024832038639792)
XLA Ops:
  0.7 1.1 slice.504
  1.8 1.8 %collective-permute-start = (bf16[17,4096]{1,0:T(8,128)(2,1)S(1)}, bf16[17,4096]{1,0:T(8,128)(2,1)S(1)}, u32[]{:S(2)}, u32[]{:S(2)}) collective-permute-start(bf16[17,4096]{1,0:T(8,128)(2,1)S(1)} %slice.504), channel_id=1, source_target_pairs={{0,16},{16,32},{32,48},{48,64},{64,80},{80,96},{96,112},{112,128},... | collective-permute-start | bytes 417800 | tf_op jit(solution)/shard_map/ppermute | solution.py:16
  3.6 0.9 slice.505
  4.4 1.3 collective-permute-start.1
  5.7 1.0 slice_bitcast_fusion.10
  7.7 1.5 %collective-permute-done.1 = bf16[2,4096]{1,0:T(2,128)(2,1)S(1)} collective-permute-done((bf16[2,4096]{1,0:T(2,128)(2,1)S(1)}, bf16[2,4096]{1,0:T(2,128)(2,1)S(1)}, u32[]{:S(2)}, u32[]{:S(2)}) %collective-permute-start.1) | collective-permute-done | bytes 16416 | tf_op jit(solution)/shard_map/ppermute | solution.py:16
  9.6 3.5 %collective-permute-start.2 = (bf16[51,544]{1,0:T(8,128)(2,1)S(1)}, bf16[51,544]{1,0:T(8,128)(2,1)S(1)}, u32[]{:S(2)}, u32[]{:S(2)}) collective-permute-start(bf16[51,544]{1,0:T(8,128)(2,1)S(1)} %slice.506), channel_id=1, source_target_pairs={{0,1},{1,2},{2,3},{3,4},{4,5},{5,6},{6,7},{7,8},{8,9},{9,10},{10,1... | collective-permute-start | bytes 166472 | tf_op jit(solution)/shard_map/ppermute | solution.py:16
  13.0 4.5 %collective-permute-start.3 = (bf16[51,64]{1,0:T(8,128)(2,1)S(1)}, bf16[51,64]{1,0:T(8,128)(2,1)S(1)}, u32[]{:S(2)}, u32[]{:S(2)}) collective-permute-start(bf16[51,64]{1,0:T(8,128)(2,1)S(1)} %slice.514), channel_id=1, source_target_pairs={{1,0},{2,1},{3,2},{4,3},{5,4},{6,5},{7,6},{8,7},{9,8},{10,9},{11,1... | collective-permute-start | bytes 19592 | tf_op jit(solution)/shard_map/ppermute | solution.py:16
  17.6 0.6 pad_maximum_fusion.5.w_ref
  18.2 0.7 pad_maximum_fusion.3.w_ref
  18.8 0.9 pad_maximum_fusion.w_ref
  20.6 0.7 tile.84.far_ref
  21.4 0.6 tile.81.near_ref
  22.0 0.7 mul.589.w_ref
  22.7 0.7 tile_reshape.21.far_ref
  23.4 0.7 tile_reshape.20.near_ref
  24.1 0.6 copy.52
  25.3 0.8 concatenate.58
  26.1 1.5 %fusion.5 = bf16[47,4576]{1,0:T(8,128)(2,1)S(1)} fusion(bf16[51,544]{1,0:T(8,128)(2,1)S(1)} %collective-permute-done.2, bf16[51,4704]{1,0:T(8,128)(2,1)S(1)} %concatenate.58, bf16[51,4096]{1,0:T(8,128)(2,1)S(1)} %pad_maximum_fusion.1, f32[4576]{0:T(1024)S(1)} %tile.78, f32[4576]{0:T(1024)S(1)} %tile.76, f32[4576]{0:T(1024)S(1)} %tile.74, f32[4576]{0:T(1024)S(1)} %tile.72, ...), kind=kLoop, calls=%fused_computation.13 | loop fusion | flops 9678240 | bytes 2358592 | tf_op jit(solution)/shard_map/convert_element_type | solution.py:38
  27.6 1.6 %reshape.216 = bf16[6721,32]{1,0:T(8,128)(2,1)S(1)} reshape(bf16[47,4576]{1,0:T(8,128)(2,1)S(1)} %fusion.5) | data formatting | bytes 860288 | tf_op jit(solution)/shard_map/reshape | solution.py:38
  29.2 1.7 %fusion.13 = f32[6721,32]{0,1:T(8,128)} fusion(bf16[6721,32]{1,0:T(8,128)(2,1)S(1)} %reshape.216, bf16[32,32]{1,0:T(8,128)(2,1)S(1)} %copy-done), kind=kOutput, calls=%fused_computation.22 | convolution fusion | flops 15485184 | bytes 1292480 | tf_op jit(solution)/shard_map/dot_general | solution.py:39
  30.9 2.7 %copy.28 = f32[6721,32]{1,0:T(8,128)S(1)} copy(f32[6721,32]{0,1:T(8,128)} %fusion.13) | data formatting | bytes 1720576 | tf_op jit(solution)/shard_map/mul | solution.py:33
  33.6 1.7 %reshape.217 = f32[47,4576]{1,0:T(8,128)} reshape(f32[6721,32]{1,0:T(8,128)S(1)} %copy.28) | data formatting | bytes 1720576 | tf_op jit(solution)/shard_map/reshape | solution.py:40
  35.3 1.6 %and_select_fusion = bf16[47,4576]{1,0:T(8,128)(2,1)S(1)} fusion(f32[47,4576]{1,0:T(8,128)} %reshape.217, pred[4576]{0:T(1024)(128)(4,1)S(1)} %fusion.64, pred[47]{0:T(512)(128)(4,1)S(1)} %compare_or_fusion, bf16[51,4096]{1,0:T(8,128)(2,1)} %copy-done.1, bf16[51,544]{1,0:T(8,128)(2,1)S(1)} %collective-permute-done.2), kind=kLoop, calls=%fused_computation.15 | loop fusion | flops 1720576 | bytes 1768335 | tf_op jit(solution)/shard_map/jit(_where)/select_n | solution.py:179
  37.0 1.5 %slice.536.even_ref = f32[25,4608]{1,0:T(8,128)} slice(f32[49,4608]{1,0:T(8,128)S(1)} %pad_convert_fusion), slice={[0:49:2], [0:4608:1]} | slice | bytes 921600 | tf_op jit(solution)/shard_map/slice | solution.py:142
  38.5 1.5 %slice.537.odd_ref = f32[24,4608]{1,0:T(8,128)} slice(f32[49,4608]{1,0:T(8,128)S(1)} %pad_convert_fusion), slice={[1:49:2], [0:4608:1]} | slice | bytes 884736 | tf_op jit(solution)/shard_map/slice | solution.py:142
  40.0 2.5 %shard_map.140 = bf16[24,4608]{1,0:T(8,128)(2,1)} custom-call(f32[25,4608]{1,0:T(8,128)} %slice.536.even_ref, f32[24,4608]{1,0:T(8,128)} %slice.537.odd_ref, f32[3,128]{1,0:T(4,128)} %tile.81.near_ref, f32[3,128]{1,0:T(4,128)} %tile.84.far_ref, bf16[128,128]{1,0:T(8,128)(2,1)} %mul.589.w_ref), custom_call_target="tpu_custom_call" | custom-call | tf_op jit(solution)/shard_map/pallas_call | solution.py:139
  42.5 1.0 pad_convert_fusion.1
  43.5 1.5 %slice.541.even_ref = f32[17,4608]{1,0:T(8,128)} slice(f32[33,4608]{1,0:T(8,128)S(1)} %pad_convert_fusion.1), slice={[0:33:2], [0:4608:1]} | slice | bytes 626688 | tf_op jit(solution)/shard_map/slice | solution.py:142
  45.0 0.8 slice.542.odd_ref
  45.8 2.2 %shard_map.141 = bf16[16,4608]{1,0:T(8,128)(2,1)} custom-call(f32[17,4608]{1,0:T(8,128)} %slice.541.even_ref, f32[16,4608]{1,0:T(8,128)} %slice.542.odd_ref, f32[3,128]{1,0:T(4,128)} %tile_reshape.20.near_ref, f32[3,128]{1,0:T(4,128)} %tile_reshape.21.far_ref, bf16[128,128]{1,0:T(8,128)(2,1)} %pad_maximum_fusion.5.w_ref), custom_call_target="tpu_custom_call" | custom-call | tf_op jit(solution)/shard_map/pallas_call | solution.py:139
  48.0 0.9 slice.654
  49.0 0.8 slice.546.even_ref
  49.7 0.7 slice.547.odd_ref
  50.4 2.3 %shard_map.142 = bf16[8,4608]{1,0:T(8,128)(2,1)} custom-call(f32[9,4608]{1,0:T(8,128)} %slice.546.even_ref, f32[8,4608]{1,0:T(8,128)} %slice.547.odd_ref, f32[3,256]{1,0:T(4,128)} %get-tuple-element.66.near_ref, f32[3,256]{1,0:T(4,128)} %get-tuple-element.65.far_ref, bf16[256,256]{1,0:T(8,128)(2,1)} %pad_maximum_fusion.3.w_ref), custom_call_target="tpu_custom_call" | custom-call | tf_op jit(solution)/shard_map/pallas_call | solution.py:139
  52.7 0.9 slice.657
  53.7 0.8 slice.551.even_ref
  54.4 0.7 slice.552.odd_ref
  55.1 2.6 %shard_map.143 = bf16[8,4608]{1,0:T(8,128)(2,1)} custom-call(f32[9,4608]{1,0:T(8,128)} %slice.551.even_ref, f32[8,4608]{1,0:T(8,128)} %slice.552.odd_ref, f32[3,512]{1,0:T(4,128)} %bitcast.121, f32[3,512]{1,0:T(4,128)} %bitcast.120, bf16[512,512]{1,0:T(8,128)(2,1)} %pad_maximum_fusion.w_ref), custom_call_target="tpu_custom_call" | custom-call | tf_op jit(solution)/shard_map/pallas_call | solution.py:139
  57.8 0.9 slice_reduce_fusion
  58.7 3.8 %collective-permute-start.4 = (bf16[1,8,512]{2,1,0:T(8,128)(2,1)S(1)}, bf16[1,8,512]{2,1,0:T(8,128)(2,1)S(1)}, u32[]{:S(2)}, u32[]{:S(2)}) collective-permute-start(bf16[1,8,512]{2,1,0:T(8,128)(2,1)S(1)} %slice.556), channel_id=1, source_target_pairs={{0,16},{16,32},{32,48},{48,64},{64,80},{80,96},{96,112},{112,128},... | collective-permute-start | bytes 24584 | tf_op jit(solution)/shard_map/ppermute | solution.py:16
  62.6 0.9 slice.661
  63.5 1.9 %collective-permute-start.5 = (bf16[3,7,512]{2,1,0:T(8,128)(2,1)S(1)}, bf16[3,7,512]{2,1,0:T(8,128)(2,1)S(1)}, u32[]{:S(2)}, u32[]{:S(2)}) collective-permute-start(bf16[3,7,512]{2,1,0:T(8,128)(2,1)S(1)} %slice.662), channel_id=1, source_target_pairs={{0,1},{1,2},{2,3},{3,4},{4,5},{5,6},{6,7},{7,8},{8,9},{9,10},{10,1... | collective-permute-start | bytes 64520 | tf_op jit(solution)/shard_map/ppermute | solution.py:16
  65.4 0.9 slice.648
  66.3 5.1 %collective-permute-done.5 = bf16[3,7,512]{2,1,0:T(8,128)(2,1)S(1)} collective-permute-done((bf16[3,7,512]{2,1,0:T(8,128)(2,1)S(1)}, bf16[3,7,512]{2,1,0:T(8,128)(2,1)S(1)}, u32[]{:S(2)}, u32[]{:S(2)}) %collective-permute-start.5) | collective-permute-done | bytes 21536 | tf_op jit(solution)/shard_map/ppermute | solution.py:16
  71.8 38.2 %all-gather.2 = bf16[32,7,512]{2,1,0:T(8,128)(2,1)S(1)} all-gather(bf16[1,7,512]{2,1,0:T(8,128)(2,1)S(1)} %fusion.77), channel_id=2, replica_groups=mesh['gx'=32,'gy'=16] {'gx'}, dimensions={0}, use_global_device_ids=true | all-gather | bytes 236544 | tf_op jit(solution)/shard_map/all_gather | solution.py:192
  112.5 21.5 %all-gather.1 = bf16[8,8192]{1,0:T(8,128)(2,1)S(1)} all-gather(bf16[8,512]{1,0:T(8,128)(2,1)S(1)} %fusion.89), channel_id=3, replica_groups=mesh['gx'=32,'gy'=16] {'gy'}, dimensions={1}, use_global_device_ids=true | all-gather | bytes 139264 | tf_op jit(solution)/shard_map/all_gather | solution.py:195
  135.8 0.6 reshape_reshape.3
  (139 shorter events, 7.3 us)
Async XLA Ops:
  0.6 28.6 %copy-start = (bf16[32,32]{1,0:T(8,128)(2,1)S(1)}, bf16[32,32]{1,0:T(8,128)(2,1)}, u32[]{:S(2)}) copy-start(bf16[32,32]{1,0:T(8,128)(2,1)} %param.15) | copy-start | bytes 6148
  0.6 8.6 %copy-start.2 = (bf16[32,4096]{1,0:T(8,128)(2,1)S(1)}, bf16[32,4096]{1,0:T(8,128)(2,1)}, u32[]{:S(2)}) copy-start(bf16[32,4096]{1,0:T(8,128)(2,1)} %param.13) | copy-start | bytes 786436
  0.7 19.8 %copy-start.10 = (f32[9,32]{1,0:T(8,128)S(1)}, f32[9,32]{1,0:T(8,128)}, u32[]{:S(2)}) copy-start(f32[9,32]{1,0:T(8,128)} %param.16) | copy-start | bytes 3460
  0.7 16.9 %copy-start.8 = (bf16[32,64]{1,0:T(8,128)(2,1)S(1)}, bf16[32,64]{1,0:T(8,128)(2,1)}, u32[]{:S(2)}) copy-start(bf16[32,64]{1,0:T(8,128)(2,1)} %param.17) | copy-start | bytes 12292
  0.7 19.8 %copy-start.11 = (f32[9,64]{1,0:T(8,128)S(1)}, f32[9,64]{1,0:T(8,128)}, u32[]{:S(2)}) copy-start(f32[9,64]{1,0:T(8,128)} %param.18) | copy-start | bytes 6916
  0.7 16.9 %copy-start.6 = (bf16[64,128]{1,0:T(8,128)(2,1)S(1)}, bf16[64,128]{1,0:T(8,128)(2,1)}, u32[]{:S(2)}) copy-start(bf16[64,128]{1,0:T(8,128)(2,1)} %param.19) | copy-start | bytes 49156
  0.7 8.8 %copy-start.9 = (f32[9,128]{1,0:T(8,128)S(1)}, f32[9,128]{1,0:T(8,128)}, u32[]{:S(2)}) copy-start(f32[9,128]{1,0:T(8,128)} %param.20) | copy-start | bytes 13828
  0.7 17.5 %copy-start.5 = (bf16[128,256]{1,0:T(8,128)(2,1)S(1)}, bf16[128,256]{1,0:T(8,128)(2,1)}, u32[]{:S(2)}) copy-start(bf16[128,256]{1,0:T(8,128)(2,1)} %param.21) | copy-start | bytes 196612
  0.7 8.8 %copy-start.7 = (f32[9,256]{1,0:T(8,128)S(1)}, f32[9,256]{1,0:T(8,128)}, u32[]{:S(2)}) copy-start(f32[9,256]{1,0:T(8,128)} %param.22) | copy-start | bytes 27652
  0.7 18.1 %copy-start.3 = (bf16[256,512]{1,0:T(8,128)(2,1)S(1)}, bf16[256,512]{1,0:T(8,128)(2,1)}, u32[]{:S(2)}) copy-start(bf16[256,512]{1,0:T(8,128)(2,1)} %param.23) | copy-start | bytes 786436
  1.8 7.4 %collective-permute-start = (bf16[17,4096]{1,0:T(8,128)(2,1)S(1)}, bf16[17,4096]{1,0:T(8,128)(2,1)S(1)}, u32[]{:S(2)}, u32[]{:S(2)}) collective-permute-start(bf16[17,4096]{1,0:T(8,128)(2,1)S(1)} %slice.504), channel_id=1, source_target_pairs={{0,16},{16,32},{32,48},{48,64},{64,80},{80,96},{96,112},{112,128},... | collective-permute-start | bytes 417800 | tf_op jit(solution)/shard_map/ppermute | solution.py:16
  4.4 4.8 %collective-permute-start.1 = (bf16[2,4096]{1,0:T(2,128)(2,1)S(1)}, bf16[2,4096]{1,0:T(2,128)(2,1)S(1)}, u32[]{:S(2)}, u32[]{:S(2)}) collective-permute-start(bf16[2,4096]{1,0:T(2,128)(2,1)S(1)} %slice.505), channel_id=1, source_target_pairs={{16,0},{32,16},{48,32},{64,48},{80,64},{96,80},{112,96},{128,112},... | collective-permute-start | bytes 49160 | tf_op jit(solution)/shard_map/ppermute | solution.py:16
  9.3 18.2 %copy-start.1 = (bf16[51,4096]{1,0:T(8,128)(2,1)}, bf16[51,4096]{1,0:T(8,128)(2,1)S(1)}, u32[]{:S(2)}) copy-start(bf16[51,4096]{1,0:T(8,128)(2,1)S(1)} %pad_maximum_fusion.1) | copy-start | bytes 1253380
  9.6 15.7 %collective-permute-start.2 = (bf16[51,544]{1,0:T(8,128)(2,1)S(1)}, bf16[51,544]{1,0:T(8,128)(2,1)S(1)}, u32[]{:S(2)}, u32[]{:S(2)}) collective-permute-start(bf16[51,544]{1,0:T(8,128)(2,1)S(1)} %slice.506), channel_id=1, source_target_pairs={{0,1},{1,2},{2,3},{3,4},{4,5},{5,6},{6,7},{7,8},{8,9},{9,10},{10,1... | collective-permute-start | bytes 166472 | tf_op jit(solution)/shard_map/ppermute | solution.py:16
  13.0 12.2 %collective-permute-start.3 = (bf16[51,64]{1,0:T(8,128)(2,1)S(1)}, bf16[51,64]{1,0:T(8,128)(2,1)S(1)}, u32[]{:S(2)}, u32[]{:S(2)}) collective-permute-start(bf16[51,64]{1,0:T(8,128)(2,1)S(1)} %slice.514), channel_id=1, source_target_pairs={{1,0},{2,1},{3,2},{4,3},{5,4},{6,5},{7,6},{8,7},{9,8},{10,9},{11,1... | collective-permute-start | bytes 19592 | tf_op jit(solution)/shard_map/ppermute | solution.py:16
  49.0 13.6 %copy-start.4 = (f32[4,9,512]{2,0,1:T(4,128)S(1)}, f32[4,9,512]{2,0,1:T(4,128)}, u32[]{:S(2)}) copy-start(f32[4,9,512]{2,0,1:T(4,128)} %param.24) | copy-start | bytes 221188
  50.4 21.2 %copy-start.12 = (bf16[4,512,512]{2,1,0:T(8,128)(2,1)S(1)}, bf16[4,512,512]{2,1,0:T(8,128)(2,1)}, u32[]{:S(2)}) copy-start(bf16[4,512,512]{2,1,0:T(8,128)(2,1)} %param.25) | copy-start | bytes 6291460
  58.7 4.7 %collective-permute-start.4 = (bf16[1,8,512]{2,1,0:T(8,128)(2,1)S(1)}, bf16[1,8,512]{2,1,0:T(8,128)(2,1)S(1)}, u32[]{:S(2)}, u32[]{:S(2)}) collective-permute-start(bf16[1,8,512]{2,1,0:T(8,128)(2,1)S(1)} %slice.556), channel_id=1, source_target_pairs={{0,16},{16,32},{32,48},{48,64},{64,80},{80,96},{96,112},{112,128},... | collective-permute-start | bytes 24584 | tf_op jit(solution)/shard_map/ppermute | solution.py:16
  63.5 7.9 %collective-permute-start.5 = (bf16[3,7,512]{2,1,0:T(8,128)(2,1)S(1)}, bf16[3,7,512]{2,1,0:T(8,128)(2,1)S(1)}, u32[]{:S(2)}, u32[]{:S(2)}) collective-permute-start(bf16[3,7,512]{2,1,0:T(8,128)(2,1)S(1)} %slice.662), channel_id=1, source_target_pairs={{0,1},{1,2},{2,3},{3,4},{4,5},{5,6},{6,7},{7,8},{8,9},{9,10},{10,1... | collective-permute-start | bytes 64520 | tf_op jit(solution)/shard_map/ppermute | solution.py:16

commit v9 on v2

--- a/solution.py
+++ b/solution.py
@@ -1,6 +1,10 @@
+import functools
+
 import jax
 import jax.numpy as jnp
 from jax import lax
+from jax.experimental import pallas as pl
+from jax.experimental.pallas import tpu as pltpu
 from jax.sharding import PartitionSpec as P
 
 LC = 4
@@ -82,6 +86,79 @@
     return point_flat(total, weight, rows, cols).astype(jnp.bfloat16)
 
 
+def prepare(taps, weight):
+    chans = taps.shape[1]
+    chunk = max(128, 2 * chans)
+    group = chunk // (2 * chans)
+    grouped = taps.reshape(3, 3, chans)
+    near = jnp.tile(grouped[:, :2].reshape(3, 2 * chans), (1, group))
+    far = jnp.tile(
+        jnp.concatenate([grouped[:, 2:], jnp.zeros_like(grouped[:, 2:])], axis=1).reshape(3, 2 * chans),
+        (1, group),
+    )
+    doubled = jnp.concatenate([weight, weight], axis=0)
+    block = jnp.kron(jnp.eye(group, dtype=weight.dtype), doubled) if group > 1 else doubled
+    return near, far, block
+
+
+def chain_kernel(*refs, plan):
+    x_ref = refs[0]
+    o_ref = refs[-1]
+    value = x_ref[...].astype(jnp.float32)
+    lanes = value.shape[1]
+    for level, (valid, rows, chans, outs) in enumerate(plan):
+        near_ref, far_ref, w_ref = refs[1 + 3 * level : 4 + 3 * level]
+        shape = (rows, value.shape[0])
+        out_row = lax.broadcasted_iota(jnp.int32, shape, 0)
+        in_row = lax.broadcasted_iota(jnp.int32, shape, 1)
+        slabs = []
+        for first in range(3):
+            pick = ((in_row == 2 * out_row + first) & (in_row < valid)).astype(jnp.float32)
+            slabs.append(jnp.dot(pick, value, preferred_element_type=jnp.float32))
+        aheads = [pltpu.roll(slab, lanes - 2 * chans, 1) for slab in slabs]
+        weight = w_ref[...]
+        chunk = max(128, 2 * chans)
+        width = weight.shape[1]
+        parts = []
+        for index in range(lanes // chunk):
+            window = slice(index * chunk, (index + 1) * chunk)
+            total = None
+            for first in range(3):
+                term = (
+                    slabs[first][:, window] * near_ref[first : first + 1, :]
+                    + aheads[first][:, window] * far_ref[first : first + 1, :]
+                )
+                total = term if total is None else total + term
+            part = jnp.dot(total.astype(jnp.bfloat16), weight, preferred_element_type=jnp.float32)
+            parts.append(gelu_tanh(part).astype(jnp.bfloat16))
+        value = jnp.concatenate(parts, axis=1).astype(jnp.float32)
+    o_ref[...] = value.astype(o_ref.dtype)
+
+
+def strided_chain(ext, chans, params):
+    rows = ext.shape[0]
+    cols = ext.shape[1] // chans
+    plan = []
+    operands = []
+    lanes = None
+    for taps, weight in params:
+        out_rows = (rows - 1) // 2
+        out_cols = (cols - 1) // 2
+        pairs = out_cols + 1
+        if pairs * 2 * chans % 128:
+            pairs += 1
+        lanes = lanes or pairs * 2 * chans
+        plan.append((rows, -(-out_rows // 8) * 8, chans, weight.shape[1]))
+        operands.extend(prepare(taps, weight))
+        rows, cols, chans = out_rows, out_cols, weight.shape[1]
+    source = jnp.pad(ext, ((0, -ext.shape[0] % 8), (0, lanes - ext.shape[1])))
+    result = pl.pallas_call(
+        functools.partial(chain_kernel, plan=tuple(plan)),
+        out_shape=jax.ShapeDtypeStruct((plan[-1][1], lanes), jnp.bfloat16),
+    )(source, *operands)
+    return result[:rows, : cols * chans]
+
+
 def local(field, dw0, pw0, dw1, pw1, dw2, pw2, dw3, pw3, dw4, pw4, dwc, pwc):
     chans = dw0.shape[1]
     rows = field.shape[0]
@@ -91,6 +168,8 @@
     upper = shifted(field[-margin - 2 :], "gx", 1)
     lower = shifted(field[:2], "gx", -1)
     stacked = jnp.concatenate([upper, field, lower], axis=0)
+    params = ((dw1, pw1), (dw2, pw2), (dw3, pw3), (dw4, pw4))
+    params, stacked = lax.optimization_barrier((params, stacked))
     leftside = shifted(stacked[:, -(margin + 2) * chans :], "gy", 1)
     rightside = shifted(stacked[:, : 2 * chans], "gy", -1)
     flat_pad = jnp.concatenate([leftside, stacked, rightside], axis=1)
@@ -115,8 +194,7 @@
     )
     hidden = jnp.where(row_ok & col_ok, hidden, jnp.zeros_like(hidden))
     fine = hidden[margin:, margin * chans :]
-    for taps, weight in ((dw1, pw1), (dw2, pw2), (dw3, pw3), (dw4, pw4)):
-        hidden = strided_flat(hidden, taps, weight)
+    hidden = strided_chain(hidden, chans, params)
     coarse_chans = dwc.shape[2]
     halo = 2 ** (LC - 1) - 1
     grid4 = hidden.reshape(hidden.shape[0], -1, coarse_chans)

time: 142 us -> 123 us (0.87)
  local copies, waits for them, and re-layouts: 40.9 us -> 23.8 us
  matrix products: 7.61 us -> 2.54 us
  Pallas kernels: 0 us -> 4.76 us
  blocking collectives: 61.8 us -> 59.6 us
  other arithmetic: 4.19 us -> 5.64 us
    slice x34 -> x8, local copies, waits for them, and re-layouts: 11.3 us -> 0.89 us  [the longest x1 0.85 us: strided_chain(): return result[:rows, :cols * chans]]
    convert_element_type x40 -> x0, local copies, waits for them, and re-layouts: 6.94 us -> none  [the longest x36 6.18 us: strided_flat(): total = total + piece.astype(jnp.float32) * tiled[3 * first + second]]
    pallas_call x0 -> x1, Pallas kernels: none -> 4.76 us  [strided_chain(): pl.pallas_call(functools.partial(chain_kernel, plan=tuple(plan)), out_sha...]
    dot_general x4, matrix products: 5.07 us -> 0.89 us  [strided_cells(): mixed = jnp.dot(flat, weight, preferred_element_type=jnp.float32)]
    another operation x0 -> x9, local copies, waits for them, and re-layouts: none -> 3.46 us  [the longest x5 2.03 us: prepare(): jnp.tile(jnp.concatenate([grouped[:, 2:], jnp.zeros_like(grouped[:, 2:])]...]
    reshape x21 -> x4, local copies, waits for them, and re-layouts: 2.91 us -> 0.04 us  [prepare(): grouped = taps.reshape(3, 3, chans)]
    unnamed x75 -> x33, local copies, waits for them, and re-layouts: 3.73 us -> 1.28 us
    all_gather x1, blocking collectives: 40.3 us -> 38.1 us  [local(): hidden = lax.all_gather(hidden, 'gx', axis=0, tiled=True)]
  transfers between devices with their start and end apart: 6 -> 6, of which waited for: 3 -> 2; matrix products, arithmetic and copies ran while one was open for 7% -> 10% of each run, Pallas kernels for 0% -> 0%
where the time goes in v9:
time: 123 us; the launch traced here: 121 us
  blocking collectives  59.6 us (48%)
  local copies, waits for them, and re-layouts  23.8 us (19%)
  starting transfers between devices  16.7 us (14%)
  waiting for transfers between devices  6.65 us (5%)
  other arithmetic  5.64 us (5%)
  Pallas kernels  4.76 us (4%)
  matrix products  2.54 us (2%)
  between operations  1.47 us (1%)
    all_gather x1, blocking collectives, local(): hidden = lax.all_gather(hidden, 'gx', axis=0, tiled=True)  38.1 us
    all_gather x1, blocking collectives, local(): hidden = lax.all_gather(hidden, 'gy', axis=1, tiled=True)  21.5 us
    ppermute x6, starting transfers between devices, shifted(): lax.ppermute(value, axis, [(source, source + steps) for source in range(l...  16.7 us
    ppermute x6, waiting for transfers between devices, shifted(): lax.ppermute(value, axis, [(source, source + steps) for source in range(l...  6.65 us
    pallas_call x1, Pallas kernels, strided_chain(): pl.pallas_call(functools.partial(chain_kernel, plan=tuple(plan)), out_sha...  4.76 us
    slice x36, local copies, waits for them, and re-layouts, strided_cells(): piece = padded[first:first + 2 * rows:2, second:second + 2 * cols:2]  3.02 us
    mul x1, local copies, waits for them, and re-layouts, gelu_tanh(): return jax.nn.gelu(value, approximate=True)  2.73 us
  transfers between devices with their start and end apart: 6, of which 2 were waited for; matrix products, arithmetic and copies ran while one was open for 10% of the time, Pallas kernels for 0%

profile of v9, /device:TPU:6, one launch (start us, length us, event | category | flops | bytes accessed | tf_op | source)
XLA Modules:
  0.0 121.2 jit_solution(14202927961790485559)
XLA Ops:
  0.7 1.1 slice.471
  1.8 1.8 %collective-permute-start = (bf16[17,4096]{1,0:T(8,128)(2,1)S(1)}, bf16[17,4096]{1,0:T(8,128)(2,1)S(1)}, u32[]{:S(2)}, u32[]{:S(2)}) collective-permute-start(bf16[17,4096]{1,0:T(8,128)(2,1)S(1)} %slice.471), channel_id=1, source_target_pairs={{0,16},{16,32},{32,48},{48,64},{64,80},{80,96},{96,112},{112,128},... | collective-permute-start | bytes 417800 | tf_op jit(solution)/shard_map/ppermute | solution.py:16
  3.6 0.9 slice.472
  4.4 1.3 %collective-permute-start.1 = (bf16[2,4096]{1,0:T(2,128)(2,1)S(1)}, bf16[2,4096]{1,0:T(2,128)(2,1)S(1)}, u32[]{:S(2)}, u32[]{:S(2)}) collective-permute-start(bf16[2,4096]{1,0:T(2,128)(2,1)S(1)} %slice.472), channel_id=1, source_target_pairs={{16,0},{32,16},{48,32},{64,48},{80,64},{96,80},{112,96},{128,112},... | collective-permute-start | bytes 49160 | tf_op jit(solution)/shard_map/ppermute | solution.py:16
  5.7 1.0 slice_bitcast_fusion.10
  7.7 1.5 %collective-permute-done.1 = bf16[2,4096]{1,0:T(2,128)(2,1)S(1)} collective-permute-done((bf16[2,4096]{1,0:T(2,128)(2,1)S(1)}, bf16[2,4096]{1,0:T(2,128)(2,1)S(1)}, u32[]{:S(2)}, u32[]{:S(2)}) %collective-permute-start.1) | collective-permute-done | bytes 16416 | tf_op jit(solution)/shard_map/ppermute | solution.py:16
  9.6 3.5 %collective-permute-start.2 = (bf16[51,544]{1,0:T(8,128)(2,1)S(1)}, bf16[51,544]{1,0:T(8,128)(2,1)S(1)}, u32[]{:S(2)}, u32[]{:S(2)}) collective-permute-start(bf16[51,544]{1,0:T(8,128)(2,1)S(1)} %slice.473), channel_id=1, source_target_pairs={{0,1},{1,2},{2,3},{3,4},{4,5},{5,6},{6,7},{7,8},{8,9},{9,10},{10,1... | collective-permute-start | bytes 166472 | tf_op jit(solution)/shard_map/ppermute | solution.py:16
  13.0 4.5 %collective-permute-start.3 = (bf16[51,64]{1,0:T(8,128)(2,1)S(1)}, bf16[51,64]{1,0:T(8,128)(2,1)S(1)}, u32[]{:S(2)}, u32[]{:S(2)}) collective-permute-start(bf16[51,64]{1,0:T(8,128)(2,1)S(1)} %slice.481), channel_id=1, source_target_pairs={{1,0},{2,1},{3,2},{4,3},{5,4},{6,5},{7,6},{8,7},{9,8},{10,9},{11,1... | collective-permute-start | bytes 19592 | tf_op jit(solution)/shard_map/ppermute | solution.py:16
  17.5 0.9 pad_maximum_fusion.refs_12_
  18.4 0.7 pad_maximum_fusion.3.refs_9_
  19.1 0.6 pad_maximum_fusion.5.refs_6_
  19.7 0.6 copy_bitcast_fusion
  20.5 0.6 copy.52
  21.1 0.6 copy.51
  21.8 0.7 tile.84.refs_2_
  22.6 0.7 tile.81.refs_1_
  23.3 0.7 tile_reshape.21.refs_5_
  24.0 0.7 tile_reshape.20.refs_4_
  24.6 0.7 mul.589.refs_3_
  25.3 0.8 concatenate.58
  26.2 1.5 %fusion.5 = bf16[47,4576]{1,0:T(8,128)(2,1)S(1)} fusion(bf16[51,544]{1,0:T(8,128)(2,1)S(1)} %collective-permute-done.2, bf16[51,4704]{1,0:T(8,128)(2,1)S(1)} %concatenate.58, bf16[51,4096]{1,0:T(8,128)(2,1)S(1)} %pad_maximum_fusion.1, f32[4576]{0:T(1024)S(1)} %tile.78, f32[4576]{0:T(1024)S(1)} %tile.76, f32[4576]{0:T(1024)S(1)} %tile.74, f32[4576]{0:T(1024)S(1)} %tile.72, ...), kind=kLoop, calls=%fused_computation.13 | loop fusion | flops 9678240 | bytes 2358592 | tf_op jit(solution)/shard_map/convert_element_type | solution.py:38
  27.7 1.6 %reshape.216 = bf16[6721,32]{1,0:T(8,128)(2,1)S(1)} reshape(bf16[47,4576]{1,0:T(8,128)(2,1)S(1)} %fusion.5) | data formatting | bytes 860288 | tf_op jit(solution)/shard_map/reshape | solution.py:38
  29.3 1.7 %fusion.13 = f32[6721,32]{0,1:T(8,128)} fusion(bf16[6721,32]{1,0:T(8,128)(2,1)S(1)} %reshape.216, bf16[32,32]{1,0:T(8,128)(2,1)S(1)} %copy-done), kind=kOutput, calls=%fused_computation.22 | convolution fusion | flops 15485184 | bytes 1292480 | tf_op jit(solution)/shard_map/dot_general | solution.py:39
  30.9 2.7 %copy.28 = f32[6721,32]{1,0:T(8,128)S(1)} copy(f32[6721,32]{0,1:T(8,128)} %fusion.13) | data formatting | bytes 1720576 | tf_op jit(solution)/shard_map/mul | solution.py:33
  33.7 1.7 %reshape.217 = f32[47,4576]{1,0:T(8,128)} reshape(f32[6721,32]{1,0:T(8,128)S(1)} %copy.28) | data formatting | bytes 1720576 | tf_op jit(solution)/shard_map/reshape | solution.py:40
  35.4 1.6 %and_select_fusion = bf16[47,4576]{1,0:T(8,128)(2,1)S(1)} fusion(f32[47,4576]{1,0:T(8,128)} %reshape.217, pred[4576]{0:T(1024)(128)(4,1)S(1)} %fusion.64, pred[47]{0:T(512)(128)(4,1)S(1)} %compare_or_fusion, bf16[51,4096]{1,0:T(8,128)(2,1)} %copy-done.1, bf16[51,544]{1,0:T(8,128)(2,1)S(1)} %collective-permute-done.2), kind=kLoop, calls=%fused_computation.15 | loop fusion | flops 1720576 | bytes 1768335 | tf_op jit(solution)/shard_map/jit(_where)/select_n | solution.py:195
  37.1 0.8 pad.12.refs_0_
  37.8 4.8 %shard_map.140 = bf16[8,4608]{1,0:T(8,128)(2,1)} custom-call(bf16[48,4608]{1,0:T(8,128)(2,1)} %pad.12.refs_0_, f32[3,128]{1,0:T(4,128)} %tile.81.refs_1_, f32[3,128]{1,0:T(4,128)} %tile.84.refs_2_, bf16[128,128]{1,0:T(8,128)(2,1)} %mul.589.refs_3_, f32[3,128]{1,0:T(4,128)} %tile_reshape.20.refs_4_, f32[3,128]{1,0:T(4,128)} %tile_reshape.21.refs_5_, ...), custom_call_target="tpu_custom_call" | custom-call | tf_op jit(solution)/shard_map/pallas_call | solution.py:155
  42.6 0.9 slice_reduce_fusion
  43.5 3.8 %collective-permute-start.4 = (bf16[1,8,512]{2,1,0:T(8,128)(2,1)S(1)}, bf16[1,8,512]{2,1,0:T(8,128)(2,1)S(1)}, u32[]{:S(2)}, u32[]{:S(2)}) collective-permute-start(bf16[1,8,512]{2,1,0:T(8,128)(2,1)S(1)} %slice.512), channel_id=1, source_target_pairs={{0,16},{16,32},{32,48},{48,64},{64,80},{80,96},{96,112},{112,128},... | collective-permute-start | bytes 24584 | tf_op jit(solution)/shard_map/ppermute | solution.py:16
  47.4 0.9 slice.614
  48.3 1.9 %collective-permute-start.5 = (bf16[3,7,512]{2,1,0:T(8,128)(2,1)S(1)}, bf16[3,7,512]{2,1,0:T(8,128)(2,1)S(1)}, u32[]{:S(2)}, u32[]{:S(2)}) collective-permute-start(bf16[3,7,512]{2,1,0:T(8,128)(2,1)S(1)} %slice.615), channel_id=1, source_target_pairs={{0,1},{1,2},{2,3},{3,4},{4,5},{5,6},{6,7},{7,8},{8,9},{9,10},{10,1... | collective-permute-start | bytes 64520 | tf_op jit(solution)/shard_map/ppermute | solution.py:16
  50.3 0.9 slice.604
  51.1 5.1 %collective-permute-done.5 = bf16[3,7,512]{2,1,0:T(8,128)(2,1)S(1)} collective-permute-done((bf16[3,7,512]{2,1,0:T(8,128)(2,1)S(1)}, bf16[3,7,512]{2,1,0:T(8,128)(2,1)S(1)}, u32[]{:S(2)}, u32[]{:S(2)}) %collective-permute-start.5) | collective-permute-done | bytes 21536 | tf_op jit(solution)/shard_map/ppermute | solution.py:16
  56.5 0.2 fusion.77
  56.7 38.1 %all-gather.2 = bf16[32,7,512]{2,1,0:T(8,128)(2,1)S(1)} all-gather(bf16[1,7,512]{2,1,0:T(8,128)(2,1)S(1)} %fusion.77), channel_id=2, replica_groups=mesh['gx'=32,'gy'=16] {'gx'}, dimensions={0}, use_global_device_ids=true | all-gather | bytes 236544 | tf_op jit(solution)/shard_map/all_gather | solution.py:206
  95.2 0.2 slice.538
  95.6 0.2 slice.544
  96.1 0.2 slice.550
  96.5 0.2 fusion.40
  97.0 0.2 fusion.89
  97.2 21.5 %all-gather.1 = bf16[8,8192]{1,0:T(8,128)(2,1)S(1)} all-gather(bf16[8,512]{1,0:T(8,128)(2,1)S(1)} %fusion.89), channel_id=3, replica_groups=mesh['gx'=32,'gy'=16] {'gy'}, dimensions={1}, use_global_device_ids=true | all-gather | bytes 139264 | tf_op jit(solution)/shard_map/all_gather | solution.py:209
  119.0 0.1 slice.578
  119.1 0.2 slice.584
  119.9 0.2 slice.586
  120.1 0.2 slice.588
  120.3 0.3 fusion.52
  120.5 0.6 reshape_reshape.3
  (123 shorter events, 3.9 us)
Async XLA Ops:
  0.6 28.6 %copy-start = (bf16[32,32]{1,0:T(8,128)(2,1)S(1)}, bf16[32,32]{1,0:T(8,128)(2,1)}, u32[]{:S(2)}) copy-start(bf16[32,32]{1,0:T(8,128)(2,1)} %param.15) | copy-start | bytes 6148
  0.6 8.6 %copy-start.2 = (bf16[32,4096]{1,0:T(8,128)(2,1)S(1)}, bf16[32,4096]{1,0:T(8,128)(2,1)}, u32[]{:S(2)}) copy-start(bf16[32,4096]{1,0:T(8,128)(2,1)} %param.13) | copy-start | bytes 786436
  0.7 19.8 %copy-start.10 = (f32[9,32]{1,0:T(8,128)S(1)}, f32[9,32]{1,0:T(8,128)}, u32[]{:S(2)}) copy-start(f32[9,32]{1,0:T(8,128)} %param.16) | copy-start | bytes 3460
  0.7 18.4 %copy-start.8 = (bf16[32,64]{1,0:T(8,128)(2,1)S(1)}, bf16[32,64]{1,0:T(8,128)(2,1)}, u32[]{:S(2)}) copy-start(bf16[32,64]{1,0:T(8,128)(2,1)} %param.17) | copy-start | bytes 12292
  0.7 19.8 %copy-start.11 = (f32[9,64]{1,0:T(8,128)S(1)}, f32[9,64]{1,0:T(8,128)}, u32[]{:S(2)}) copy-start(f32[9,64]{1,0:T(8,128)} %param.18) | copy-start | bytes 6916
  0.7 18.4 %copy-start.6 = (bf16[64,128]{1,0:T(8,128)(2,1)S(1)}, bf16[64,128]{1,0:T(8,128)(2,1)}, u32[]{:S(2)}) copy-start(bf16[64,128]{1,0:T(8,128)(2,1)} %param.19) | copy-start | bytes 49156
  0.7 8.8 %copy-start.9 = (f32[9,128]{1,0:T(8,128)S(1)}, f32[9,128]{1,0:T(8,128)}, u32[]{:S(2)}) copy-start(f32[9,128]{1,0:T(8,128)} %param.20) | copy-start | bytes 13828
  0.7 17.7 %copy-start.5 = (bf16[128,256]{1,0:T(8,128)(2,1)S(1)}, bf16[128,256]{1,0:T(8,128)(2,1)}, u32[]{:S(2)}) copy-start(bf16[128,256]{1,0:T(8,128)(2,1)} %param.21) | copy-start | bytes 196612
  0.7 8.8 %copy-start.7 = (f32[9,256]{1,0:T(8,128)S(1)}, f32[9,256]{1,0:T(8,128)}, u32[]{:S(2)}) copy-start(f32[9,256]{1,0:T(8,128)} %param.22) | copy-start | bytes 27652
  0.7 16.8 %copy-start.3 = (bf16[256,512]{1,0:T(8,128)(2,1)S(1)}, bf16[256,512]{1,0:T(8,128)(2,1)}, u32[]{:S(2)}) copy-start(bf16[256,512]{1,0:T(8,128)(2,1)} %param.23) | copy-start | bytes 786436
  1.8 7.4 %collective-permute-start = (bf16[17,4096]{1,0:T(8,128)(2,1)S(1)}, bf16[17,4096]{1,0:T(8,128)(2,1)S(1)}, u32[]{:S(2)}, u32[]{:S(2)}) collective-permute-start(bf16[17,4096]{1,0:T(8,128)(2,1)S(1)} %slice.471), channel_id=1, source_target_pairs={{0,16},{16,32},{32,48},{48,64},{64,80},{80,96},{96,112},{112,128},... | collective-permute-start | bytes 417800 | tf_op jit(solution)/shard_map/ppermute | solution.py:16
  4.4 4.8 %collective-permute-start.1 = (bf16[2,4096]{1,0:T(2,128)(2,1)S(1)}, bf16[2,4096]{1,0:T(2,128)(2,1)S(1)}, u32[]{:S(2)}, u32[]{:S(2)}) collective-permute-start(bf16[2,4096]{1,0:T(2,128)(2,1)S(1)} %slice.472), channel_id=1, source_target_pairs={{16,0},{32,16},{48,32},{64,48},{80,64},{96,80},{112,96},{128,112},... | collective-permute-start | bytes 49160 | tf_op jit(solution)/shard_map/ppermute | solution.py:16
  9.3 18.3 %copy-start.1 = (bf16[51,4096]{1,0:T(8,128)(2,1)}, bf16[51,4096]{1,0:T(8,128)(2,1)S(1)}, u32[]{:S(2)}) copy-start(bf16[51,4096]{1,0:T(8,128)(2,1)S(1)} %pad_maximum_fusion.1) | copy-start | bytes 1253380
  9.6 15.8 %collective-permute-start.2 = (bf16[51,544]{1,0:T(8,128)(2,1)S(1)}, bf16[51,544]{1,0:T(8,128)(2,1)S(1)}, u32[]{:S(2)}, u32[]{:S(2)}) collective-permute-start(bf16[51,544]{1,0:T(8,128)(2,1)S(1)} %slice.473), channel_id=1, source_target_pairs={{0,1},{1,2},{2,3},{3,4},{4,5},{5,6},{6,7},{7,8},{8,9},{9,10},{10,1... | collective-permute-start | bytes 166472 | tf_op jit(solution)/shard_map/ppermute | solution.py:16
  13.0 12.3 %collective-permute-start.3 = (bf16[51,64]{1,0:T(8,128)(2,1)S(1)}, bf16[51,64]{1,0:T(8,128)(2,1)S(1)}, u32[]{:S(2)}, u32[]{:S(2)}) collective-permute-start(bf16[51,64]{1,0:T(8,128)(2,1)S(1)} %slice.481), channel_id=1, source_target_pairs={{1,0},{2,1},{3,2},{4,3},{5,4},{6,5},{7,6},{8,7},{9,8},{10,9},{11,1... | collective-permute-start | bytes 19592 | tf_op jit(solution)/shard_map/ppermute | solution.py:16
  35.4 11.9 %copy-start.4 = (f32[4,9,512]{2,0,1:T(4,128)S(1)}, f32[4,9,512]{2,0,1:T(4,128)}, u32[]{:S(2)}) copy-start(f32[4,9,512]{2,0,1:T(4,128)} %param.24) | copy-start | bytes 221188
  37.0 19.4 %copy-start.12 = (bf16[4,512,512]{2,1,0:T(8,128)(2,1)S(1)}, bf16[4,512,512]{2,1,0:T(8,128)(2,1)}, u32[]{:S(2)}) copy-start(bf16[4,512,512]{2,1,0:T(8,128)(2,1)} %param.25) | copy-start | bytes 6291460
  43.5 4.7 %collective-permute-start.4 = (bf16[1,8,512]{2,1,0:T(8,128)(2,1)S(1)}, bf16[1,8,512]{2,1,0:T(8,128)(2,1)S(1)}, u32[]{:S(2)}, u32[]{:S(2)}) collective-permute-start(bf16[1,8,512]{2,1,0:T(8,128)(2,1)S(1)} %slice.512), channel_id=1, source_target_pairs={{0,16},{16,32},{32,48},{48,64},{64,80},{80,96},{96,112},{112,128},... | collective-permute-start | bytes 24584 | tf_op jit(solution)/shard_map/ppermute | solution.py:16
  48.3 7.9 %collective-permute-start.5 = (bf16[3,7,512]{2,1,0:T(8,128)(2,1)S(1)}, bf16[3,7,512]{2,1,0:T(8,128)(2,1)S(1)}, u32[]{:S(2)}, u32[]{:S(2)}) collective-permute-start(bf16[3,7,512]{2,1,0:T(8,128)(2,1)S(1)} %slice.615), channel_id=1, source_target_pairs={{0,1},{1,2},{2,3},{3,4},{4,5},{5,6},{6,7},{7,8},{8,9},{9,10},{10,1... | collective-permute-start | bytes 64520 | tf_op jit(solution)/shard_map/ppermute | solution.py:16

commit v10 on v9

--- a/solution.py
+++ b/solution.py
@@ -102,12 +102,54 @@
 
 
 def chain_kernel(*refs, plan):
-    x_ref = refs[0]
-    o_ref = refs[-1]
-    value = x_ref[...].astype(jnp.float32)
+    value = refs[0][...].astype(jnp.float32)
+    refs[-1][...] = chain_levels(value, refs[1:-1], plan).astype(refs[-1].dtype)
+
+
+def pick_rows(value, rows, offset, valid):
+    shape = (rows, value.shape[0])
+    out_row = lax.broadcasted_iota(jnp.int32, shape, 0)
+    in_row = lax.broadcasted_iota(jnp.int32, shape, 1)
+    pick = ((in_row == offset + out_row) & (in_row < valid)).astype(jnp.float32)
+    return jnp.dot(pick, value, preferred_element_type=jnp.float32)
+
+
+def fine_kernel(*refs, plan, rows, cols, margin, chans):
+    x_ref, pat_ref, pw_ref, row_ref, col_ref = refs[:5]
+    fine_ref, o_ref = refs[-2:]
+    source = x_ref[...].astype(jnp.float32)
+    lanes = source.shape[1]
+    width = plan[0][0] * 0 + col_ref.shape[1]
+    ext_rows = row_ref.shape[0]
+    shifted = []
+    for first in range(3):
+        slab = pick_rows(source, ext_rows, 2 * first, source.shape[0])
+        shifted.append(
+            [slab if second == 0 else pltpu.roll(slab, lanes - 2 * second * chans, 1) for second in range(3)]
+        )
+    weight = pw_ref[...]
+    parts = []
+    for index in range(width // 128):
+        window = slice(index * 128, (index + 1) * 128)
+        total = None
+        for first in range(3):
+            for second in range(3):
+                term = shifted[first][second][:, window] * pat_ref[3 * first + second : 3 * first + second + 1, :]
+                total = term if total is None else total + term
+        mixed = gelu_tanh(jnp.dot(total.astype(jnp.bfloat16), weight, preferred_element_type=jnp.float32))
+        parts.append((shifted[1][1][:, window] + mixed).astype(jnp.bfloat16))
+    hidden = jnp.concatenate(parts, axis=1)
+    keep = row_ref[...] * col_ref[...]
+    hidden = jnp.where(keep > 0, hidden, jnp.zeros_like(hidden)).astype(jnp.float32)
+    inner = pltpu.roll(hidden, width - margin * chans, 1)[:, : cols * chans]
+    fine_ref[...] = pick_rows(inner, rows, margin, ext_rows).astype(fine_ref.dtype)
+    o_ref[...] = chain_levels(hidden, refs[5:-2], plan).astype(o_ref.dtype)
+
+
+def chain_levels(value, refs, plan):
     lanes = value.shape[1]
     for level, (valid, rows, chans, outs) in enumerate(plan):
-        near_ref, far_ref, w_ref = refs[1 + 3 * level : 4 + 3 * level]
+        near_ref, far_ref, w_ref = refs[3 * level : 3 + 3 * level]
         shape = (rows, value.shape[0])
         out_row = lax.broadcasted_iota(jnp.int32, shape, 0)
         in_row = lax.broadcasted_iota(jnp.int32, shape, 1)
@@ -132,7 +174,24 @@
             part = jnp.dot(total.astype(jnp.bfloat16), weight, preferred_element_type=jnp.float32)
             parts.append(gelu_tanh(part).astype(jnp.bfloat16))
         value = jnp.concatenate(parts, axis=1).astype(jnp.float32)
-    o_ref[...] = value.astype(o_ref.dtype)
+    return value
+
+
+def chain_plan(rows, cols, chans, params):
+    plan = []
+    operands = []
+    lanes = None
+    for taps, weight in params:
+        out_rows = (rows - 1) // 2
+        out_cols = (cols - 1) // 2
+        pairs = out_cols + 1
+        if pairs * 2 * chans % 128:
+            pairs += 1
+        lanes = lanes or pairs * 2 * chans
+        plan.append((rows, -(-out_rows // 8) * 8, chans, weight.shape[1]))
+        operands.extend(prepare(taps, weight))
+        rows, cols, chans = out_rows, out_cols, weight.shape[1]
+    return tuple(plan), operands, lanes, (rows, cols, chans)
 
 
 def strided_chain(ext, chans, params):
@@ -175,26 +234,34 @@
     flat_pad = jnp.concatenate([leftside, stacked, rightside], axis=1)
     ext_rows = rows + margin
     ext_cols = cols + margin
-    tiled = jnp.tile(dw0, (1, ext_cols))
-    total = jnp.zeros((ext_rows, ext_cols * chans), jnp.float32)
-    for first in range(3):
-        for second in range(3):
-            piece = flat_pad[
-                2 * first : 2 * first + ext_rows,
-                2 * second * chans : 2 * second * chans + ext_cols * chans,
-            ]
-            total = total + piece.astype(jnp.float32) * tiled[3 * first + second]
-    centre = flat_pad[2 : 2 + ext_rows, 2 * chans : 2 * chans + ext_cols * chans]
-    hidden = (centre.astype(jnp.float32) + point_flat(total, pw0, ext_rows, ext_cols)).astype(
-        jnp.bfloat16
+    plan, operands, lanes, (last_rows, last_cols, last_chans) = chain_plan(
+        ext_rows, ext_cols, chans, params
     )
-    row_ok = (lax.axis_index("gx") > 0) | (lax.broadcasted_iota(jnp.int32, hidden.shape, 0) >= margin)
-    col_ok = (lax.axis_index("gy") > 0) | (
-        lax.broadcasted_iota(jnp.int32, hidden.shape, 1) >= margin * chans
+    padded_rows = -(-ext_rows // 8) * 8
+    source = jnp.pad(
+        flat_pad,
+        (
+            (0, padded_rows + 8 - flat_pad.shape[0]),
+            (0, lanes + 128 - flat_pad.shape[1]),
+        ),
     )
-    hidden = jnp.where(row_ok & col_ok, hidden, jnp.zeros_like(hidden))
-    fine = hidden[margin:, margin * chans :]
-    hidden = strided_chain(hidden, chans, params)
+    pattern = jnp.tile(dw0, (1, 128 // chans))
+    block = jnp.kron(jnp.eye(128 // chans, dtype=pw0.dtype), pw0)
+    row_keep = (
+        (lax.axis_index("gx") > 0) | (lax.broadcasted_iota(jnp.int32, (padded_rows, 1), 0) >= margin)
+    ).astype(jnp.float32)
+    col_keep = (
+        (lax.axis_index("gy") > 0) | (lax.broadcasted_iota(jnp.int32, (1, lanes), 1) >= margin * chans)
+    ).astype(jnp.float32)
+    body = functools.partial(fine_kernel, plan=plan, rows=rows, cols=cols, margin=margin, chans=chans)
+    fine, hidden = pl.pallas_call(
+        body,
+        out_shape=(
+            jax.ShapeDtypeStruct((rows, cols * chans), jnp.bfloat16),
+            jax.ShapeDtypeStruct((plan[-1][1], lanes), jnp.bfloat16),
+        ),
+    )(source, pattern, block, row_keep, col_keep, *operands)
+    hidden = hidden[:last_rows, : last_cols * last_chans]
     coarse_chans = dwc.shape[2]
     halo = 2 ** (LC - 1) - 1
     grid4 = hidden.reshape(hidden.shape[0], -1, coarse_chans)

time: 123 us -> 118 us (0.959)
  local copies, waits for them, and re-layouts: 23.8 us -> 18.5 us
  Pallas kernels: 4.76 us -> 6.41 us
  matrix products: 2.54 us -> 0.89 us
    reshape x2 -> x0, local copies, waits for them, and re-layouts: 3.35 us -> none  [the longest x1 1.75 us: point_flat(): return gelu_tanh(mixed).reshape(rows, cols * weight.shape[1])]
    mul x1, local copies, waits for them, and re-layouts: 2.73 us -> 0.74 us  [local(): block = jnp.kron(jnp.eye(128 // chans, dtype=pw0.dtype), pw0)]
    slice x3 -> x1, local copies, waits for them, and re-layouts: 2.7 us -> 0.85 us  [local(): hidden = hidden[:last_rows, :last_cols * last_chans]]
    pallas_call x1, Pallas kernels: 4.76 us -> 6.41 us  [local(): pl.pallas_call(body, out_shape=(jax.ShapeDtypeStruct((rows, cols * chans)...]
    dot_general x1 -> x0, matrix products: 1.65 us -> none  [point_flat(): mixed = jnp.dot(flat, weight, preferred_element_type=jnp.float32)]
    select_n x1 -> x0, other arithmetic: 1.61 us -> none  [local(): hidden = jnp.where(row_ok & col_ok, hidden, jnp.zeros_like(hidden))]
    reshape x4, local copies, waits for them, and re-layouts: 0.04 us -> 1.45 us  [prepare(): grouped = taps.reshape(3, 3, chans)]
    all_gather x1, blocking collectives: 38.1 us -> 39.3 us  [local(): hidden = lax.all_gather(hidden, 'gx', axis=0, tiled=True)]
  transfers between devices with their start and end apart: 6 -> 6, of which waited for: 2 -> 1; matrix products, arithmetic and copies ran while one was open for 10% -> 12% of each run, Pallas kernels for 0% -> 0%
where the time goes in v10:
time: 118 us; the launch traced here: 116 us
  blocking collectives  60.8 us (52%)
  local copies, waits for them, and re-layouts  18.5 us (16%)
  starting transfers between devices  17.1 us (14%)
  Pallas kernels  6.41 us (5%)
  waiting for transfers between devices  5.88 us (5%)
  other arithmetic  5.47 us (5%)
  between operations  1.21 us (1%)
    all_gather x1, blocking collectives, local(): hidden = lax.all_gather(hidden, 'gx', axis=0, tiled=True)  39.3 us
    all_gather x1, blocking collectives, local(): hidden = lax.all_gather(hidden, 'gy', axis=1, tiled=True)  21.5 us
    ppermute x6, starting transfers between devices, shifted(): lax.ppermute(value, axis, [(source, source + steps) for source in range(l...  17.1 us
    pallas_call x1, Pallas kernels, local(): pl.pallas_call(body, out_shape=(jax.ShapeDtypeStruct((rows, cols * chans)...  6.41 us
    ppermute x6, waiting for transfers between devices, shifted(): lax.ppermute(value, axis, [(source, source + steps) for source in range(l...  5.88 us
    slice x36, local copies, waits for them, and re-layouts, strided_cells(): piece = padded[first:first + 2 * rows:2, second:second + 2 * cols:2]  3.02 us
  transfers between devices with their start and end apart: 6, of which 1 were waited for; matrix products, arithmetic and copies ran while one was open for 12% of the time, Pallas kernels for 0%

profile of v10, /device:TPU:6, one launch (start us, length us, event | category | flops | bytes accessed | tf_op | source)
XLA Modules:
  0.0 116.3 jit_solution(10590226025099117576)
XLA Ops:
  0.7 1.0 slice.371
  1.7 1.8 %collective-permute-start = (bf16[17,4096]{1,0:T(8,128)(2,1)S(1)}, bf16[17,4096]{1,0:T(8,128)(2,1)S(1)}, u32[]{:S(2)}, u32[]{:S(2)}) collective-permute-start(bf16[17,4096]{1,0:T(8,128)(2,1)S(1)} %slice.371), channel_id=1, source_target_pairs={{0,16},{16,32},{32,48},{48,64},{64,80},{80,96},{96,112},{112,128},... | collective-permute-start | bytes 417800 | tf_op jit(solution)/shard_map/ppermute | solution.py:16
  3.5 0.9 slice.372
  4.3 1.3 %collective-permute-start.1 = (bf16[2,4096]{1,0:T(2,128)(2,1)S(1)}, bf16[2,4096]{1,0:T(2,128)(2,1)S(1)}, u32[]{:S(2)}, u32[]{:S(2)}) collective-permute-start(bf16[2,4096]{1,0:T(2,128)(2,1)S(1)} %slice.372), channel_id=1, source_target_pairs={{16,0},{32,16},{48,32},{64,48},{80,64},{96,80},{112,96},{128,112},... | collective-permute-start | bytes 49160 | tf_op jit(solution)/shard_map/ppermute | solution.py:16
  5.7 0.6 or_convert_fusion.refs_4_
  6.3 0.8 broadcast_multiply_fusion
  7.1 0.6 fusion.46.refs_3_
  7.7 0.7 mul.495.refs_2_
  8.4 0.7 tile.29
  9.1 0.7 tile.30.refs_1_
  9.8 1.1 pad_maximum_fusion.1
  11.0 0.7 reshape.223
  11.7 0.7 reshape.224
  12.5 3.5 %collective-permute-start.2 = (bf16[51,544]{1,0:T(8,128)(2,1)S(1)}, bf16[51,544]{1,0:T(8,128)(2,1)S(1)}, u32[]{:S(2)}, u32[]{:S(2)}) collective-permute-start(bf16[51,544]{1,0:T(8,128)(2,1)S(1)} %slice.373), channel_id=1, source_target_pairs={{0,1},{1,2},{2,3},{3,4},{4,5},{5,6},{6,7},{7,8},{8,9},{9,10},{10,1... | collective-permute-start | bytes 166472 | tf_op jit(solution)/shard_map/ppermute | solution.py:16
  16.0 4.5 %collective-permute-start.3 = (bf16[51,64]{1,0:T(8,128)(2,1)S(1)}, bf16[51,64]{1,0:T(8,128)(2,1)S(1)}, u32[]{:S(2)}, u32[]{:S(2)}) collective-permute-start(bf16[51,64]{1,0:T(8,128)(2,1)S(1)} %slice.374), channel_id=1, source_target_pairs={{1,0},{2,1},{3,2},{4,3},{5,4},{6,5},{7,6},{8,7},{9,8},{10,9},{11,1... | collective-permute-start | bytes 19592 | tf_op jit(solution)/shard_map/ppermute | solution.py:16
  20.5 0.8 pad_maximum_fusion.refs_16_
  21.3 0.7 pad_maximum_fusion.2.refs_13_
  22.0 0.6 pad_maximum_fusion.4.refs_10_
  22.6 0.6 copy_bitcast_fusion
  23.4 0.6 copy.49
  24.0 0.6 copy.48
  24.7 0.7 tile.36.refs_6_
  25.5 0.7 tile.33.refs_5_
  26.1 0.7 tile_reshape.21.refs_9_
  26.8 0.6 tile_reshape.20.refs_8_
  27.4 0.7 mul.499.refs_7_
  28.1 0.8 concatenate.49
  29.0 0.8 pad.12.refs_0_
  29.8 6.4 %shard_map.140 = (bf16[32,4096]{1,0:T(8,128)(2,1)}, bf16[8,4608]{1,0:T(8,128)(2,1)}) custom-call(bf16[56,4736]{1,0:T(8,128)(2,1)} %pad.12.refs_0_, f32[9,128]{1,0:T(8,128)} %tile.30.refs_1_, bf16[128,128]{1,0:T(8,128)(2,1)} %mul.495.refs_2_, f32[48,1]{1,0:T(8,128)} %fusion.46.refs_3_, f32[1,4608]{1,0:T(1,128)} %or_convert_fusion.refs_4_, ...), custom_call_target="tpu_custom_call" | custom-call | tf_op jit(solution)/shard_map/pallas_call | solution.py:257
  36.2 0.9 slice_reduce_fusion
  37.1 4.2 %collective-permute-start.4 = (bf16[1,8,512]{2,1,0:T(8,128)(2,1)S(1)}, bf16[1,8,512]{2,1,0:T(8,128)(2,1)S(1)}, u32[]{:S(2)}, u32[]{:S(2)}) collective-permute-start(bf16[1,8,512]{2,1,0:T(8,128)(2,1)S(1)} %slice.384), channel_id=1, source_target_pairs={{0,16},{16,32},{32,48},{48,64},{64,80},{80,96},{96,112},{112,128},... | collective-permute-start | bytes 24584 | tf_op jit(solution)/shard_map/ppermute | solution.py:16
  41.4 0.9 slice.385
  42.3 1.9 %collective-permute-start.5 = (bf16[3,7,512]{2,1,0:T(8,128)(2,1)S(1)}, bf16[3,7,512]{2,1,0:T(8,128)(2,1)S(1)}, u32[]{:S(2)}, u32[]{:S(2)}) collective-permute-start(bf16[3,7,512]{2,1,0:T(8,128)(2,1)S(1)} %slice.471), channel_id=1, source_target_pairs={{0,1},{1,2},{2,3},{3,4},{4,5},{5,6},{6,7},{7,8},{8,9},{9,10},{10,1... | collective-permute-start | bytes 64520 | tf_op jit(solution)/shard_map/ppermute | solution.py:16
  44.2 5.9 %collective-permute-done.5 = bf16[3,7,512]{2,1,0:T(8,128)(2,1)S(1)} collective-permute-done((bf16[3,7,512]{2,1,0:T(8,128)(2,1)S(1)}, bf16[3,7,512]{2,1,0:T(8,128)(2,1)S(1)}, u32[]{:S(2)}, u32[]{:S(2)}) %collective-permute-start.5) | collective-permute-done | bytes 21536 | tf_op jit(solution)/shard_map/ppermute | solution.py:16
  50.3 0.2 fusion.59
  50.5 39.3 %all-gather.2 = bf16[32,7,512]{2,1,0:T(8,128)(2,1)S(1)} all-gather(bf16[1,7,512]{2,1,0:T(8,128)(2,1)S(1)} %fusion.59), channel_id=2, replica_groups=mesh['gx'=32,'gy'=16] {'gx'}, dimensions={0}, use_global_device_ids=true | all-gather | bytes 236544 | tf_op jit(solution)/shard_map/all_gather | solution.py:273
  90.3 0.2 slice.410
  90.7 0.2 slice.416
  91.2 0.2 slice.422
  91.6 0.2 fusion.21
  92.1 0.2 fusion.71
  92.3 21.5 %all-gather.1 = bf16[8,8192]{1,0:T(8,128)(2,1)S(1)} all-gather(bf16[8,512]{1,0:T(8,128)(2,1)S(1)} %fusion.71), channel_id=3, replica_groups=mesh['gx'=32,'gy'=16] {'gy'}, dimensions={1}, use_global_device_ids=true | all-gather | bytes 139264 | tf_op jit(solution)/shard_map/all_gather | solution.py:276
  114.1 0.1 slice.450
  114.2 0.2 slice.456
  115.0 0.2 slice.458
  115.2 0.2 slice.460
  115.4 0.3 fusion.33
  115.6 0.6 reshape_reshape.3
  (92 shorter events, 2.9 us)
Async XLA Ops:
  0.6 22.7 %copy-start.5 = (f32[9,32]{1,0:T(8,128)S(1)}, f32[9,32]{1,0:T(8,128)}, u32[]{:S(2)}) copy-start(f32[9,32]{1,0:T(8,128)} %param.16) | copy-start | bytes 3460
  0.6 21.3 %copy-start.4 = (bf16[32,64]{1,0:T(8,128)(2,1)S(1)}, bf16[32,64]{1,0:T(8,128)(2,1)}, u32[]{:S(2)}) copy-start(bf16[32,64]{1,0:T(8,128)(2,1)} %param.17) | copy-start | bytes 12292
  0.7 22.7 %copy-start.6 = (f32[9,64]{1,0:T(8,128)S(1)}, f32[9,64]{1,0:T(8,128)}, u32[]{:S(2)}) copy-start(f32[9,64]{1,0:T(8,128)} %param.18) | copy-start | bytes 6916
  0.7 21.3 %copy-start.3 = (bf16[64,128]{1,0:T(8,128)(2,1)S(1)}, bf16[64,128]{1,0:T(8,128)(2,1)}, u32[]{:S(2)}) copy-start(bf16[64,128]{1,0:T(8,128)(2,1)} %param.19) | copy-start | bytes 49156
  0.7 20.6 %copy-start.2 = (bf16[128,256]{1,0:T(8,128)(2,1)S(1)}, bf16[128,256]{1,0:T(8,128)(2,1)}, u32[]{:S(2)}) copy-start(bf16[128,256]{1,0:T(8,128)(2,1)} %param.21) | copy-start | bytes 196612
  0.7 19.8 %copy-start = (bf16[256,512]{1,0:T(8,128)(2,1)S(1)}, bf16[256,512]{1,0:T(8,128)(2,1)}, u32[]{:S(2)}) copy-start(bf16[256,512]{1,0:T(8,128)(2,1)} %param.23) | copy-start | bytes 786436
  1.7 8.1 %collective-permute-start = (bf16[17,4096]{1,0:T(8,128)(2,1)S(1)}, bf16[17,4096]{1,0:T(8,128)(2,1)S(1)}, u32[]{:S(2)}, u32[]{:S(2)}) collective-permute-start(bf16[17,4096]{1,0:T(8,128)(2,1)S(1)} %slice.371), channel_id=1, source_target_pairs={{0,16},{16,32},{32,48},{48,64},{64,80},{80,96},{96,112},{112,128},... | collective-permute-start | bytes 417800 | tf_op jit(solution)/shard_map/ppermute | solution.py:16
  4.3 5.5 %collective-permute-start.1 = (bf16[2,4096]{1,0:T(2,128)(2,1)S(1)}, bf16[2,4096]{1,0:T(2,128)(2,1)S(1)}, u32[]{:S(2)}, u32[]{:S(2)}) collective-permute-start(bf16[2,4096]{1,0:T(2,128)(2,1)S(1)} %slice.372), channel_id=1, source_target_pairs={{16,0},{32,16},{48,32},{64,48},{80,64},{96,80},{112,96},{128,112},... | collective-permute-start | bytes 49160 | tf_op jit(solution)/shard_map/ppermute | solution.py:16
  12.5 15.7 %collective-permute-start.2 = (bf16[51,544]{1,0:T(8,128)(2,1)S(1)}, bf16[51,544]{1,0:T(8,128)(2,1)S(1)}, u32[]{:S(2)}, u32[]{:S(2)}) collective-permute-start(bf16[51,544]{1,0:T(8,128)(2,1)S(1)} %slice.373), channel_id=1, source_target_pairs={{0,1},{1,2},{2,3},{3,4},{4,5},{5,6},{6,7},{7,8},{8,9},{9,10},{10,1... | collective-permute-start | bytes 166472 | tf_op jit(solution)/shard_map/ppermute | solution.py:16
  16.0 12.2 %collective-permute-start.3 = (bf16[51,64]{1,0:T(8,128)(2,1)S(1)}, bf16[51,64]{1,0:T(8,128)(2,1)S(1)}, u32[]{:S(2)}, u32[]{:S(2)}) collective-permute-start(bf16[51,64]{1,0:T(8,128)(2,1)S(1)} %slice.374), channel_id=1, source_target_pairs={{1,0},{2,1},{3,2},{4,3},{5,4},{6,5},{7,6},{8,7},{9,8},{10,9},{11,1... | collective-permute-start | bytes 19592 | tf_op jit(solution)/shard_map/ppermute | solution.py:16
  21.3 20.0 %copy-start.1 = (f32[4,9,512]{2,0,1:T(4,128)S(1)}, f32[4,9,512]{2,0,1:T(4,128)}, u32[]{:S(2)}) copy-start(f32[4,9,512]{2,0,1:T(4,128)} %param.24) | copy-start | bytes 221188
  27.4 22.9 %copy-start.7 = (bf16[4,512,512]{2,1,0:T(8,128)(2,1)S(1)}, bf16[4,512,512]{2,1,0:T(8,128)(2,1)}, u32[]{:S(2)}) copy-start(bf16[4,512,512]{2,1,0:T(8,128)(2,1)} %param.25) | copy-start | bytes 6291460
  37.1 5.1 %collective-permute-start.4 = (bf16[1,8,512]{2,1,0:T(8,128)(2,1)S(1)}, bf16[1,8,512]{2,1,0:T(8,128)(2,1)S(1)}, u32[]{:S(2)}, u32[]{:S(2)}) collective-permute-start(bf16[1,8,512]{2,1,0:T(8,128)(2,1)S(1)} %slice.384), channel_id=1, source_target_pairs={{0,16},{16,32},{32,48},{48,64},{64,80},{80,96},{96,112},{112,128},... | collective-permute-start | bytes 24584 | tf_op jit(solution)/shard_map/ppermute | solution.py:16
  42.3 7.8 %collective-permute-start.5 = (bf16[3,7,512]{2,1,0:T(8,128)(2,1)S(1)}, bf16[3,7,512]{2,1,0:T(8,128)(2,1)S(1)}, u32[]{:S(2)}, u32[]{:S(2)}) collective-permute-start(bf16[3,7,512]{2,1,0:T(8,128)(2,1)S(1)} %slice.471), channel_id=1, source_target_pairs={{0,1},{1,2},{2,3},{3,4},{4,5},{5,6},{6,7},{7,8},{8,9},{9,10},{10,1... | collective-permute-start | bytes 64520 | tf_op jit(solution)/shard_map/ppermute | solution.py:16

commit v11 on v10

--- a/solution.py
+++ b/solution.py
@@ -228,7 +228,8 @@
     lower = shifted(field[:2], "gx", -1)
     stacked = jnp.concatenate([upper, field, lower], axis=0)
     params = ((dw1, pw1), (dw2, pw2), (dw3, pw3), (dw4, pw4))
-    params, stacked = lax.optimization_barrier((params, stacked))
+    places = (lax.axis_index("gx"), lax.axis_index("gy"))
+    (params, dw0, pw0, places), stacked = lax.optimization_barrier(((params, dw0, pw0, places), stacked))
     leftside = shifted(stacked[:, -(margin + 2) * chans :], "gy", 1)
     rightside = shifted(stacked[:, : 2 * chans], "gy", -1)
     flat_pad = jnp.concatenate([leftside, stacked, rightside], axis=1)
@@ -248,10 +249,10 @@
     pattern = jnp.tile(dw0, (1, 128 // chans))
     block = jnp.kron(jnp.eye(128 // chans, dtype=pw0.dtype), pw0)
     row_keep = (
-        (lax.axis_index("gx") > 0) | (lax.broadcasted_iota(jnp.int32, (padded_rows, 1), 0) >= margin)
+        (places[0] > 0) | (lax.broadcasted_iota(jnp.int32, (padded_rows, 1), 0) >= margin)
     ).astype(jnp.float32)
     col_keep = (
-        (lax.axis_index("gy") > 0) | (lax.broadcasted_iota(jnp.int32, (1, lanes), 1) >= margin * chans)
+        (places[1] > 0) | (lax.broadcasted_iota(jnp.int32, (1, lanes), 1) >= margin * chans)
     ).astype(jnp.float32)
     body = functools.partial(fine_kernel, plan=plan, rows=rows, cols=cols, margin=margin, chans=chans)
     fine, hidden = pl.pallas_call(

time: 118 us -> 119 us (level)
  waiting for transfers between devices: 5.88 us -> 9.32 us
  blocking collectives: 60.8 us -> 59.1 us
    ppermute x6, waiting for transfers between devices: 5.88 us -> 9.32 us  [shifted(): lax.ppermute(value, axis, [(source, source + steps) for source in range(l...]
    all_gather x1, blocking collectives: 39.3 us -> 37.6 us  [local(): hidden = lax.all_gather(hidden, 'gx', axis=0, tiled=True)]
  transfers between devices with their start and end apart: 6 -> 6, of which waited for: 1 -> 2; matrix products, arithmetic and copies ran while one was open for 12% -> 11% of each run, Pallas kernels for 0% -> 0%
where the time goes in v11:
time: 119 us; the launch traced here: 117 us
  blocking collectives  59.1 us (50%)
  local copies, waits for them, and re-layouts  17.8 us (15%)
  starting transfers between devices  16.7 us (14%)
  waiting for transfers between devices  9.32 us (8%)
  Pallas kernels  6.42 us (5%)
  other arithmetic  5.85 us (5%)
  between operations  1.22 us (1%)
    all_gather x1, blocking collectives, local(): hidden = lax.all_gather(hidden, 'gx', axis=0, tiled=True)  37.6 us
    all_gather x1, blocking collectives, local(): hidden = lax.all_gather(hidden, 'gy', axis=1, tiled=True)  21.5 us
    ppermute x6, starting transfers between devices, shifted(): lax.ppermute(value, axis, [(source, source + steps) for source in range(l...  16.7 us
    ppermute x6, waiting for transfers between devices, shifted(): lax.ppermute(value, axis, [(source, source + steps) for source in range(l...  9.32 us
    pallas_call x1, Pallas kernels, local(): pl.pallas_call(body, out_shape=(jax.ShapeDtypeStruct((rows, cols * chans)...  6.42 us
    concatenate x4, other arithmetic, prepare(): doubled = jnp.concatenate([weight, weight], axis=0)  3.19 us
    slice x36, local copies, waits for them, and re-layouts, strided_cells(): piece = padded[first:first + 2 * rows:2, second:second + 2 * cols:2]  3.02 us
  transfers between devices with their start and end apart: 6, of which 2 were waited for; matrix products, arithmetic and copies ran while one was open for 11% of the time, Pallas kernels for 0%

profile of v11, /device:TPU:6, one launch (start us, length us, event | category | flops | bytes accessed | tf_op | source)
XLA Modules:
  0.0 117.3 jit_solution(12112716525227469331)
XLA Ops:
  0.7 1.0 slice.371
  1.7 1.8 %collective-permute-start = (bf16[17,4096]{1,0:T(8,128)(2,1)S(1)}, bf16[17,4096]{1,0:T(8,128)(2,1)S(1)}, u32[]{:S(2)}, u32[]{:S(2)}) collective-permute-start(bf16[17,4096]{1,0:T(8,128)(2,1)S(1)} %slice.371), channel_id=1, source_target_pairs={{0,16},{16,32},{32,48},{48,64},{64,80},{80,96},{96,112},{112,128},... | collective-permute-start | bytes 417800 | tf_op jit(solution)/shard_map/ppermute | solution.py:16
  3.5 0.9 slice.372
  4.3 1.3 %collective-permute-start.1 = (bf16[2,4096]{1,0:T(2,128)(2,1)S(1)}, bf16[2,4096]{1,0:T(2,128)(2,1)S(1)}, u32[]{:S(2)}, u32[]{:S(2)}) collective-permute-start(bf16[2,4096]{1,0:T(2,128)(2,1)S(1)} %slice.372), channel_id=1, source_target_pairs={{16,0},{32,16},{48,32},{64,48},{80,64},{96,80},{112,96},{128,112},... | collective-permute-start | bytes 49160 | tf_op jit(solution)/shard_map/ppermute | solution.py:16
  5.7 3.4 %collective-permute-done.1 = bf16[2,4096]{1,0:T(2,128)(2,1)S(1)} collective-permute-done((bf16[2,4096]{1,0:T(2,128)(2,1)S(1)}, bf16[2,4096]{1,0:T(2,128)(2,1)S(1)}, u32[]{:S(2)}, u32[]{:S(2)}) %collective-permute-start.1) | collective-permute-done | bytes 16416 | tf_op jit(solution)/shard_map/ppermute | solution.py:16
  9.1 1.1 pad_maximum_fusion.1
  10.3 0.7 reshape.223
  11.0 0.7 reshape.224
  11.7 3.5 %collective-permute-start.2 = (bf16[51,544]{1,0:T(8,128)(2,1)S(1)}, bf16[51,544]{1,0:T(8,128)(2,1)S(1)}, u32[]{:S(2)}, u32[]{:S(2)}) collective-permute-start(bf16[51,544]{1,0:T(8,128)(2,1)S(1)} %slice.373), channel_id=1, source_target_pairs={{0,1},{1,2},{2,3},{3,4},{4,5},{5,6},{6,7},{7,8},{8,9},{9,10},{10,1... | collective-permute-start | bytes 166472 | tf_op jit(solution)/shard_map/ppermute | solution.py:16
  15.2 4.5 %collective-permute-start.3 = (bf16[51,64]{1,0:T(8,128)(2,1)S(1)}, bf16[51,64]{1,0:T(8,128)(2,1)S(1)}, u32[]{:S(2)}, u32[]{:S(2)}) collective-permute-start(bf16[51,64]{1,0:T(8,128)(2,1)S(1)} %slice.374), channel_id=1, source_target_pairs={{1,0},{2,1},{3,2},{4,3},{5,4},{6,5},{7,6},{8,7},{9,8},{10,9},{11,1... | collective-permute-start | bytes 19592 | tf_op jit(solution)/shard_map/ppermute | solution.py:16
  19.7 1.9 %pad_maximum_fusion.refs_16_ = bf16[512,512]{1,0:T(8,128)(2,1)} fusion(bf16[256,512]{1,0:T(8,128)(2,1)} %param.23), kind=kLoop, calls=%fused_computation | loop fusion | flops 1048576 | bytes 786432 | tf_op jit(solution)/shard_map/concatenate | solution.py:99
  21.6 0.7 pad_maximum_fusion.2.refs_13_
  22.3 0.6 pad_maximum_fusion.4.refs_10_
  22.9 0.6 fusion.46.refs_3_
  23.5 0.6 or_convert_fusion.refs_4_
  24.1 0.6 copy_bitcast_fusion
  25.1 0.6 copy.49
  25.7 0.6 copy.48
  26.4 0.6 tile.36.refs_6_
  27.1 0.7 tile.33.refs_5_
  27.8 0.7 tile_reshape.21.refs_9_
  28.5 0.7 tile_reshape.20.refs_8_
  29.1 0.7 mul.495.refs_2_
  29.9 0.7 mul.499.refs_7_
  30.6 0.7 tile.30.refs_1_
  31.3 0.8 concatenate.49
  32.1 0.8 pad.12.refs_0_
  32.9 6.4 %shard_map.140 = (bf16[32,4096]{1,0:T(8,128)(2,1)}, bf16[8,4608]{1,0:T(8,128)(2,1)}) custom-call(bf16[56,4736]{1,0:T(8,128)(2,1)} %pad.12.refs_0_, f32[9,128]{1,0:T(8,128)} %tile.30.refs_1_, bf16[128,128]{1,0:T(8,128)(2,1)} %mul.495.refs_2_, f32[48,1]{1,0:T(8,128)} %fusion.46.refs_3_, f32[1,4608]{1,0:T(1,128)} %or_convert_fusion.refs_4_, ...), custom_call_target="tpu_custom_call" | custom-call | tf_op jit(solution)/shard_map/pallas_call | solution.py:258
  39.3 0.9 slice_reduce_fusion
  40.3 3.8 %collective-permute-start.4 = (bf16[1,8,512]{2,1,0:T(8,128)(2,1)S(1)}, bf16[1,8,512]{2,1,0:T(8,128)(2,1)S(1)}, u32[]{:S(2)}, u32[]{:S(2)}) collective-permute-start(bf16[1,8,512]{2,1,0:T(8,128)(2,1)S(1)} %slice.384), channel_id=1, source_target_pairs={{0,16},{16,32},{32,48},{48,64},{64,80},{80,96},{96,112},{112,128},... | collective-permute-start | bytes 24584 | tf_op jit(solution)/shard_map/ppermute | solution.py:16
  44.1 0.9 slice.385
  45.1 1.9 %collective-permute-start.5 = (bf16[3,7,512]{2,1,0:T(8,128)(2,1)S(1)}, bf16[3,7,512]{2,1,0:T(8,128)(2,1)S(1)}, u32[]{:S(2)}, u32[]{:S(2)}) collective-permute-start(bf16[3,7,512]{2,1,0:T(8,128)(2,1)S(1)} %slice.471), channel_id=1, source_target_pairs={{0,1},{1,2},{2,3},{3,4},{4,5},{5,6},{6,7},{7,8},{8,9},{9,10},{10,1... | collective-permute-start | bytes 64520 | tf_op jit(solution)/shard_map/ppermute | solution.py:16
  47.0 5.9 %collective-permute-done.5 = bf16[3,7,512]{2,1,0:T(8,128)(2,1)S(1)} collective-permute-done((bf16[3,7,512]{2,1,0:T(8,128)(2,1)S(1)}, bf16[3,7,512]{2,1,0:T(8,128)(2,1)S(1)}, u32[]{:S(2)}, u32[]{:S(2)}) %collective-permute-start.5) | collective-permute-done | bytes 21536 | tf_op jit(solution)/shard_map/ppermute | solution.py:16
  53.1 0.2 fusion.59
  53.3 37.6 %all-gather.2 = bf16[32,7,512]{2,1,0:T(8,128)(2,1)S(1)} all-gather(bf16[1,7,512]{2,1,0:T(8,128)(2,1)S(1)} %fusion.59), channel_id=2, replica_groups=mesh['gx'=32,'gy'=16] {'gx'}, dimensions={0}, use_global_device_ids=true | all-gather | bytes 236544 | tf_op jit(solution)/shard_map/all_gather | solution.py:274
  91.2 0.1 slice.408
  91.4 0.2 slice.410
  91.8 0.2 slice.416
  92.3 0.2 slice.422
  92.7 0.2 fusion.21
  93.2 0.2 fusion.71
  93.4 21.5 %all-gather.1 = bf16[8,8192]{1,0:T(8,128)(2,1)S(1)} all-gather(bf16[8,512]{1,0:T(8,128)(2,1)S(1)} %fusion.71), channel_id=3, replica_groups=mesh['gx'=32,'gy'=16] {'gy'}, dimensions={1}, use_global_device_ids=true | all-gather | bytes 139264 | tf_op jit(solution)/shard_map/all_gather | solution.py:277
  115.2 0.1 slice.450
  115.3 0.2 slice.456
  116.0 0.2 slice.458
  116.2 0.2 slice.460
  116.4 0.3 fusion.33
  116.7 0.6 reshape_reshape.3
  (94 shorter events, 2.9 us)
Async XLA Ops:
  0.6 29.9 %copy-start.7 = (f32[9,32]{1,0:T(8,128)S(1)}, f32[9,32]{1,0:T(8,128)}, u32[]{:S(2)}) copy-start(f32[9,32]{1,0:T(8,128)} %param.14) | copy-start | bytes 3460
  0.6 24.1 %copy-start.4 = (bf16[32,32]{1,0:T(8,128)(2,1)S(1)}, bf16[32,32]{1,0:T(8,128)(2,1)}, u32[]{:S(2)}) copy-start(bf16[32,32]{1,0:T(8,128)(2,1)} %param.15) | copy-start | bytes 6148
  0.7 24.4 %copy-start.5 = (f32[9,32]{1,0:T(8,128)S(1)}, f32[9,32]{1,0:T(8,128)}, u32[]{:S(2)}) copy-start(f32[9,32]{1,0:T(8,128)} %param.16) | copy-start | bytes 3460
  0.7 21.6 %copy-start.3 = (bf16[32,64]{1,0:T(8,128)(2,1)S(1)}, bf16[32,64]{1,0:T(8,128)(2,1)}, u32[]{:S(2)}) copy-start(bf16[32,64]{1,0:T(8,128)(2,1)} %param.17) | copy-start | bytes 12292
  0.7 24.4 %copy-start.6 = (f32[9,64]{1,0:T(8,128)S(1)}, f32[9,64]{1,0:T(8,128)}, u32[]{:S(2)}) copy-start(f32[9,64]{1,0:T(8,128)} %param.18) | copy-start | bytes 6916
  0.7 21.6 %copy-start.2 = (bf16[64,128]{1,0:T(8,128)(2,1)S(1)}, bf16[64,128]{1,0:T(8,128)(2,1)}, u32[]{:S(2)}) copy-start(bf16[64,128]{1,0:T(8,128)(2,1)} %param.19) | copy-start | bytes 49156
  0.7 20.9 %copy-start.1 = (bf16[128,256]{1,0:T(8,128)(2,1)S(1)}, bf16[128,256]{1,0:T(8,128)(2,1)}, u32[]{:S(2)}) copy-start(bf16[128,256]{1,0:T(8,128)(2,1)} %param.21) | copy-start | bytes 196612
  1.7 7.4 %collective-permute-start = (bf16[17,4096]{1,0:T(8,128)(2,1)S(1)}, bf16[17,4096]{1,0:T(8,128)(2,1)S(1)}, u32[]{:S(2)}, u32[]{:S(2)}) collective-permute-start(bf16[17,4096]{1,0:T(8,128)(2,1)S(1)} %slice.371), channel_id=1, source_target_pairs={{0,16},{16,32},{32,48},{48,64},{64,80},{80,96},{96,112},{112,128},... | collective-permute-start | bytes 417800 | tf_op jit(solution)/shard_map/ppermute | solution.py:16
  4.3 4.8 %collective-permute-start.1 = (bf16[2,4096]{1,0:T(2,128)(2,1)S(1)}, bf16[2,4096]{1,0:T(2,128)(2,1)S(1)}, u32[]{:S(2)}, u32[]{:S(2)}) collective-permute-start(bf16[2,4096]{1,0:T(2,128)(2,1)S(1)} %slice.372), channel_id=1, source_target_pairs={{16,0},{32,16},{48,32},{64,48},{80,64},{96,80},{112,96},{128,112},... | collective-permute-start | bytes 49160 | tf_op jit(solution)/shard_map/ppermute | solution.py:16
  11.7 19.5 %collective-permute-start.2 = (bf16[51,544]{1,0:T(8,128)(2,1)S(1)}, bf16[51,544]{1,0:T(8,128)(2,1)S(1)}, u32[]{:S(2)}, u32[]{:S(2)}) collective-permute-start(bf16[51,544]{1,0:T(8,128)(2,1)S(1)} %slice.373), channel_id=1, source_target_pairs={{0,1},{1,2},{2,3},{3,4},{4,5},{5,6},{6,7},{7,8},{8,9},{9,10},{10,1... | collective-permute-start | bytes 166472 | tf_op jit(solution)/shard_map/ppermute | solution.py:16
  15.2 16.0 %collective-permute-start.3 = (bf16[51,64]{1,0:T(8,128)(2,1)S(1)}, bf16[51,64]{1,0:T(8,128)(2,1)S(1)}, u32[]{:S(2)}, u32[]{:S(2)}) collective-permute-start(bf16[51,64]{1,0:T(8,128)(2,1)S(1)} %slice.374), channel_id=1, source_target_pairs={{1,0},{2,1},{3,2},{4,3},{5,4},{6,5},{7,6},{8,7},{9,8},{10,9},{11,1... | collective-permute-start | bytes 19592 | tf_op jit(solution)/shard_map/ppermute | solution.py:16
  24.7 19.3 %copy-start = (f32[4,9,512]{2,0,1:T(4,128)S(1)}, f32[4,9,512]{2,0,1:T(4,128)}, u32[]{:S(2)}) copy-start(f32[4,9,512]{2,0,1:T(4,128)} %param.24) | copy-start | bytes 221188
  30.6 22.5 %copy-start.8 = (bf16[4,512,512]{2,1,0:T(8,128)(2,1)S(1)}, bf16[4,512,512]{2,1,0:T(8,128)(2,1)}, u32[]{:S(2)}) copy-start(bf16[4,512,512]{2,1,0:T(8,128)(2,1)} %param.25) | copy-start | bytes 6291460
  40.3 4.7 %collective-permute-start.4 = (bf16[1,8,512]{2,1,0:T(8,128)(2,1)S(1)}, bf16[1,8,512]{2,1,0:T(8,128)(2,1)S(1)}, u32[]{:S(2)}, u32[]{:S(2)}) collective-permute-start(bf16[1,8,512]{2,1,0:T(8,128)(2,1)S(1)} %slice.384), channel_id=1, source_target_pairs={{0,16},{16,32},{32,48},{48,64},{64,80},{80,96},{96,112},{112,128},... | collective-permute-start | bytes 24584 | tf_op jit(solution)/shard_map/ppermute | solution.py:16
  45.1 7.8 %collective-permute-start.5 = (bf16[3,7,512]{2,1,0:T(8,128)(2,1)S(1)}, bf16[3,7,512]{2,1,0:T(8,128)(2,1)S(1)}, u32[]{:S(2)}, u32[]{:S(2)}) collective-permute-start(bf16[3,7,512]{2,1,0:T(8,128)(2,1)S(1)} %slice.471), channel_id=1, source_target_pairs={{0,1},{1,2},{2,3},{3,4},{4,5},{5,6},{6,7},{7,8},{8,9},{9,10},{10,1... | collective-permute-start | bytes 64520 | tf_op jit(solution)/shard_map/ppermute | solution.py:16

commit v12 on v11

--- a/solution.py
+++ b/solution.py
@@ -1,4 +1,6 @@
 import functools
+
+import numpy as np
 
 import jax
 import jax.numpy as jnp
@@ -114,9 +116,8 @@
     return jnp.dot(pick, value, preferred_element_type=jnp.float32)
 
 
-def fine_kernel(*refs, plan, rows, cols, margin, chans):
-    x_ref, pat_ref, pw_ref, row_ref, col_ref = refs[:5]
-    fine_ref, o_ref = refs[-2:]
+def fine_kernel(x_ref, pats_ref, mats_ref, row_ref, col_ref, fine_ref, o_ref, *, plan, rows, cols, margin, chans, spots):
+    pat_ref = pats_ref
     source = x_ref[...].astype(jnp.float32)
     lanes = source.shape[1]
     width = plan[0][0] * 0 + col_ref.shape[1]
@@ -127,14 +128,15 @@
         shifted.append(
             [slab if second == 0 else pltpu.roll(slab, lanes - 2 * second * chans, 1) for second in range(3)]
         )
-    weight = pw_ref[...]
+    weight = mats_ref[0:128, 0:128]
     parts = []
     for index in range(width // 128):
         window = slice(index * 128, (index + 1) * 128)
         total = None
         for first in range(3):
             for second in range(3):
-                term = shifted[first][second][:, window] * pat_ref[3 * first + second : 3 * first + second + 1, :]
+                tap = 3 * first + second
+                term = shifted[first][second][:, window] * pat_ref[tap : tap + 1, 0:128]
                 total = term if total is None else total + term
         mixed = gelu_tanh(jnp.dot(total.astype(jnp.bfloat16), weight, preferred_element_type=jnp.float32))
         parts.append((shifted[1][1][:, window] + mixed).astype(jnp.bfloat16))
@@ -143,13 +145,14 @@
     hidden = jnp.where(keep > 0, hidden, jnp.zeros_like(hidden)).astype(jnp.float32)
     inner = pltpu.roll(hidden, width - margin * chans, 1)[:, : cols * chans]
     fine_ref[...] = pick_rows(inner, rows, margin, ext_rows).astype(fine_ref.dtype)
-    o_ref[...] = chain_levels(hidden, refs[5:-2], plan).astype(o_ref.dtype)
+    o_ref[...] = chain_levels(hidden, (pats_ref, mats_ref, spots), plan).astype(o_ref.dtype)
 
 
 def chain_levels(value, refs, plan):
     lanes = value.shape[1]
     for level, (valid, rows, chans, outs) in enumerate(plan):
-        near_ref, far_ref, w_ref = refs[3 * level : 3 + 3 * level]
+        pats_ref, mats_ref, spots = refs
+        row_at, mat_at, span, depth, across = spots[level]
         shape = (rows, value.shape[0])
         out_row = lax.broadcasted_iota(jnp.int32, shape, 0)
         in_row = lax.broadcasted_iota(jnp.int32, shape, 1)
@@ -158,7 +161,7 @@
             pick = ((in_row == 2 * out_row + first) & (in_row < valid)).astype(jnp.float32)
             slabs.append(jnp.dot(pick, value, preferred_element_type=jnp.float32))
         aheads = [pltpu.roll(slab, lanes - 2 * chans, 1) for slab in slabs]
-        weight = w_ref[...]
+        weight = mats_ref[mat_at : mat_at + depth, 0:across]
         chunk = max(128, 2 * chans)
         width = weight.shape[1]
         parts = []
@@ -166,10 +169,9 @@
             window = slice(index * chunk, (index + 1) * chunk)
             total = None
             for first in range(3):
-                term = (
-                    slabs[first][:, window] * near_ref[first : first + 1, :]
-                    + aheads[first][:, window] * far_ref[first : first + 1, :]
-                )
+                near = pats_ref[row_at + first : row_at + first + 1, 0:span]
+                far = pats_ref[row_at + 3 + first : row_at + 4 + first, 0:span]
+                term = slabs[first][:, window] * near + aheads[first][:, window] * far
                 total = term if total is None else total + term
             part = jnp.dot(total.astype(jnp.bfloat16), weight, preferred_element_type=jnp.float32)
             parts.append(gelu_tanh(part).astype(jnp.bfloat16))
@@ -248,20 +250,50 @@
     )
     pattern = jnp.tile(dw0, (1, 128 // chans))
     block = jnp.kron(jnp.eye(128 // chans, dtype=pw0.dtype), pw0)
+    span = max(piece.shape[1] for piece in operands)
+    taps_all = [dw0] + [taps for taps, _ in params]
+    flat_taps = jnp.concatenate([taps.reshape(-1) for taps in taps_all] + [jnp.zeros((1,), dw0.dtype)])
+    zero_at = flat_taps.shape[0] - 1
+    index = np.full((9 + 6 * len(plan), span), zero_at, np.int32)
+    lane = np.arange(span)
+    index[:9, :128] = np.arange(9)[:, None] * chans + lane[None, :128] % chans
+    mat_rows = [block]
+    spots = []
+    row_at, mat_at, base = 9, 128, dw0.size
+    for level, (taps, _) in enumerate(params):
+        width = taps.shape[1]
+        mat = operands[3 * level + 2]
+        chunk = max(128, 2 * width)
+        inner = lane[:chunk] % (2 * width)
+        for first in range(3):
+            index[row_at + first, :chunk] = base + (3 * first + inner // width) * width + inner % width
+            far = np.where(inner < width, base + (3 * first + 2) * width + inner % width, zero_at)
+            index[row_at + 3 + first, :chunk] = far
+        mat_rows.append(mat)
+        spots.append((row_at, mat_at, chunk, mat.shape[0], mat.shape[1]))
+        row_at += 6
+        mat_at += mat.shape[0]
+        base += taps.size
+    pats = flat_taps[jnp.asarray(index)]
+    mats = jnp.concatenate(
+        [jnp.pad(piece, ((0, 0), (0, span - piece.shape[1]))) for piece in mat_rows], axis=0
+    )
     row_keep = (
         (places[0] > 0) | (lax.broadcasted_iota(jnp.int32, (padded_rows, 1), 0) >= margin)
     ).astype(jnp.float32)
     col_keep = (
         (places[1] > 0) | (lax.broadcasted_iota(jnp.int32, (1, lanes), 1) >= margin * chans)
     ).astype(jnp.float32)
-    body = functools.partial(fine_kernel, plan=plan, rows=rows, cols=cols, margin=margin, chans=chans)
+    body = functools.partial(
+        fine_kernel, plan=plan, rows=rows, cols=cols, margin=margin, chans=chans, spots=tuple(spots)
+    )
     fine, hidden = pl.pallas_call(
         body,
         out_shape=(
             jax.ShapeDtypeStruct((rows, cols * chans), jnp.bfloat16),
             jax.ShapeDtypeStruct((plan[-1][1], lanes), jnp.bfloat16),
         ),
-    )(source, pattern, block, row_keep, col_keep, *operands)
+    )(source, pats, mats, row_keep, col_keep)
     hidden = hidden[:last_rows, : last_cols * last_chans]
     coarse_chans = dwc.shape[2]
     halo = 2 ** (LC - 1) - 1

time: 119 us -> 196 us (1.65)
  local copies, waits for them, and re-layouts: 17.8 us -> 97.7 us
  other arithmetic: 5.85 us -> 3.6 us
    gather x0 -> x2, local copies, waits for them, and re-layouts: none -> 87.5 us  [local(): pats = flat_taps[jnp.asarray(index)]]
    another operation x11 -> x0, local copies, waits for them, and re-layouts: 4.08 us -> none  [the longest x5 1.99 us: prepare(): jnp.tile(jnp.concatenate([grouped[:, 2:], jnp.zeros_like(grouped[:, 2:])]...]
    concatenate x4 -> x1, other arithmetic: 3.19 us -> 0.01 us  [prepare(): doubled = jnp.concatenate([weight, weight], axis=0)]
  transfers between devices with their start and end apart: 6 -> 6, of which waited for: 2 -> 2; matrix products, arithmetic and copies ran while one was open for 11% -> 47% of each run, Pallas kernels for 0% -> 0%
where the time goes in v12:
time: 196 us; the launch traced here: 194 us
  local copies, waits for them, and re-layouts  97.7 us (50%)
  blocking collectives  59.1 us (30%)
  starting transfers between devices  16.9 us (9%)
  waiting for transfers between devices  8.4 us (4%)
  Pallas kernels  6.64 us (3%)
  other arithmetic  3.6 us (2%)
    gather x2, local copies, waits for them, and re-layouts, local(): pats = flat_taps[jnp.asarray(index)]  87.5 us
    all_gather x1, blocking collectives, local(): hidden = lax.all_gather(hidden, 'gx', axis=0, tiled=True)  37.6 us
    all_gather x1, blocking collectives, local(): hidden = lax.all_gather(hidden, 'gy', axis=1, tiled=True)  21.5 us
    ppermute x6, starting transfers between devices, shifted(): lax.ppermute(value, axis, [(source, source + steps) for source in range(l...  16.9 us
    ppermute x6, waiting for transfers between devices, shifted(): lax.ppermute(value, axis, [(source, source + steps) for source in range(l...  8.4 us
    pallas_call x1, Pallas kernels, local(): pl.pallas_call(body, out_shape=(jax.ShapeDtypeStruct((rows, cols * chans)...  6.64 us
  transfers between devices with their start and end apart: 6, of which 2 were waited for; matrix products, arithmetic and copies ran while one was open for 47% of the time, Pallas kernels for 0%

profile of v12, /device:TPU:6, one launch (start us, length us, event | category | flops | bytes accessed | tf_op | source)
XLA Modules:
  0.0 194.5 jit_solution(12933387890482393014)
XLA Ops:
  0.7 1.0 slice.347
  1.7 1.9 collective-permute-start
  3.6 0.9 slice.348
  4.4 1.3 collective-permute-start.1
  5.7 0.9 pad_clamp_fusion
  6.7 2.5 %collective-permute-done.1 = bf16[2,4096]{1,0:T(2,128)(2,1)S(1)} collective-permute-done((bf16[2,4096]{1,0:T(2,128)(2,1)S(1)}, bf16[2,4096]{1,0:T(2,128)(2,1)S(1)}, u32[]{:S(2)}, u32[]{:S(2)}) %collective-permute-start.1) | collective-permute-done | bytes 16416 | tf_op jit(solution)/shard_map/ppermute | solution.py:18
  9.2 1.1 pad_maximum_fusion
  10.6 0.1 mul.495
  10.7 0.1 broadcast_multiply_fusion.1
  11.1 3.5 %collective-permute-start.2 = (bf16[51,544]{1,0:T(8,128)(2,1)S(1)}, bf16[51,544]{1,0:T(8,128)(2,1)S(1)}, u32[]{:S(2)}, u32[]{:S(2)}) collective-permute-start(bf16[51,544]{1,0:T(8,128)(2,1)S(1)} %slice.349), channel_id=1, source_target_pairs={{0,1},{1,2},{2,3},{3,4},{4,5},{5,6},{6,7},{7,8},{8,9},{9,10},{10,1... | collective-permute-start | bytes 166472 | tf_op jit(solution)/shard_map/ppermute | solution.py:18
  14.6 4.5 %collective-permute-start.3 = (bf16[51,64]{1,0:T(8,128)(2,1)S(1)}, bf16[51,64]{1,0:T(8,128)(2,1)S(1)}, u32[]{:S(2)}, u32[]{:S(2)}) collective-permute-start(bf16[51,64]{1,0:T(8,128)(2,1)S(1)} %slice.350), channel_id=1, source_target_pairs={{1,0},{2,1},{3,2},{4,3},{5,4},{6,5},{7,6},{8,7},{9,8},{10,9},{11,1... | collective-permute-start | bytes 19592 | tf_op jit(solution)/shard_map/ppermute | solution.py:18
  19.1 0.6 or_convert_fusion.col_ref
  19.7 0.6 fusion.54.row_ref
  20.6 86.9 %gather_fusion = f32[16896]{0:T(1024)S(1)} fusion(f32[4609]{0:T(1024)S(1)} %concatenate.43, s32[17408]{0:T(1024)S(1)} %pad_clamp_fusion), kind=kCustom, calls=%fused_computation | custom fusion | bytes 202752 | tf_op jit(solution)/shard_map/gather | solution.py:277
  107.5 0.6 reshape.226.pats_ref
  108.2 0.8 concatenate.42
  109.0 0.8 pad.22.x_ref
  109.8 6.6 %shard_map.149 = (bf16[32,4096]{1,0:T(8,128)(2,1)}, bf16[8,4608]{1,0:T(8,128)(2,1)}) custom-call(bf16[56,4736]{1,0:T(8,128)(2,1)} %pad.22.x_ref, f32[33,512]{1,0:T(8,128)} %reshape.226.pats_ref, bf16[1152,512]{1,0:T(8,128)(2,1)} %copy-done, f32[48,1]{1,0:T(8,128)} %fusion.54.row_ref, f32[1,4608]{1,0:T(1,128)} %or_convert_fusion.col_ref), custom_call_target="tpu_custom_call" | custom-call | tf_op jit(solution)/shard_map/pallas_call | solution.py:290
  116.5 0.9 slice_reduce_fusion
  117.4 3.8 %collective-permute-start.4 = (bf16[1,8,512]{2,1,0:T(8,128)(2,1)S(1)}, bf16[1,8,512]{2,1,0:T(8,128)(2,1)S(1)}, u32[]{:S(2)}, u32[]{:S(2)}) collective-permute-start(bf16[1,8,512]{2,1,0:T(8,128)(2,1)S(1)} %slice.352), channel_id=1, source_target_pairs={{0,16},{16,32},{32,48},{48,64},{64,80},{80,96},{96,112},{112,128},... | collective-permute-start | bytes 24584 | tf_op jit(solution)/shard_map/ppermute | solution.py:18
  121.3 0.9 slice.353
  122.2 1.9 collective-permute-start.5
  124.1 5.9 %collective-permute-done.5 = bf16[3,7,512]{2,1,0:T(8,128)(2,1)S(1)} collective-permute-done((bf16[3,7,512]{2,1,0:T(8,128)(2,1)S(1)}, bf16[3,7,512]{2,1,0:T(8,128)(2,1)S(1)}, u32[]{:S(2)}, u32[]{:S(2)}) %collective-permute-start.5) | collective-permute-done | bytes 21536 | tf_op jit(solution)/shard_map/ppermute | solution.py:18
  130.2 0.2 fusion.67
  130.4 37.6 %all-gather.2 = bf16[32,7,512]{2,1,0:T(8,128)(2,1)S(1)} all-gather(bf16[1,7,512]{2,1,0:T(8,128)(2,1)S(1)} %fusion.67), channel_id=2, replica_groups=mesh['gx'=32,'gy'=16] {'gx'}, dimensions={0}, use_global_device_ids=true | all-gather | bytes 236544 | tf_op jit(solution)/shard_map/all_gather | solution.py:306
  168.2 0.1 slice.374
  168.3 0.1 slice.376
  168.5 0.2 slice.378
  168.7 0.1 slice.380
  168.8 0.1 slice.382
  168.9 0.2 slice.384
  169.1 0.1 slice.386
  169.3 0.1 slice.388
  169.4 0.2 slice.390
  169.8 0.2 fusion.29
  170.3 0.2 fusion.79
  170.5 21.5 %all-gather.1 = bf16[8,8192]{1,0:T(8,128)(2,1)S(1)} all-gather(bf16[8,512]{1,0:T(8,128)(2,1)S(1)} %fusion.79), channel_id=3, replica_groups=mesh['gx'=32,'gy'=16] {'gy'}, dimensions={1}, use_global_device_ids=true | all-gather | bytes 139264 | tf_op jit(solution)/shard_map/all_gather | solution.py:309
  192.2 0.1 slice.412
  192.3 0.1 slice.418
  192.4 0.2 slice.424
  192.6 0.1 slice.414
  192.8 0.1 slice.416
  192.9 0.1 slice.420
  193.0 0.1 slice.422
  193.2 0.2 slice.426
  193.4 0.2 slice.428
  193.6 0.3 fusion.41
  193.8 0.6 reshape_reshape.3
  (84 shorter events, 1.8 us)
Async XLA Ops:
  0.6 9.7 %copy-start.6 = (bf16[32,32]{1,0:T(8,128)(2,1)S(1)}, bf16[32,32]{1,0:T(8,128)(2,1)}, u32[]{:S(2)}) copy-start(bf16[32,32]{1,0:T(8,128)(2,1)} %param.16) | copy-start | bytes 6148
  0.6 10.1 %copy-start.7 = (bf16[32,64]{1,0:T(8,128)(2,1)S(1)}, bf16[32,64]{1,0:T(8,128)(2,1)}, u32[]{:S(2)}) copy-start(bf16[32,64]{1,0:T(8,128)(2,1)} %param.18) | copy-start | bytes 12292
  0.7 10.3 %copy-start.4 = (bf16[64,128]{1,0:T(8,128)(2,1)S(1)}, bf16[64,128]{1,0:T(8,128)(2,1)}, u32[]{:S(2)}) copy-start(bf16[64,128]{1,0:T(8,128)(2,1)} %param.20) | copy-start | bytes 49156
  1.7 9.3 %copy-start.3 = (bf16[128,256]{1,0:T(8,128)(2,1)S(1)}, bf16[128,256]{1,0:T(8,128)(2,1)}, u32[]{:S(2)}) copy-start(bf16[128,256]{1,0:T(8,128)(2,1)} %param.22) | copy-start | bytes 196612
  1.7 7.5 %collective-permute-start = (bf16[17,4096]{1,0:T(8,128)(2,1)S(1)}, bf16[17,4096]{1,0:T(8,128)(2,1)S(1)}, u32[]{:S(2)}, u32[]{:S(2)}) collective-permute-start(bf16[17,4096]{1,0:T(8,128)(2,1)S(1)} %slice.347), channel_id=1, source_target_pairs={{0,16},{16,32},{32,48},{48,64},{64,80},{80,96},{96,112},{112,128},... | collective-permute-start | bytes 417800 | tf_op jit(solution)/shard_map/ppermute | solution.py:18
  4.4 4.8 %collective-permute-start.1 = (bf16[2,4096]{1,0:T(2,128)(2,1)S(1)}, bf16[2,4096]{1,0:T(2,128)(2,1)S(1)}, u32[]{:S(2)}, u32[]{:S(2)}) collective-permute-start(bf16[2,4096]{1,0:T(2,128)(2,1)S(1)} %slice.348), channel_id=1, source_target_pairs={{16,0},{32,16},{48,32},{64,48},{80,64},{96,80},{112,96},{128,112},... | collective-permute-start | bytes 49160 | tf_op jit(solution)/shard_map/ppermute | solution.py:18
  6.6 4.4 %copy-start.1 = (bf16[256,512]{1,0:T(8,128)(2,1)S(1)}, bf16[256,512]{1,0:T(8,128)(2,1)}, u32[]{:S(2)}) copy-start(bf16[256,512]{1,0:T(8,128)(2,1)} %param.24) | copy-start | bytes 786436
  10.4 9.9 %copy-start.5 = (f32[9,256]{1,0:T(8,128)S(1)}, f32[9,256]{1,0:T(8,128)}, u32[]{:S(2)}) copy-start(f32[9,256]{1,0:T(8,128)} %param.23) | copy-start | bytes 27652
  10.5 9.8 %copy-start.11 = (f32[9,64]{1,0:T(8,128)S(1)}, f32[9,64]{1,0:T(8,128)}, u32[]{:S(2)}) copy-start(f32[9,64]{1,0:T(8,128)} %param.19) | copy-start | bytes 6916
  10.5 9.9 %copy-start.9 = (f32[9,32]{1,0:T(8,128)S(1)}, f32[9,32]{1,0:T(8,128)}, u32[]{:S(2)}) copy-start(f32[9,32]{1,0:T(8,128)} %param.15) | copy-start | bytes 3460
  10.5 9.9 %copy-start.10 = (f32[9,32]{1,0:T(8,128)S(1)}, f32[9,32]{1,0:T(8,128)}, u32[]{:S(2)}) copy-start(f32[9,32]{1,0:T(8,128)} %param.17) | copy-start | bytes 3460
  10.5 10.0 %copy-start.8 = (f32[9,128]{1,0:T(8,128)S(1)}, f32[9,128]{1,0:T(8,128)}, u32[]{:S(2)}) copy-start(f32[9,128]{1,0:T(8,128)} %param.21) | copy-start | bytes 13828
  11.1 96.4 %copy-start = (bf16[1152,512]{1,0:T(8,128)(2,1)}, bf16[1152,512]{1,0:T(8,128)(2,1)S(1)}, u32[]{:S(2)}) copy-start(bf16[1152,512]{1,0:T(8,128)(2,1)S(1)} %constant_dynamic-update-slice_fusion.mats_ref) | copy-start | bytes 3538948
  11.1 97.0 %collective-permute-start.2 = (bf16[51,544]{1,0:T(8,128)(2,1)S(1)}, bf16[51,544]{1,0:T(8,128)(2,1)S(1)}, u32[]{:S(2)}, u32[]{:S(2)}) collective-permute-start(bf16[51,544]{1,0:T(8,128)(2,1)S(1)} %slice.349), channel_id=1, source_target_pairs={{0,1},{1,2},{2,3},{3,4},{4,5},{5,6},{6,7},{7,8},{8,9},{9,10},{10,1... | collective-permute-start | bytes 166472 | tf_op jit(solution)/shard_map/ppermute | solution.py:18
  14.6 93.5 %collective-permute-start.3 = (bf16[51,64]{1,0:T(8,128)(2,1)S(1)}, bf16[51,64]{1,0:T(8,128)(2,1)S(1)}, u32[]{:S(2)}, u32[]{:S(2)}) collective-permute-start(bf16[51,64]{1,0:T(8,128)(2,1)S(1)} %slice.350), channel_id=1, source_target_pairs={{1,0},{2,1},{3,2},{4,3},{5,4},{6,5},{7,6},{8,7},{9,8},{10,9},{11,1... | collective-permute-start | bytes 19592 | tf_op jit(solution)/shard_map/ppermute | solution.py:18
  109.8 11.4 %copy-start.2 = (f32[4,9,512]{2,0,1:T(4,128)S(1)}, f32[4,9,512]{2,0,1:T(4,128)}, u32[]{:S(2)}) copy-start(f32[4,9,512]{2,0,1:T(4,128)} %param.25) | copy-start | bytes 221188
  109.8 20.4 %copy-start.12 = (bf16[4,512,512]{2,1,0:T(8,128)(2,1)S(1)}, bf16[4,512,512]{2,1,0:T(8,128)(2,1)}, u32[]{:S(2)}) copy-start(bf16[4,512,512]{2,1,0:T(8,128)(2,1)} %param.26) | copy-start | bytes 6291460
  117.4 4.7 %collective-permute-start.4 = (bf16[1,8,512]{2,1,0:T(8,128)(2,1)S(1)}, bf16[1,8,512]{2,1,0:T(8,128)(2,1)S(1)}, u32[]{:S(2)}, u32[]{:S(2)}) collective-permute-start(bf16[1,8,512]{2,1,0:T(8,128)(2,1)S(1)} %slice.352), channel_id=1, source_target_pairs={{0,16},{16,32},{32,48},{48,64},{64,80},{80,96},{96,112},{112,128},... | collective-permute-start | bytes 24584 | tf_op jit(solution)/shard_map/ppermute | solution.py:18
  122.2 7.8 %collective-permute-start.5 = (bf16[3,7,512]{2,1,0:T(8,128)(2,1)S(1)}, bf16[3,7,512]{2,1,0:T(8,128)(2,1)S(1)}, u32[]{:S(2)}, u32[]{:S(2)}) collective-permute-start(bf16[3,7,512]{2,1,0:T(8,128)(2,1)S(1)} %slice.433), channel_id=1, source_target_pairs={{0,1},{1,2},{2,3},{3,4},{4,5},{5,6},{6,7},{7,8},{8,9},{9,10},{10,1... | collective-permute-start | bytes 64520 | tf_op jit(solution)/shard_map/ppermute | solution.py:18
